TPU v7x, 256 devices: a whole 4x4x8 slice. The times are simulated.
256 devices in a mesh: dp: 16 (over x, y), tensor: 16 (over z, core).
Axes of the slice: x: 4, y: 4, z: 8, core: 2. Of those that a mesh axis runs over, the one named last changes fastest.
Arguments:
- tokens: bfloat16 [2048, 8192], P('tensor', 'dp'), may hold values from -6 to 6
- cotangent: bfloat16 [2048, 8192], P('tensor', 'dp'), may hold values from -0.625 to 0.625
- gate_weight: bfloat16 [8192, 14336], P('dp', 'tensor'), may hold values from -0.0625 to 0.0625
- up_weight: bfloat16 [8192, 14336], P('dp', 'tensor'), may hold values from -0.0625 to 0.0625
- down_weight: bfloat16 [14336, 8192], P('tensor', 'dp'), may hold values from -0.046875 to 0.046875
- gate_in: bfloat16 [64, 8192, 16], P(None, 'dp'), may hold values from -0.0625 to 0.0625
- up_in: bfloat16 [64, 8192, 16], P(None, 'dp'), may hold values from -0.0625 to 0.0625
- down_out: bfloat16 [64, 16, 8192], P(None, None, 'dp'), may hold values from -1.5 to 1.5
- gate_out: bfloat16 [64, 16, 14336], P(None, None, 'tensor'), may hold values from -1.5 to 1.5
- up_out: bfloat16 [64, 16, 14336], P(None, None, 'tensor'), may hold values from -1.5 to 1.5
- down_in: bfloat16 [64, 14336, 16], P(None, 'tensor'), may hold values from -0.046875 to 0.046875
- tenants: int32 [32], replicated, may hold values from 0 to 63
- owners: int32 [64], replicated, may hold values from 0 to 63, each once
Outputs:
- mixed: bfloat16 [2048, 8192], P('tensor', 'dp')
- grad_gate_in: float32 [64, 8192, 16], P('tensor', 'dp')
- grad_up_in: float32 [64, 8192, 16], P('tensor', 'dp')
- grad_down_out: float32 [64, 16, 8192], P('tensor', None, 'dp')
- grad_gate_out: float32 [64, 16, 14336], P('dp', None, 'tensor')
- grad_up_out: float32 [64, 16, 14336], P('dp', None, 'tensor')
- grad_down_in: float32 [64, 14336, 16], P('dp', 'tensor')
Inputs may be any that keep to these rules, and one draw needn't show every extreme that they name: `tenants`: tenant numbers lie in 0 to 63; a tenant may own no block. `owners`: every owner slot is given to exactly one tenant.
All inputs are finite; a program needn't handle non-finite values.
Results may differ from a plain program's by a relative error of at most 0.029.
Values may be sent and summed in bfloat16 or wider, within the bound.
No kernel may reach another device: no remote copies, remote signals or barrier semaphores. Data moves between devices by JAX's collectives and lax.ppermute only.
A program may use at most 128 MiB of HBM per device.

v0:
```python
import jax
import jax.numpy as jnp
from jax import lax
from jax.sharding import PartitionSpec as P

BLOCK = 64


adapter_scale = 0.5


def shards(
    tokens,
    cotangent,
    gate_weight,
    up_weight,
    down_weight,
    gate_in,
    up_in,
    down_out,
    gate_out,
    up_out,
    down_in,
    tenants,
    owners,
):
    highest = lax.Precision.HIGHEST
    dp_count = lax.axis_size("dp")
    tensor_count = lax.axis_size("tensor")
    dp_index = lax.axis_index("dp")
    tensor_index = lax.axis_index("tensor")
    rows_in = tokens.shape[0]
    feat_here = tokens.shape[1]
    width_here = gate_weight.shape[1]
    rank_width = gate_in.shape[2]
    every_token_row = rows_in * tensor_count
    group_rows = every_token_row // dp_count
    blocks_all = tenants.shape[0]
    blocks_group = group_rows // BLOCK
    blocks_in = rows_in // BLOCK
    tenant_count = owners.shape[0]
    slots_here = tenant_count // dp_count
    tenants_here = tenant_count // tensor_count
    group_tenants = lax.dynamic_slice_in_dim(tenants, dp_index * blocks_group, blocks_group)
    input_tenants = lax.dynamic_slice_in_dim(tenants, tensor_index * blocks_in, blocks_in)
    contract_rows = (((0,), (0,)), ((), ()))
    token_tenants = jnp.broadcast_to(tenants[:, None], (blocks_all, BLOCK)).reshape(every_token_row)
    held_tenants = tensor_index * tenants_here + jnp.arange(tenants_here, dtype=jnp.int32)
    token_onehot = (token_tenants[:, None] == held_tenants[None, :]).astype(jnp.bfloat16)
    all_inputs = lax.all_gather(tokens, "tensor", axis=0, tiled=True)
    gate_part = jnp.dot(all_inputs, gate_weight, preferred_element_type=jnp.float32)
    up_part = jnp.dot(all_inputs, up_weight, preferred_element_type=jnp.float32)
    input_blocks = all_inputs.reshape(blocks_all, BLOCK, feat_here)
    gate_rank_part = jnp.einsum(
        "btk,bkr->btr", input_blocks, gate_in[tenants], preferred_element_type=jnp.float32
    ).reshape(every_token_row, rank_width)
    up_rank_part = jnp.einsum(
        "btk,bkr->btr", input_blocks, up_in[tenants], preferred_element_type=jnp.float32
    ).reshape(every_token_row, rank_width)
    gate_total_sum, up_total_sum, gate_rank, up_rank = (
        lax.psum_scatter(
            gate_part.astype(jnp.bfloat16), "dp", scatter_dimension=0, tiled=True
        ).astype(jnp.float32),
        lax.psum_scatter(
            up_part.astype(jnp.bfloat16), "dp", scatter_dimension=0, tiled=True
        ).astype(jnp.float32),
        lax.psum_scatter(
            gate_rank_part.astype(jnp.bfloat16), "dp", scatter_dimension=0, tiled=True
        ).astype(jnp.float32),
        lax.psum_scatter(
            up_rank_part.astype(jnp.bfloat16), "dp", scatter_dimension=0, tiled=True
        ).astype(jnp.float32),
    )
    gate_rank_second = gate_rank.astype(jnp.bfloat16).reshape(blocks_group, BLOCK, rank_width)
    up_rank_second = up_rank.astype(jnp.bfloat16).reshape(blocks_group, BLOCK, rank_width)
    gate_raise = gate_out[group_tenants]
    up_raise = up_out[group_tenants]
    gate_complete = gate_total_sum + adapter_scale * jnp.einsum(
        "uim,umn->uin", gate_rank_second, gate_raise, preferred_element_type=jnp.float32
    ).reshape(group_rows, width_here)
    up_complete = up_total_sum + adapter_scale * jnp.einsum(
        "uim,umn->uin", up_rank_second, up_raise, preferred_element_type=jnp.float32
    ).reshape(group_rows, width_here)
    hidden = (jax.nn.silu(gate_complete) * up_complete).astype(jnp.bfloat16)
    all_hidden = lax.all_gather(hidden, "dp", axis=0, tiled=True)
    out_part = jnp.dot(all_hidden, down_weight, preferred_element_type=jnp.float32)
    down_rank_part = jnp.einsum(
        "btf,bfr->btr",
        all_hidden.reshape(blocks_all, BLOCK, width_here),
        down_in[tenants],
        preferred_element_type=jnp.float32,
    ).reshape(every_token_row, rank_width)
    out_sum, down_rank = (
        lax.psum_scatter(
            out_part.astype(jnp.bfloat16), "tensor", scatter_dimension=0, tiled=True
        ).astype(jnp.float32),
        lax.psum_scatter(
            down_rank_part.astype(jnp.bfloat16), "tensor", scatter_dimension=0, tiled=True
        ).astype(jnp.float32),
    )
    down_rank_flat = down_rank.astype(jnp.bfloat16)
    down_rank_second = down_rank_flat.reshape(blocks_in, BLOCK, rank_width)
    down_raise = down_out[input_tenants]
    mixed = (
        out_sum
        + adapter_scale
        * jnp.einsum(
            "vmn,vnx->vmx", down_rank_second, down_raise, preferred_element_type=jnp.float32
        ).reshape(rows_in, feat_here)
    ).astype(jnp.bfloat16)
    cotangent_block_list = cotangent.reshape(blocks_in, BLOCK, feat_here)
    down_backward_piece = adapter_scale * jnp.einsum(
        "env,ejv->enj", cotangent_block_list, down_raise, preferred_element_type=jnp.float32
    )
    down_backward = lax.psum(down_backward_piece, "dp").astype(jnp.bfloat16)
    tenant_ids = jnp.arange(tenant_count, dtype=jnp.int32)
    input_onehot = (tenant_ids[:, None] == input_tenants[None, :]).astype(jnp.float32)
    raise_gradient_block_list = adapter_scale * jnp.einsum(
        "jpy,jpz->jyz", down_rank_second, cotangent_block_list, preferred_element_type=jnp.float32
    )
    lift_grad_part = jnp.einsum(
        "eb,brd->erd", input_onehot, raise_gradient_block_list, precision=highest
    )
    grad_down_out = lax.psum_scatter(
        lift_grad_part.astype(jnp.bfloat16), "tensor", scatter_dimension=0, tiled=True
    ).astype(jnp.float32)
    all_cot, all_down_back = (
        lax.all_gather(cotangent, "tensor", axis=0, tiled=True),
        lax.all_gather(down_backward.reshape(rows_in, rank_width), "tensor", axis=0, tiled=True),
    )
    hidden_grad_part = lax.dot_general(
        all_cot, down_weight, (((1,), (1,)), ((), ())), preferred_element_type=jnp.float32
    )
    hidden_grad_sum = lax.psum_scatter(
        hidden_grad_part.astype(jnp.bfloat16), "dp", scatter_dimension=0, tiled=True
    ).astype(jnp.float32)
    group_down_back = lax.dynamic_slice_in_dim(
        all_down_back, dp_index * group_rows, group_rows
    ).reshape(blocks_group, BLOCK, rank_width)
    down_drop = down_in[group_tenants]
    hidden_grad = hidden_grad_sum + jnp.einsum(
        "btr,bfr->btf", group_down_back, down_drop, preferred_element_type=jnp.float32
    ).reshape(group_rows, width_here)
    sig = jax.nn.sigmoid(gate_complete)
    up_gradient = (
        (hidden_grad * gate_complete * sig)
        .astype(jnp.bfloat16)
        .reshape(blocks_group, BLOCK, width_here)
    )
    gate_gradient = (
        (hidden_grad * up_complete * sig * (1.0 + gate_complete * (1.0 - sig)))
        .astype(jnp.bfloat16)
        .reshape(blocks_group, BLOCK, width_here)
    )
    gate_backward_piece = adapter_scale * jnp.einsum(
        "yae,yve->yav", gate_gradient, gate_raise, preferred_element_type=jnp.float32
    )
    up_backward_piece = adapter_scale * jnp.einsum(
        "yae,yve->yav", up_gradient, up_raise, preferred_element_type=jnp.float32
    )
    gate_backward, up_backward = lax.psum((gate_backward_piece, up_backward_piece), "tensor")
    gate_raise_block_list = adapter_scale * jnp.einsum(
        "yap,yau->ypu", gate_rank_second, gate_gradient, preferred_element_type=jnp.float32
    )
    up_raise_block_list = adapter_scale * jnp.einsum(
        "yap,yau->ypu", up_rank_second, up_gradient, preferred_element_type=jnp.float32
    )
    own_slots = dp_index * slots_here + jnp.arange(slots_here, dtype=jnp.int32)
    group_onehot = (tenant_ids[:, None] == owners[group_tenants][None, :]).astype(jnp.float32)
    gate_lift_part = jnp.einsum(
        "sb,brf->srf", group_onehot, gate_raise_block_list, precision=highest
    )
    up_lift_part = jnp.einsum("sb,brf->srf", group_onehot, up_raise_block_list, precision=highest)
    grad_gate_out, grad_up_out = (
        lax.psum_scatter(
            gate_lift_part.astype(jnp.bfloat16), "dp", scatter_dimension=0, tiled=True
        ).astype(jnp.float32),
        lax.psum_scatter(
            up_lift_part.astype(jnp.bfloat16), "dp", scatter_dimension=0, tiled=True
        ).astype(jnp.float32),
    )
    all_gate_back, all_up_back = (
        lax.all_gather(
            gate_backward.astype(jnp.bfloat16).reshape(group_rows, rank_width),
            "dp",
            axis=0,
            tiled=True,
        ),
        lax.all_gather(
            up_backward.astype(jnp.bfloat16).reshape(group_rows, rank_width),
            "dp",
            axis=0,
            tiled=True,
        ),
    )
    gate_weighted = (token_onehot[:, :, None] * all_gate_back[:, None, :]).reshape(
        every_token_row, tenants_here * rank_width
    )
    up_weighted = (token_onehot[:, :, None] * all_up_back[:, None, :]).reshape(
        every_token_row, tenants_here * rank_width
    )
    grad_gate_in = (
        lax.dot_general(
            all_inputs, gate_weighted, contract_rows, preferred_element_type=jnp.float32
        )
        .reshape(feat_here, tenants_here, rank_width)
        .transpose(1, 0, 2)
    )
    grad_up_in = (
        lax.dot_general(all_inputs, up_weighted, contract_rows, preferred_element_type=jnp.float32)
        .reshape(feat_here, tenants_here, rank_width)
        .transpose(1, 0, 2)
    )
    token_slots = owners[token_tenants]
    slot_onehot = (token_slots[:, None] == own_slots[None, :]).astype(jnp.bfloat16)
    drop_weighted = (slot_onehot[:, :, None] * all_down_back[:, None, :]).reshape(
        every_token_row, slots_here * rank_width
    )
    grad_down_in = (
        lax.dot_general(
            all_hidden, drop_weighted, contract_rows, preferred_element_type=jnp.float32
        )
        .reshape(width_here, slots_here, rank_width)
        .transpose(1, 0, 2)
    )
    return (
        mixed,
        grad_gate_in,
        grad_up_in,
        grad_down_out,
        grad_gate_out,
        grad_up_out,
        grad_down_in,
    )


def solution(mesh):
    in_specs = (
        P("tensor", "dp"),
        P("tensor", "dp"),
        P("dp", "tensor"),
        P("dp", "tensor"),
        P("tensor", "dp"),
        P(None, "dp", None),
        P(None, "dp", None),
        P(None, None, "dp"),
        P(None, None, "tensor"),
        P(None, None, "tensor"),
        P(None, "tensor", None),
        P(),
        P(),
    )
    out_specs = (
        P("tensor", "dp"),
        P("tensor", "dp", None),
        P("tensor", "dp", None),
        P("tensor", None, "dp"),
        P("dp", None, "tensor"),
        P("dp", None, "tensor"),
        P("dp", "tensor", None),
    )
    return jax.shard_map(shards, mesh=mesh, in_specs=in_specs, out_specs=out_specs, check_vma=False)
```

profile of v0, /device:TPU:8, one launch (start us, length us, event | category | flops | bytes accessed | tf_op | source)
XLA Modules:
  0.0 921.3 jit_solution(15388209541601431929)
XLA Ops:
  13.0 39.2 %all-gather.4.cloned.1.call-done = bf16[2048,512]{1,0:T(8,128)(2,1)} async-done(((bf16[128,512]{1,0:T(8,128)(2,1)}), bf16[2048,512]{1,0:T(8,128)(2,1)}) %all-gather.4.cloned.1.call-update) | async-done | bytes 2097168 | tf_op jit(solution)/shard_map/all_gather | solution.py:50
  52.2 2.2 fusion.5
  55.6 2.3 fusion.6
  59.0 32.9 %all-gather.8.cloned.1.call-done = bf16[2048,512]{1,0:T(8,128)(2,1)} async-done(((bf16[128,512]{1,0:T(8,128)(2,1)}), bf16[2048,512]{1,0:T(8,128)(2,1)}) %all-gather.8.cloned.1.call-update) | async-done | bytes 2097168 | tf_op jit(solution)/shard_map/all_gather | solution.py:128
  91.9 5.8 convolution_convert_fusion
  98.8 5.8 convolution_convert_fusion.2
  105.8 5.8 convolution_convert_fusion.1
  114.3 69.2 %psum.21 = bf16[2,64,16]{1,2,0:T(8,128)(2,1)S(1)} all-reduce(f32[2,64,16]{1,2,0:T(8,128)S(1)} %fusion.7), channel_id=1, replica_groups=mesh['dp'=16,'tensor'=16] {'dp'}, use_global_device_ids=true, to_apply=%region_7.8 | all-reduce | flops 2048 | bytes 12288 | tf_op jit(solution)/shard_map/psum | solution.py:115
  183.6 15.8 %all_gather.21 = bf16[2048,16]{0,1:T(8,128)(2,1)S(1)} all-gather(bf16[128,16]{0,1:T(8,128)(2,1)S(1)} %reshape.200), channel_id=1, replica_groups=mesh['dp'=16,'tensor'=16] {'tensor'}, dimensions={0}, use_global_device_ids=true | all-gather | bytes 69632 | tf_op jit(solution)/shard_map/all_gather | solution.py:129
  202.7 2.1 gather_fusion.3
  206.8 46.4 %reduce-scatter.33.cloned.1.call-done = bf16[128,16]{1,0:T(8,128)(2,1)} async-done(((bf16[2048,16]{1,0:T(8,128)(2,1)}), bf16[128,16]{1,0:T(8,128)(2,1)}) %reduce-scatter.33.cloned.1.call-update) | async-done | bytes 4112
  254.9 83.6 %reduce-scatter.23.cloned.1.call-done = bf16[128,896]{1,0:T(8,128)(2,1)} async-done(((bf16[2048,896]{1,0:T(8,128)(2,1)}), bf16[128,896]{1,0:T(8,128)(2,1)}) %reduce-scatter.23.cloned.1.call-update) | async-done | bytes 229392 | tf_op jit(solution)/shard_map/reduce_scatter | solution.py:134
  338.5 85.2 %reduce-scatter.17.cloned.1.call-done = bf16[128,896]{1,0:T(8,128)(2,1)} async-done(((bf16[2048,896]{1,0:T(8,128)(2,1)}), bf16[128,896]{1,0:T(8,128)(2,1)}) %reduce-scatter.17.cloned.1.call-update) | async-done | bytes 229392 | tf_op jit(solution)/shard_map/reduce_scatter | solution.py:61
  423.7 85.3 %reduce-scatter.19.cloned.1.call-done = bf16[128,896]{1,0:T(8,128)(2,1)} async-done(((bf16[2048,896]{1,0:T(8,128)(2,1)}), bf16[128,896]{1,0:T(8,128)(2,1)}) %reduce-scatter.19.cloned.1.call-update) | async-done | bytes 229392 | tf_op jit(solution)/shard_map/reduce_scatter | solution.py:64
  509.0 2.4 multiply_convert_fusion
  513.7 52.0 %all-gather.6.cloned.1.call-done = bf16[2048,896]{1,0:T(8,128)(2,1)} async-done(((bf16[128,896]{1,0:T(8,128)(2,1)}), bf16[2048,896]{1,0:T(8,128)(2,1)}) %all-gather.6.cloned.1.call-update) | async-done | bytes 3670032 | tf_op jit(solution)/shard_map/all_gather | solution.py:85
  565.7 3.2 convolution_convert_fusion.7
  570.2 2.6 convolution_convert_fusion.5
  572.9 2.3 copy.51
  577.2 2.3 copy.54
  579.6 47.7 %reduce-scatter.35.cloned.1.call-done = bf16[128,16]{1,0:T(8,128)(2,1)} async-done(((bf16[2048,16]{1,0:T(8,128)(2,1)}), bf16[128,16]{1,0:T(8,128)(2,1)}) %reduce-scatter.35.cloned.1.call-update) | async-done | bytes 4112
  632.6 6.0 convolution_convert_fusion.3
  640.1 4.4 compare_select_fusion.1
  645.9 35.1 %select_select_fusion = s32[2048]{0:T(1024)S(1)} fusion(pred[2048]{0:T(1024)(128)(4,1)S(1)} %get-tuple-element.77, pred[2048]{0:T(1024)(128)(4,1)S(1)} %get-tuple-element.76, pred[2048]{0:T(1024)(128)(4,1)S(1)} %get-tuple-element.75, pred[2048]{0:T(1024)(128)(4,1)S(1)} %get-tuple-element.74, pred[2048]{0:T(1024)(128)(4,1)S(1)} %get-tuple-element.73, ...), kind=kLoop, calls=%fused_computation.119 | loop fusion | flops 116736 | bytes 133348 | tf_op jit(solution)/shard_map/gather | solution.py:214
  681.5 46.3 %all-reduce = (bf16[2,64,16]{1,2,0:T(8,128)(2,1)S(1)}, bf16[2,64,16]{1,2,0:T(8,128)(2,1)S(1)}) all-reduce(f32[2,64,16]{1,2,0:T(8,128)S(1)} %convolution_multiply_fusion.7, f32[2,64,16]{1,2,0:T(8,128)S(1)} %convolution_multiply_fusion.6), channel_id=1, replica_groups=mesh['dp'=16,'tensor'=16] {'tensor'}, use_global_device_ids=true, to_apply=%region_8.9 | all-reduce | flops 4096 | bytes 24576 | tf_op jit(solution)/shard_map/psum | solution.py:161
  728.0 23.1 %all_gather.23 = bf16[2048,16]{0,1:T(8,128)(2,1)S(1)} all-gather(bf16[128,16]{0,1:T(8,128)(2,1)S(1)} %reshape.207), channel_id=1, replica_groups=mesh['dp'=16,'tensor'=16] {'dp'}, dimensions={0}, use_global_device_ids=true | all-gather | bytes 69632 | tf_op jit(solution)/shard_map/all_gather | solution.py:189
  751.1 21.6 %all_gather.22 = bf16[2048,16]{0,1:T(8,128)(2,1)S(1)} all-gather(bf16[128,16]{0,1:T(8,128)(2,1)S(1)} %reshape.204), channel_id=1, replica_groups=mesh['dp'=16,'tensor'=16] {'dp'}, dimensions={0}, use_global_device_ids=true | all-gather | bytes 69632 | tf_op jit(solution)/shard_map/all_gather | solution.py:183
  772.8 2.7 fusion.30
  778.3 13.4 %reduce-scatter.29.cloned.1.call-done = bf16[4,16,896]{2,1,0:T(8,128)(2,1)} async-done(((bf16[64,16,896]{2,1,0:T(8,128)(2,1)}), bf16[4,16,896]{2,1,0:T(8,128)(2,1)}) %reduce-scatter.29.cloned.1.call-update) | async-done | bytes 114704 | tf_op jit(solution)/shard_map/reduce_scatter | solution.py:178
  793.3 3.4 fusion.2
  796.8 55.1 %reduce-scatter.25.cloned.1.call-done = bf16[4,16,512]{2,1,0:T(8,128)(2,1)} async-done(((bf16[64,16,512]{2,1,0:T(8,128)(2,1)}), bf16[4,16,512]{2,1,0:T(8,128)(2,1)}) %reduce-scatter.25.cloned.1.call-update) | async-done | bytes 65552 | tf_op jit(solution)/shard_map/reduce_scatter | solution.py:124
  853.4 59.7 %reduce-scatter.21.cloned.1.call-done = bf16[128,512]{1,0:T(8,128)(2,1)} async-done(((bf16[2048,512]{1,0:T(8,128)(2,1)}), bf16[128,512]{1,0:T(8,128)(2,1)}) %reduce-scatter.21.cloned.1.call-update) | async-done | bytes 131088 | tf_op jit(solution)/shard_map/reduce_scatter | solution.py:94
  (116 shorter events, 42.1 us)
Async XLA Ops:
  7.2 192.8 %copy-start = (bf16[64,896,16]{1,2,0:T(8,128)(2,1)S(1)}, bf16[64,896,16]{1,2,0:T(8,128)(2,1)}, u32[]{:S(2)}) copy-start(bf16[64,896,16]{1,2,0:T(8,128)(2,1)} %param.23) | copy-start | bytes 5505028
  7.2 45.0 %all-gather.4.cloned.1.call-start = ((), (), s32[]{:S(2)}) async-start(), calls=%async_computation.10 | async-start | bytes 2228224 | tf_op jit(solution)/shard_map/all_gather | solution.py:50
  7.9 83.9 %all-gather.8.cloned.1.call-start = ((), (), s32[]{:S(2)}) async-start(), calls=%async_computation.15 | async-start | bytes 2228224 | tf_op jit(solution)/shard_map/all_gather | solution.py:128
  8.7 196.4 %reduce-scatter.31.cloned.1.call-start = ((), (), s32[]{:S(2)}) async-start(), calls=%async_computation.20 | async-start | bytes 557056
  55.5 36.3 %copy-start.16 = (bf16[896,512]{1,0:T(8,128)(2,1)S(1)}, bf16[896,512]{1,0:T(8,128)(2,1)}, u32[]{:S(2)}) copy-start(bf16[896,512]{1,0:T(8,128)(2,1)} %param.17) | copy-start | bytes 2752516
  55.5 197.7 %reduce-scatter.33.cloned.1.call-start = ((), (), s32[]{:S(2)}) async-start(), calls=%async_computation.21 | async-start | bytes 557056
  58.9 279.6 %reduce-scatter.23.cloned.1.call-start = ((), (), s32[]{:S(2)}) async-start(), calls=%async_computation.16 | async-start | bytes 3899392 | tf_op jit(solution)/shard_map/reduce_scatter | solution.py:134
  97.6 1.2 copy-start.14
  97.6 326.0 %reduce-scatter.17.cloned.1.call-start = ((), (), s32[]{:S(2)}) async-start(), calls=%async_computation.11 | async-start | bytes 3899392 | tf_op jit(solution)/shard_map/reduce_scatter | solution.py:61
  104.6 1.2 copy-start.15
  104.6 404.4 %reduce-scatter.19.cloned.1.call-start = ((), (), s32[]{:S(2)}) async-start(), calls=%async_computation.12 | async-start | bytes 3899392 | tf_op jit(solution)/shard_map/reduce_scatter | solution.py:64
  111.6 0.7 copy-start.13
  111.6 2.5 copy-start.3
  111.6 454.1 %all-gather.6.cloned.1.call-start = ((), (), s32[]{:S(2)}) async-start(), calls=%async_computation.13 | async-start | bytes 3899392 | tf_op jit(solution)/shard_map/all_gather | solution.py:85
  114.1 85.3 %copy-start.6 = (bf16[2,16,512]{2,1,0:T(8,128)(2,1)}, bf16[2,16,512]{2,1,0:T(8,128)(2,1)S(1)}, u32[]{:S(2)}) copy-start(bf16[2,16,512]{2,1,0:T(8,128)(2,1)S(1)} %gather_fusion.5) | copy-start | bytes 98308
  199.4 0.6 copy-start.11
  202.7 308.8 %copy-start.4 = (bf16[2,16,896]{2,1,0:T(8,128)(2,1)}, bf16[2,16,896]{2,1,0:T(8,128)(2,1)S(1)}, u32[]{:S(2)}) copy-start(bf16[2,16,896]{2,1,0:T(8,128)(2,1)S(1)} %gather_fusion.1) | copy-start | bytes 172036
  511.4 0.8 copy-start.1
  511.5 1.4 copy-start.10
  511.5 115.9 %reduce-scatter.35.cloned.1.call-start = ((), (), s32[]{:S(2)}) async-start(), calls=%async_computation.22 | async-start | bytes 557056
  570.0 206.7 %reduce-scatter.27.cloned.1.call-start = ((), (), s32[]{:S(2)}) async-start(), calls=%async_computation.18 | async-start | bytes 1949696 | tf_op jit(solution)/shard_map/reduce_scatter | solution.py:175
  572.9 2.4 copy-start.9
  575.2 216.5 %reduce-scatter.29.cloned.1.call-start = ((), (), s32[]{:S(2)}) async-start(), calls=%async_computation.19 | async-start | bytes 1949696 | tf_op jit(solution)/shard_map/reduce_scatter | solution.py:178
  579.6 272.4 %reduce-scatter.25.cloned.1.call-start = ((), (), s32[]{:S(2)}) async-start(), calls=%async_computation.17 | async-start | bytes 1114112 | tf_op jit(solution)/shard_map/reduce_scatter | solution.py:124
  631.0 282.2 %reduce-scatter.21.cloned.1.call-start = ((), (), s32[]{:S(2)}) async-start(), calls=%async_computation.14 | async-start | bytes 2228224 | tf_op jit(solution)/shard_map/reduce_scatter | solution.py:94
  638.6 42.6 %copy-start.5 = (bf16[2,16,896]{2,1,0:T(8,128)(2,1)S(1)}, bf16[2,16,896]{2,1,0:T(8,128)(2,1)}, u32[]{:S(2)}) copy-start(bf16[2,16,896]{2,1,0:T(8,128)(2,1)} %copy-done.4) | copy-start | bytes 172036
  728.0 47.5 %copy-start.2 = (bf16[2048,512]{1,0:T(8,128)(2,1)S(1)}, bf16[2048,512]{1,0:T(8,128)(2,1)}, u32[]{:S(2)}) copy-start(bf16[2048,512]{1,0:T(8,128)(2,1)} %all-gather.4.cloned.1.call-done) | copy-start | bytes 6291460
  775.5 17.8 %copy-start.12 = (bf16[2048,16]{0,1:T(8,128)(2,1)S(1)}, bf16[2048,16]{0,1:T(8,128)(2,1)}, u32[]{:S(2)}) copy-start(bf16[2048,16]{0,1:T(8,128)(2,1)} %copy-done.11) | copy-start | bytes 196612
  793.3 3.4 copy-start.7
  793.3 3.4 copy-start.8
Sparse Core Ops, SparseCore 0:
  9.8 42.3 all-gather.3
  54.0 37.8 all-gather.7
  95.3 76.5 reduce-scatter.30
  175.3 77.9 reduce-scatter.32
  256.7 81.7 reduce-scatter.22
  342.0 81.6 reduce-scatter.16
  427.4 81.6 reduce-scatter.18
  512.1 53.5 all-gather.5
  570.1 57.1 reduce-scatter.34
  630.7 78.1 reduce-scatter.26
  712.4 79.2 reduce-scatter.28
  794.0 57.8 reduce-scatter.24
  854.5 58.6 reduce-scatter.20
where the time goes:
time: 923 us; the launch traced here: 921 us
  waiting for transfers between devices  602 us (65%)
  blocking collectives  176 us (19%)
  other arithmetic  50.6 us (5%)
  matrix products  50.2 us (5%)
  local copies, waits for them, and re-layouts  27.5 us (3%)
  between operations  14.2 us (2%)
    unnamed x16, waiting for transfers between devices  95.7 us
    reduce_scatter x1, waiting for transfers between devices, shards(): lax.psum_scatter(up_part.astype(jnp.bfloat16), 'dp', scatter_dimension=0,...  85.3 us
    reduce_scatter x1, waiting for transfers between devices, shards(): lax.psum_scatter(gate_part.astype(jnp.bfloat16), 'dp', scatter_dimension=...  85.2 us
    reduce_scatter x1, waiting for transfers between devices, shards(): lax.psum_scatter(hidden_grad_part.astype(jnp.bfloat16), 'dp', scatter_dim...  83.6 us
    psum x1, blocking collectives, shards(): down_backward = lax.psum(down_backward_piece, 'dp').astype(jnp.bfloat16)  69.2 us
    reduce_scatter x1, waiting for transfers between devices, shards(): lax.psum_scatter(out_part.astype(jnp.bfloat16), 'tensor', scatter_dimensi...  59.7 us
    reduce_scatter x1, waiting for transfers between devices, shards(): lax.psum_scatter(lift_grad_part.astype(jnp.bfloat16), 'tensor', scatter_d...  55.1 us
    all_gather x1, waiting for transfers between devices, shards(): all_hidden = lax.all_gather(hidden, 'dp', axis=0, tiled=True)  52 us
  transfers between devices with their start and end apart: 13, of which 11 were waited for; matrix products, arithmetic and copies ran while one was open for 13% of the time, Pallas kernels for 0%

commit v1 on v0

--- a/solution.py
+++ b/solution.py
@@ -7,6 +7,19 @@
 
 
 adapter_scale = 0.5
+
+
+def scatter_sum(x, axis):
+    count = lax.axis_size(axis)
+    pieces = x.astype(jnp.bfloat16).reshape((count, x.shape[0] // count) + x.shape[1:])
+    got = lax.all_to_all(pieces, axis, 0, 0, tiled=False)
+    return got.astype(jnp.float32).sum(0)
+
+
+def gather_rows(x, axis):
+    count = lax.axis_size(axis)
+    got = lax.all_to_all(jnp.broadcast_to(x[None], (count,) + x.shape), axis, 0, 0, tiled=False)
+    return got.reshape((count * x.shape[0],) + x.shape[1:])
 
 
 def shards(
@@ -48,6 +61,8 @@
     held_tenants = tensor_index * tenants_here + jnp.arange(tenants_here, dtype=jnp.int32)
     token_onehot = (token_tenants[:, None] == held_tenants[None, :]).astype(jnp.bfloat16)
     all_inputs = lax.all_gather(tokens, "tensor", axis=0, tiled=True)
+    all_cot = lax.all_gather(cotangent, "tensor", axis=0, tiled=True)
+
     gate_part = jnp.dot(all_inputs, gate_weight, preferred_element_type=jnp.float32)
     up_part = jnp.dot(all_inputs, up_weight, preferred_element_type=jnp.float32)
     input_blocks = all_inputs.reshape(blocks_all, BLOCK, feat_here)
@@ -57,20 +72,22 @@
     up_rank_part = jnp.einsum(
         "btk,bkr->btr", input_blocks, up_in[tenants], preferred_element_type=jnp.float32
     ).reshape(every_token_row, rank_width)
-    gate_total_sum, up_total_sum, gate_rank, up_rank = (
-        lax.psum_scatter(
-            gate_part.astype(jnp.bfloat16), "dp", scatter_dimension=0, tiled=True
-        ).astype(jnp.float32),
-        lax.psum_scatter(
-            up_part.astype(jnp.bfloat16), "dp", scatter_dimension=0, tiled=True
-        ).astype(jnp.float32),
-        lax.psum_scatter(
-            gate_rank_part.astype(jnp.bfloat16), "dp", scatter_dimension=0, tiled=True
-        ).astype(jnp.float32),
-        lax.psum_scatter(
-            up_rank_part.astype(jnp.bfloat16), "dp", scatter_dimension=0, tiled=True
-        ).astype(jnp.float32),
-    )
+    forward_sums = scatter_sum(
+        jnp.concatenate(
+            [
+                gate_part.astype(jnp.bfloat16),
+                up_part.astype(jnp.bfloat16),
+                gate_rank_part.astype(jnp.bfloat16),
+                up_rank_part.astype(jnp.bfloat16),
+            ],
+            axis=1,
+        ),
+        "dp",
+    )
+    gate_total_sum = forward_sums[:, :width_here]
+    up_total_sum = forward_sums[:, width_here : 2 * width_here]
+    gate_rank = forward_sums[:, 2 * width_here : 2 * width_here + rank_width]
+    up_rank = forward_sums[:, 2 * width_here + rank_width :]
     gate_rank_second = gate_rank.astype(jnp.bfloat16).reshape(blocks_group, BLOCK, rank_width)
     up_rank_second = up_rank.astype(jnp.bfloat16).reshape(blocks_group, BLOCK, rank_width)
     gate_raise = gate_out[group_tenants]
@@ -82,7 +99,8 @@
         "uim,umn->uin", up_rank_second, up_raise, preferred_element_type=jnp.float32
     ).reshape(group_rows, width_here)
     hidden = (jax.nn.silu(gate_complete) * up_complete).astype(jnp.bfloat16)
-    all_hidden = lax.all_gather(hidden, "dp", axis=0, tiled=True)
+    all_hidden = gather_rows(hidden, "dp")
+
     out_part = jnp.dot(all_hidden, down_weight, preferred_element_type=jnp.float32)
     down_rank_part = jnp.einsum(
         "btf,bfr->btr",
@@ -90,15 +108,14 @@
         down_in[tenants],
         preferred_element_type=jnp.float32,
     ).reshape(every_token_row, rank_width)
-    out_sum, down_rank = (
-        lax.psum_scatter(
-            out_part.astype(jnp.bfloat16), "tensor", scatter_dimension=0, tiled=True
-        ).astype(jnp.float32),
-        lax.psum_scatter(
-            down_rank_part.astype(jnp.bfloat16), "tensor", scatter_dimension=0, tiled=True
-        ).astype(jnp.float32),
-    )
-    down_rank_flat = down_rank.astype(jnp.bfloat16)
+    down_sums = scatter_sum(
+        jnp.concatenate(
+            [out_part.astype(jnp.bfloat16), down_rank_part.astype(jnp.bfloat16)], axis=1
+        ),
+        "tensor",
+    )
+    out_sum = down_sums[:, :feat_here]
+    down_rank_flat = down_sums[:, feat_here:].astype(jnp.bfloat16)
     down_rank_second = down_rank_flat.reshape(blocks_in, BLOCK, rank_width)
     down_raise = down_out[input_tenants]
     mixed = (
@@ -108,38 +125,39 @@
             "vmn,vnx->vmx", down_rank_second, down_raise, preferred_element_type=jnp.float32
         ).reshape(rows_in, feat_here)
     ).astype(jnp.bfloat16)
-    cotangent_block_list = cotangent.reshape(blocks_in, BLOCK, feat_here)
-    down_backward_piece = adapter_scale * jnp.einsum(
-        "env,ejv->enj", cotangent_block_list, down_raise, preferred_element_type=jnp.float32
-    )
-    down_backward = lax.psum(down_backward_piece, "dp").astype(jnp.bfloat16)
-    tenant_ids = jnp.arange(tenant_count, dtype=jnp.int32)
-    input_onehot = (tenant_ids[:, None] == input_tenants[None, :]).astype(jnp.float32)
-    raise_gradient_block_list = adapter_scale * jnp.einsum(
-        "jpy,jpz->jyz", down_rank_second, cotangent_block_list, preferred_element_type=jnp.float32
-    )
-    lift_grad_part = jnp.einsum(
-        "eb,brd->erd", input_onehot, raise_gradient_block_list, precision=highest
-    )
-    grad_down_out = lax.psum_scatter(
-        lift_grad_part.astype(jnp.bfloat16), "tensor", scatter_dimension=0, tiled=True
-    ).astype(jnp.float32)
-    all_cot, all_down_back = (
-        lax.all_gather(cotangent, "tensor", axis=0, tiled=True),
-        lax.all_gather(down_backward.reshape(rows_in, rank_width), "tensor", axis=0, tiled=True),
-    )
+
+    all_down_rank = lax.all_gather(down_rank_flat, "tensor", axis=0, tiled=True)
+    rank_weighted = (token_onehot[:, :, None] * all_down_rank[:, None, :]).reshape(
+        every_token_row, tenants_here * rank_width
+    )
+    grad_down_out = adapter_scale * (
+        lax.dot_general(rank_weighted, all_cot, contract_rows, preferred_element_type=jnp.float32)
+        .reshape(tenants_here, rank_width, feat_here)
+    )
+
     hidden_grad_part = lax.dot_general(
         all_cot, down_weight, (((1,), (1,)), ((), ())), preferred_element_type=jnp.float32
     )
-    hidden_grad_sum = lax.psum_scatter(
-        hidden_grad_part.astype(jnp.bfloat16), "dp", scatter_dimension=0, tiled=True
-    ).astype(jnp.float32)
-    group_down_back = lax.dynamic_slice_in_dim(
-        all_down_back, dp_index * group_rows, group_rows
-    ).reshape(blocks_group, BLOCK, rank_width)
+    down_back_part = adapter_scale * jnp.einsum(
+        "env,ejv->enj",
+        all_cot.reshape(blocks_all, BLOCK, feat_here),
+        down_out[tenants],
+        preferred_element_type=jnp.float32,
+    ).reshape(every_token_row, rank_width)
+    back_sums = scatter_sum(
+        jnp.concatenate(
+            [hidden_grad_part.astype(jnp.bfloat16), down_back_part.astype(jnp.bfloat16)], axis=1
+        ),
+        "dp",
+    )
+    hidden_grad_sum = back_sums[:, :width_here]
+    group_down_back = back_sums[:, width_here:].astype(jnp.bfloat16)
     down_drop = down_in[group_tenants]
     hidden_grad = hidden_grad_sum + jnp.einsum(
-        "btr,bfr->btf", group_down_back, down_drop, preferred_element_type=jnp.float32
+        "btr,bfr->btf",
+        group_down_back.reshape(blocks_group, BLOCK, rank_width),
+        down_drop,
+        preferred_element_type=jnp.float32,
     ).reshape(group_rows, width_here)
     sig = jax.nn.sigmoid(gate_complete)
     up_gradient = (
@@ -159,40 +177,40 @@
         "yae,yve->yav", up_gradient, up_raise, preferred_element_type=jnp.float32
     )
     gate_backward, up_backward = lax.psum((gate_backward_piece, up_backward_piece), "tensor")
+
     gate_raise_block_list = adapter_scale * jnp.einsum(
         "yap,yau->ypu", gate_rank_second, gate_gradient, preferred_element_type=jnp.float32
     )
     up_raise_block_list = adapter_scale * jnp.einsum(
         "yap,yau->ypu", up_rank_second, up_gradient, preferred_element_type=jnp.float32
     )
+    all_raise_blocks = gather_rows(
+        jnp.stack([gate_raise_block_list, up_raise_block_list], axis=1).astype(jnp.bfloat16),
+        "dp",
+    ).astype(jnp.float32)
     own_slots = dp_index * slots_here + jnp.arange(slots_here, dtype=jnp.int32)
-    group_onehot = (tenant_ids[:, None] == owners[group_tenants][None, :]).astype(jnp.float32)
-    gate_lift_part = jnp.einsum(
-        "sb,brf->srf", group_onehot, gate_raise_block_list, precision=highest
-    )
-    up_lift_part = jnp.einsum("sb,brf->srf", group_onehot, up_raise_block_list, precision=highest)
-    grad_gate_out, grad_up_out = (
-        lax.psum_scatter(
-            gate_lift_part.astype(jnp.bfloat16), "dp", scatter_dimension=0, tiled=True
-        ).astype(jnp.float32),
-        lax.psum_scatter(
-            up_lift_part.astype(jnp.bfloat16), "dp", scatter_dimension=0, tiled=True
-        ).astype(jnp.float32),
-    )
-    all_gate_back, all_up_back = (
-        lax.all_gather(
-            gate_backward.astype(jnp.bfloat16).reshape(group_rows, rank_width),
-            "dp",
-            axis=0,
-            tiled=True,
-        ),
-        lax.all_gather(
-            up_backward.astype(jnp.bfloat16).reshape(group_rows, rank_width),
-            "dp",
-            axis=0,
-            tiled=True,
-        ),
-    )
+    block_onehot = (own_slots[:, None] == owners[tenants][None, :]).astype(jnp.float32)
+    grad_gate_out = jnp.einsum(
+        "sb,brf->srf", block_onehot, all_raise_blocks[:, 0], precision=highest
+    )
+    grad_up_out = jnp.einsum("sb,brf->srf", block_onehot, all_raise_blocks[:, 1], precision=highest)
+
+    all_backs = lax.all_gather(
+        jnp.concatenate(
+            [
+                gate_backward.astype(jnp.bfloat16).reshape(group_rows, rank_width),
+                up_backward.astype(jnp.bfloat16).reshape(group_rows, rank_width),
+                group_down_back,
+            ],
+            axis=1,
+        ),
+        "dp",
+        axis=0,
+        tiled=True,
+    )
+    all_gate_back = all_backs[:, :rank_width]
+    all_up_back = all_backs[:, rank_width : 2 * rank_width]
+    all_down_back = all_backs[:, 2 * rank_width :]
     gate_weighted = (token_onehot[:, :, None] * all_gate_back[:, None, :]).reshape(
         every_token_row, tenants_here * rank_width
     )

time: 923 us -> 552 us (0.60)
  waiting for transfers between devices: 602 us -> 210 us
  starting transfers between devices: 0.71 us -> 52.4 us
  blocking collectives: 176 us -> 126 us
  local copies, waits for them, and re-layouts: 27.5 us -> 41.5 us
  other arithmetic: 50.6 us -> 63.4 us
  matrix products: 50.2 us -> 40.5 us
    reduce_scatter x7 -> x0, waiting for transfers between devices: 382 us -> none  [the longest x1 85.3 us: shards(): lax.psum_scatter(up_part.astype(jnp.bfloat16), 'dp', scatter_dimension=0,...]
    all_to_all x0 -> x5, waiting for transfers between devices: none -> 148 us  [the longest x3 112 us: scatter_sum(): got = lax.all_to_all(pieces, axis, 0, 0, tiled=False)]
    unnamed x16 -> x2, waiting for transfers between devices: 95.7 us -> 1.38 us
    psum x1 -> x0, blocking collectives: 69.2 us -> none  [shards(): down_backward = lax.psum(down_backward_piece, 'dp').astype(jnp.bfloat16)]
    all_to_all x0 -> x5, starting transfers between devices: none -> 52.3 us  [the longest x2 26.5 us: gather_rows(): lax.all_to_all(jnp.broadcast_to(x[None], (count,) + x.shape), axis, 0, 0,...]
    all_gather x2 -> x1, waiting for transfers between devices: 84.8 us -> 41 us  [shards(): all_cot = lax.all_gather(cotangent, 'tensor', axis=0, tiled=True)]
    psum x1, blocking collectives: 46.3 us -> 87.1 us  [shards(): lax.psum((gate_backward_piece, up_backward_piece), 'tensor')]
    all_gather x3 -> x2, blocking collectives: 60.5 us -> 38.8 us  [the longest x1 23.6 us: shards(): lax.all_gather(jnp.concatenate([gate_backward.astype(jnp.bfloat16).reshap...]
  transfers between devices with their start and end apart: 13 -> 7, of which waited for: 11 -> 5; matrix products, arithmetic and copies ran while one was open for 13% -> 22% of each run, Pallas kernels for 0% -> 0%
where the time goes in v1:
time: 552 us; the launch traced here: 549 us
  waiting for transfers between devices  210 us (38%)
  blocking collectives  126 us (23%)
  other arithmetic  63.4 us (11%)
  starting transfers between devices  52.4 us (9%)
  local copies, waits for them, and re-layouts  41.5 us (8%)
  matrix products  40.5 us (7%)
  between operations  14.5 us (3%)
    all_to_all x3, waiting for transfers between devices, scatter_sum(): got = lax.all_to_all(pieces, axis, 0, 0, tiled=False)  112 us
    psum x1, blocking collectives, shards(): lax.psum((gate_backward_piece, up_backward_piece), 'tensor')  87.1 us
    gather x3, other arithmetic, shards(): token_slots = owners[token_tenants]  42.3 us
    all_gather x1, waiting for transfers between devices, shards(): all_cot = lax.all_gather(cotangent, 'tensor', axis=0, tiled=True)  41 us
    all_to_all x2, waiting for transfers between devices, gather_rows(): lax.all_to_all(jnp.broadcast_to(x[None], (count,) + x.shape), axis, 0, 0,...  35.7 us
    all_to_all x2, starting transfers between devices, gather_rows(): lax.all_to_all(jnp.broadcast_to(x[None], (count,) + x.shape), axis, 0, 0,...  26.5 us
    all_to_all x3, starting transfers between devices, scatter_sum(): got = lax.all_to_all(pieces, axis, 0, 0, tiled=False)  25.8 us
    all_gather x1, blocking collectives, shards(): lax.all_gather(jnp.concatenate([gate_backward.astype(jnp.bfloat16).reshap...  23.6 us
  transfers between devices with their start and end apart: 7, of which 5 were waited for; matrix products, arithmetic and copies ran while one was open for 22% of the time, Pallas kernels for 0%

profile of v1, /device:TPU:8, one launch (start us, length us, event | category | flops | bytes accessed | tf_op | source)
XLA Modules:
  0.0 548.7 jit_solution(5057442251980211274)
XLA Ops:
  11.2 41.0 %all-gather.5.cloned.1.call-done = bf16[2048,512]{1,0:T(8,128)(2,1)} async-done(((bf16[128,512]{1,0:T(8,128)(2,1)}), bf16[2048,512]{1,0:T(8,128)(2,1)}) %all-gather.5.cloned.1.call-update) | async-done | bytes 2097168 | tf_op jit(solution)/shard_map/all_gather | solution.py:64
  54.7 3.7 convolution_convert_fusion
  58.4 2.3 copy_bitcast_fusion.1
  60.7 7.3 %all-to-all-start.3 = ((bf16[16,128,912]{1,2,0:T(8,128)(2,1)}), bf16[16,128,912]{1,2,0:T(8,128)(2,1)}, u32[]{:S(2)}, u32[]{:S(2)}) async-start(bf16[16,128,912]{1,2,0:T(8,128)(2,1)} %copy_bitcast_fusion.1), calls=%async_computation.3 | async-start | bytes 7471104 | tf_op jit(solution)/shard_map/all_to_all | solution.py:15
  71.5 20.3 %all-gather.3.cloned.1.call-done = bf16[2048,512]{1,0:T(8,128)(2,1)} async-done(((bf16[128,512]{1,0:T(8,128)(2,1)}), bf16[2048,512]{1,0:T(8,128)(2,1)}) %all-gather.3.cloned.1.call-update) | async-done | bytes 2097168 | tf_op jit(solution)/shard_map/all_gather | solution.py:63
  94.3 2.3 fusion.4
  96.9 3.9 convolution_convert_fusion.1
  102.9 3.8 copy_bitcast_fusion
  106.7 10.6 %all-to-all-done.3 = bf16[16,128,912]{1,2,0:T(8,128)(2,1)} async-done(((bf16[16,128,912]{1,2,0:T(8,128)(2,1)}), bf16[16,128,912]{1,2,0:T(8,128)(2,1)}, u32[]{:S(2)}, u32[]{:S(2)}) %all-to-all-start.3) | async-done | bytes 3735584 | tf_op jit(solution)/shard_map/all_to_all | solution.py:15
  117.3 14.0 %all-to-all-start = ((bf16[16,128,1824]{1,2,0:T(8,128)(2,1)}), bf16[16,128,1824]{1,2,0:T(8,128)(2,1)}, u32[]{:S(2)}, u32[]{:S(2)}) async-start(bf16[16,128,1824]{1,2,0:T(8,128)(2,1)} %copy_bitcast_fusion), calls=%async_computation | async-start | bytes 14942208 | tf_op jit(solution)/shard_map/all_to_all | solution.py:15
  136.7 2.6 convert_reduce_fusion.1
  140.6 101.4 %all-to-all-done = bf16[16,128,1824]{1,2,0:T(8,128)(2,1)} async-done(((bf16[16,128,1824]{1,2,0:T(8,128)(2,1)}), bf16[16,128,1824]{1,2,0:T(8,128)(2,1)}, u32[]{:S(2)}, u32[]{:S(2)}) %all-to-all-start) | async-done | bytes 7471136 | tf_op jit(solution)/shard_map/all_to_all | solution.py:15
  242.0 4.2 convert_reduce_fusion
  252.5 2.4 multiply_convert_fusion.1
  256.0 2.3 broadcast_in_dim.14
  258.3 18.3 %all-to-all-start.1 = ((bf16[16,128,896]{2,1,0:T(8,128)(2,1)}), bf16[16,128,896]{2,1,0:T(8,128)(2,1)}, u32[]{:S(2)}, u32[]{:S(2)}) async-start(bf16[16,128,896]{2,1,0:T(8,128)(2,1)} %broadcast_in_dim.14), calls=%async_computation.1 | async-start | bytes 7340032 | tf_op jit(solution)/shard_map/all_to_all | solution.py:21
  282.4 35.7 %all-to-all-done.1 = bf16[16,128,896]{2,1,0:T(8,128)(2,1)} async-done(((bf16[16,128,896]{2,1,0:T(8,128)(2,1)}), bf16[16,128,896]{2,1,0:T(8,128)(2,1)}, u32[]{:S(2)}, u32[]{:S(2)}) %all-to-all-start.1) | async-done | bytes 3670048 | tf_op jit(solution)/shard_map/all_to_all | solution.py:21
  318.1 2.7 broadcast_in_dim.17
  320.8 8.2 %all-to-all-start.4 = ((bf16[16,2,2,16,896]{4,1,3,2,0:T(2,128)(2,1)}), bf16[16,2,2,16,896]{4,1,3,2,0:T(2,128)(2,1)}, u32[]{:S(2)}, u32[]{:S(2)}) async-start(bf16[16,2,2,16,896]{4,1,3,2,0:T(2,128)(2,1)} %broadcast_in_dim.17), calls=%async_computation.4 | async-start | bytes 3670016 | tf_op jit(solution)/shard_map/all_to_all | solution.py:21
  329.0 5.1 compare_select_fusion.1
  335.5 35.7 %select_select_fusion = s32[2048]{0:T(1024)S(1)} fusion(pred[2048]{0:T(1024)(128)(4,1)S(1)} %get-tuple-element.91, pred[2048]{0:T(1024)(128)(4,1)S(1)} %get-tuple-element.90, pred[2048]{0:T(1024)(128)(4,1)S(1)} %get-tuple-element.89, pred[2048]{0:T(1024)(128)(4,1)S(1)} %get-tuple-element.88, pred[2048]{0:T(1024)(128)(4,1)S(1)} %get-tuple-element.87, ...), kind=kLoop, calls=%fused_computation.141 | loop fusion | flops 116736 | bytes 133348 | tf_op jit(solution)/shard_map/gather | solution.py:232
  371.3 3.2 convolution_convert_fusion.4
  374.8 4.7 convolution_convert_fusion.3
  381.2 4.6 all-to-all-start.2
  389.1 87.1 %all-reduce = (bf16[2,64,16]{1,2,0:T(8,128)(2,1)S(1)}, bf16[2,64,16]{1,2,0:T(8,128)(2,1)S(1)}) all-reduce(f32[2,64,16]{1,2,0:T(8,128)S(1)} %convolution_multiply_fusion.6, f32[2,64,16]{1,2,0:T(8,128)S(1)} %convolution_multiply_fusion.7), channel_id=1, replica_groups=mesh['dp'=16,'tensor'=16] {'tensor'}, use_global_device_ids=true, to_apply=%region_4.5 | all-reduce | flops 4096 | bytes 24576 | tf_op jit(solution)/shard_map/psum | solution.py:179
  476.4 23.6 %all_gather.14 = bf16[2048,48]{0,1:T(8,128)(2,1)S(1)} all-gather(bf16[128,48]{0,1:T(8,128)(2,1)S(1)} %pad_maximum_fusion.1), channel_id=1, replica_groups=mesh['dp'=16,'tensor'=16] {'dp'}, dimensions={0}, use_global_device_ids=true | all-gather | bytes 208896 | tf_op jit(solution)/shard_map/all_gather | solution.py:198
  500.1 2.7 fusion.46
  503.9 4.0 copy.107
  507.9 5.0 reshape.254
  517.2 3.4 convolution_bitcast_fusion
  522.6 15.3 %all_gather.15 = bf16[2048,16]{0,1:T(8,128)(2,1)S(1)} all-gather(bf16[128,16]{0,1:T(8,128)(2,1)S(1)} %slice.179), channel_id=1, replica_groups=mesh['dp'=16,'tensor'=16] {'tensor'}, dimensions={0}, use_global_device_ids=true | all-gather | bytes 69632 | tf_op jit(solution)/shard_map/all_gather | solution.py:129
  539.1 2.7 fusion.6
  (116 shorter events, 50.2 us)
Async XLA Ops:
  7.2 128.9 %copy-start = (bf16[64,896,16]{1,2,0:T(8,128)(2,1)S(1)}, bf16[64,896,16]{1,2,0:T(8,128)(2,1)}, u32[]{:S(2)}) copy-start(bf16[64,896,16]{1,2,0:T(8,128)(2,1)} %param.23) | copy-start | bytes 5505028
  7.2 47.5 %copy-start.15 = (bf16[896,512]{1,0:T(8,128)(2,1)S(1)}, bf16[896,512]{1,0:T(8,128)(2,1)}, u32[]{:S(2)}) copy-start(bf16[896,512]{1,0:T(8,128)(2,1)} %param.17) | copy-start | bytes 2752516
  7.2 45.0 %all-gather.5.cloned.1.call-start = ((), (), s32[]{:S(2)}) async-start(), calls=%async_computation.6 | async-start | bytes 2228224 | tf_op jit(solution)/shard_map/all_gather | solution.py:64
  7.9 83.9 %all-gather.3.cloned.1.call-start = ((), (), s32[]{:S(2)}) async-start(), calls=%async_computation.5 | async-start | bytes 2228224 | tf_op jit(solution)/shard_map/all_gather | solution.py:63
  9.3 267.3 %copy-start.9 = (s32[1024]{0:T(1024)}, s32[1024]{0:T(1024)S(1)}, u32[]{:S(2)}) copy-start(s32[1024]{0:T(1024)S(1)} %pad_clamp_fusion.2) | copy-start | bytes 12292
  60.7 56.7 %all-to-all-start.3 = ((bf16[16,128,912]{1,2,0:T(8,128)(2,1)}), bf16[16,128,912]{1,2,0:T(8,128)(2,1)}, u32[]{:S(2)}, u32[]{:S(2)}) async-start(bf16[16,128,912]{1,2,0:T(8,128)(2,1)} %copy_bitcast_fusion.1), calls=%async_computation.3 | async-start | bytes 7471104 | tf_op jit(solution)/shard_map/all_to_all | solution.py:15
  94.1 2.8 copy-start.13
  96.9 3.9 copy-start.2
  96.9 3.9 copy-start.14
  106.7 24.6 %copy-start.10 = (s32[32]{0:T(128)S(1)}, s32[32]{0:T(128)}, u32[]{:S(2)}) copy-start(s32[32]{0:T(128)} %param.24) | copy-start | bytes 388
  117.3 124.7 %all-to-all-start = ((bf16[16,128,1824]{1,2,0:T(8,128)(2,1)}), bf16[16,128,1824]{1,2,0:T(8,128)(2,1)}, u32[]{:S(2)}, u32[]{:S(2)}) async-start(bf16[16,128,1824]{1,2,0:T(8,128)(2,1)} %copy_bitcast_fusion), calls=%async_computation | async-start | bytes 14942208 | tf_op jit(solution)/shard_map/all_to_all | solution.py:15
  136.1 113.4 %copy-start.5 = (bf16[2,16,896]{2,1,0:T(8,128)(2,1)}, bf16[2,16,896]{2,1,0:T(8,128)(2,1)S(1)}, u32[]{:S(2)}) copy-start(bf16[2,16,896]{2,1,0:T(8,128)(2,1)S(1)} %gather_fusion.3) | copy-start | bytes 172036
  139.3 107.0 %copy-start.7 = (bf16[128,16]{0,1:T(8,128)(2,1)}, bf16[128,16]{0,1:T(8,128)(2,1)S(1)}, u32[]{:S(2)}) copy-start(bf16[128,16]{0,1:T(8,128)(2,1)S(1)} %slice.178) | copy-start | bytes 12292
  258.3 59.8 %all-to-all-start.1 = ((bf16[16,128,896]{2,1,0:T(8,128)(2,1)}), bf16[16,128,896]{2,1,0:T(8,128)(2,1)}, u32[]{:S(2)}, u32[]{:S(2)}) async-start(bf16[16,128,896]{2,1,0:T(8,128)(2,1)} %broadcast_in_dim.14), calls=%async_computation.1 | async-start | bytes 7340032 | tf_op jit(solution)/shard_map/all_to_all | solution.py:21
  276.6 0.8 copy-start.11
  276.6 1.5 copy-start.12
  276.7 2.1 copy-start.1
  276.7 4.9 copy-start.4
  320.8 60.4 %all-to-all-start.4 = ((bf16[16,2,2,16,896]{4,1,3,2,0:T(2,128)(2,1)}), bf16[16,2,2,16,896]{4,1,3,2,0:T(2,128)(2,1)}, u32[]{:S(2)}, u32[]{:S(2)}) async-start(bf16[16,2,2,16,896]{4,1,3,2,0:T(2,128)(2,1)} %broadcast_in_dim.17), calls=%async_computation.4 | async-start | bytes 3670016 | tf_op jit(solution)/shard_map/all_to_all | solution.py:21
  379.4 9.3 %copy-start.6 = (bf16[2,16,896]{2,1,0:T(8,128)(2,1)S(1)}, bf16[2,16,896]{2,1,0:T(8,128)(2,1)}, u32[]{:S(2)}) copy-start(bf16[2,16,896]{2,1,0:T(8,128)(2,1)} %copy-done.5) | copy-start | bytes 172036
  381.2 95.2 %copy-start.8 = (bf16[128,16]{0,1:T(8,128)(2,1)S(1)}, bf16[128,16]{0,1:T(8,128)(2,1)}, u32[]{:S(2)}) copy-start(bf16[128,16]{0,1:T(8,128)(2,1)} %copy-done.7) | copy-start | bytes 12292
  381.2 139.4 %all-to-all-start.2 = ((bf16[16,128,528]{1,2,0:T(8,128)(2,1)}), bf16[16,128,528]{1,2,0:T(8,128)(2,1)}, u32[]{:S(2)}, u32[]{:S(2)}) async-start(bf16[16,128,528]{1,2,0:T(8,128)(2,1)} %copy_bitcast_fusion.2), calls=%async_computation.2 | async-start | bytes 4325376 | tf_op jit(solution)/shard_map/all_to_all | solution.py:15
  476.4 26.4 %copy-start.3 = (bf16[2048,512]{1,0:T(8,128)(2,1)S(1)}, bf16[2048,512]{1,0:T(8,128)(2,1)}, u32[]{:S(2)}) copy-start(bf16[2048,512]{1,0:T(8,128)(2,1)} %all-gather.3.cloned.1.call-done) | copy-start | bytes 6291460
Sparse Core Ops, SparseCore 0:
  9.8 42.3 all-gather.4
  54.0 37.7 all-gather.2

commit v2 on v1

--- a/solution.py
+++ b/solution.py
@@ -61,6 +61,7 @@
     held_tenants = tensor_index * tenants_here + jnp.arange(tenants_here, dtype=jnp.int32)
     token_onehot = (token_tenants[:, None] == held_tenants[None, :]).astype(jnp.bfloat16)
     all_inputs = lax.all_gather(tokens, "tensor", axis=0, tiled=True)
+    cotangent = lax.optimization_barrier((all_inputs, cotangent))[1]
     all_cot = lax.all_gather(cotangent, "tensor", axis=0, tiled=True)
 
     gate_part = jnp.dot(all_inputs, gate_weight, preferred_element_type=jnp.float32)
@@ -126,15 +127,6 @@
         ).reshape(rows_in, feat_here)
     ).astype(jnp.bfloat16)
 
-    all_down_rank = lax.all_gather(down_rank_flat, "tensor", axis=0, tiled=True)
-    rank_weighted = (token_onehot[:, :, None] * all_down_rank[:, None, :]).reshape(
-        every_token_row, tenants_here * rank_width
-    )
-    grad_down_out = adapter_scale * (
-        lax.dot_general(rank_weighted, all_cot, contract_rows, preferred_element_type=jnp.float32)
-        .reshape(tenants_here, rank_width, feat_here)
-    )
-
     hidden_grad_part = lax.dot_general(
         all_cot, down_weight, (((1,), (1,)), ((), ())), preferred_element_type=jnp.float32
     )
@@ -144,12 +136,11 @@
         down_out[tenants],
         preferred_element_type=jnp.float32,
     ).reshape(every_token_row, rank_width)
-    back_sums = scatter_sum(
-        jnp.concatenate(
-            [hidden_grad_part.astype(jnp.bfloat16), down_back_part.astype(jnp.bfloat16)], axis=1
-        ),
-        "dp",
-    )
+    back_pieces = jnp.concatenate(
+        [hidden_grad_part.astype(jnp.bfloat16), down_back_part.astype(jnp.bfloat16)], axis=1
+    )
+    forward_sums, back_pieces = lax.optimization_barrier((forward_sums, back_pieces))
+    back_sums = scatter_sum(back_pieces, "dp")
     hidden_grad_sum = back_sums[:, :width_here]
     group_down_back = back_sums[:, width_here:].astype(jnp.bfloat16)
     down_drop = down_in[group_tenants]
@@ -176,7 +167,30 @@
     up_backward_piece = adapter_scale * jnp.einsum(
         "yae,yve->yav", up_gradient, up_raise, preferred_element_type=jnp.float32
     )
-    gate_backward, up_backward = lax.psum((gate_backward_piece, up_backward_piece), "tensor")
+    rank_partials = lax.all_gather(
+        jnp.concatenate(
+            [
+                gate_backward_piece.reshape(group_rows, rank_width),
+                up_backward_piece.reshape(group_rows, rank_width),
+                down_rank_flat.astype(jnp.float32),
+            ],
+            axis=1,
+        ),
+        "tensor",
+        axis=0,
+        tiled=False,
+    )
+    back_rank_sums = rank_partials[:, :, : 2 * rank_width].sum(0)
+    gate_backward = back_rank_sums[:, :rank_width]
+    up_backward = back_rank_sums[:, rank_width:]
+    all_down_rank = rank_partials[:, :, 2 * rank_width :].reshape(every_token_row, rank_width)
+    rank_weighted = (token_onehot[:, :, None] * all_down_rank[:, None, :]).reshape(
+        every_token_row, tenants_here * rank_width
+    )
+    grad_down_out = adapter_scale * (
+        lax.dot_general(rank_weighted, all_cot, contract_rows, preferred_element_type=jnp.float32)
+        .reshape(tenants_here, rank_width, feat_here)
+    )
 
     gate_raise_block_list = adapter_scale * jnp.einsum(
         "yap,yau->ypu", gate_rank_second, gate_gradient, preferred_element_type=jnp.float32
@@ -198,8 +212,8 @@
     all_backs = lax.all_gather(
         jnp.concatenate(
             [
-                gate_backward.astype(jnp.bfloat16).reshape(group_rows, rank_width),
-                up_backward.astype(jnp.bfloat16).reshape(group_rows, rank_width),
+                gate_backward.astype(jnp.bfloat16),
+                up_backward.astype(jnp.bfloat16),
                 group_down_back,
             ],
             axis=1,
@@ -229,8 +243,10 @@
         .reshape(feat_here, tenants_here, rank_width)
         .transpose(1, 0, 2)
     )
-    token_slots = owners[token_tenants]
-    slot_onehot = (token_slots[:, None] == own_slots[None, :]).astype(jnp.bfloat16)
+    block_slot_onehot = (owners[tenants][:, None] == own_slots[None, :]).astype(jnp.bfloat16)
+    slot_onehot = jnp.broadcast_to(
+        block_slot_onehot[:, None, :], (blocks_all, BLOCK, slots_here)
+    ).reshape(every_token_row, slots_here)
     drop_weighted = (slot_onehot[:, :, None] * all_down_back[:, None, :]).reshape(
         every_token_row, slots_here * rank_width
     )

time: 552 us -> 478 us (0.87)
  blocking collectives: 126 us -> 38.8 us
  waiting for transfers between devices: 210 us -> 284 us
  other arithmetic: 63.4 us -> 20.4 us
  starting transfers between devices: 52.4 us -> 43.3 us
    psum x1 -> x0, blocking collectives: 87.1 us -> none  [shards(): lax.psum((gate_backward_piece, up_backward_piece), 'tensor')]
    gather x3 -> x0, other arithmetic: 42.3 us -> none  [shards(): token_slots = owners[token_tenants]]
    all_to_all x3, waiting for transfers between devices: 112 us -> 150 us  [scatter_sum(): got = lax.all_to_all(pieces, axis, 0, 0, tiled=False)]
    all_gather x1, waiting for transfers between devices: 20.3 us -> 40 us  [shards(): all_inputs = lax.all_gather(tokens, 'tensor', axis=0, tiled=True)]
    all_to_all x2, waiting for transfers between devices: 35.7 us -> 53.9 us  [gather_rows(): lax.all_to_all(jnp.broadcast_to(x[None], (count,) + x.shape), axis, 0, 0,...]
    all_to_all x2, starting transfers between devices: 26.5 us -> 14.4 us  [gather_rows(): lax.all_to_all(jnp.broadcast_to(x[None], (count,) + x.shape), axis, 0, 0,...]
  transfers between devices with their start and end apart: 7 -> 7, of which waited for: 5 -> 7; matrix products, arithmetic and copies ran while one was open for 22% -> 10% of each run, Pallas kernels for 0% -> 0%
where the time goes in v2:
time: 478 us; the launch traced here: 476 us
  waiting for transfers between devices  284 us (59%)
  starting transfers between devices  43.3 us (9%)
  blocking collectives  38.8 us (8%)
  local copies, waits for them, and re-layouts  38.4 us (8%)
  matrix products  36.9 us (8%)
  other arithmetic  20.4 us (4%)
  between operations  14.5 us (3%)
    all_to_all x3, waiting for transfers between devices, scatter_sum(): got = lax.all_to_all(pieces, axis, 0, 0, tiled=False)  150 us
    all_to_all x2, waiting for transfers between devices, gather_rows(): lax.all_to_all(jnp.broadcast_to(x[None], (count,) + x.shape), axis, 0, 0,...  53.9 us
    all_gather x1, waiting for transfers between devices, shards(): all_inputs = lax.all_gather(tokens, 'tensor', axis=0, tiled=True)  40 us
    all_gather x1, waiting for transfers between devices, shards(): all_cot = lax.all_gather(cotangent, 'tensor', axis=0, tiled=True)  39.1 us
    all_to_all x3, starting transfers between devices, scatter_sum(): got = lax.all_to_all(pieces, axis, 0, 0, tiled=False)  28.8 us
    all_gather x1, blocking collectives, shards(): lax.all_gather(jnp.concatenate([gate_backward.astype(jnp.bfloat16), up_ba...  22.2 us
    all_gather x1, blocking collectives, shards(): lax.all_gather(jnp.concatenate([gate_backward_piece.reshape(group_rows, r...  16.6 us
    all_to_all x2, starting transfers between devices, gather_rows(): lax.all_to_all(jnp.broadcast_to(x[None], (count,) + x.shape), axis, 0, 0,...  14.4 us
  transfers between devices with their start and end apart: 7, of which 7 were waited for; matrix products, arithmetic and copies ran while one was open for 10% of the time, Pallas kernels for 0%

profile of v2, /device:TPU:8, one launch (start us, length us, event | category | flops | bytes accessed | tf_op | source)
XLA Modules:
  0.0 476.5 jit_solution(8798262301497184777)
XLA Ops:
  12.2 40.0 %all-gather.4.cloned.1.call-done = bf16[2048,512]{1,0:T(8,128)(2,1)} async-done(((bf16[128,512]{1,0:T(8,128)(2,1)}), bf16[2048,512]{1,0:T(8,128)(2,1)}) %all-gather.4.cloned.1.call-update) | async-done | bytes 2097168 | tf_op jit(solution)/shard_map/all_gather | solution.py:63
  52.2 2.2 fusion.3
  54.7 2.3 fusion.4
  57.2 3.9 convolution_convert_fusion.1
  63.3 3.9 copy_bitcast_fusion
  67.2 7.4 %all-to-all-start = ((bf16[16,128,1824]{1,2,0:T(8,128)(2,1)}), bf16[16,128,1824]{1,2,0:T(8,128)(2,1)}, u32[]{:S(2)}, u32[]{:S(2)}) async-start(bf16[16,128,1824]{1,2,0:T(8,128)(2,1)} %copy_bitcast_fusion), calls=%async_computation | async-start | bytes 14942208 | tf_op jit(solution)/shard_map/all_to_all | solution.py:15
  75.9 39.1 %all-gather.6.cloned.1.call-done = bf16[2048,512]{1,0:T(8,128)(2,1)} async-done(((bf16[128,512]{1,0:T(8,128)(2,1)}), bf16[2048,512]{1,0:T(8,128)(2,1)}) %all-gather.6.cloned.1.call-update) | async-done | bytes 2097168 | tf_op jit(solution)/shard_map/all_gather | solution.py:65
  115.0 2.2 fusion.2
  117.5 3.9 convolution_convert_fusion
  121.4 2.3 pad_maximum_fusion
  123.8 75.1 %all-to-all-done = bf16[16,128,1824]{1,2,0:T(8,128)(2,1)} async-done(((bf16[16,128,1824]{1,2,0:T(8,128)(2,1)}), bf16[16,128,1824]{1,2,0:T(8,128)(2,1)}, u32[]{:S(2)}, u32[]{:S(2)}) %all-to-all-start) | async-done | bytes 7471136 | tf_op jit(solution)/shard_map/all_to_all | solution.py:15
  198.9 4.4 convert_reduce_fusion
  203.3 2.5 copy_bitcast_fusion.1
  205.8 16.8 %all-to-all-start.3 = ((bf16[16,128,912]{1,2,0:T(8,128)(2,1)}), bf16[16,128,912]{1,2,0:T(8,128)(2,1)}, u32[]{:S(2)}, u32[]{:S(2)}) async-start(bf16[16,128,912]{1,2,0:T(8,128)(2,1)} %copy_bitcast_fusion.1), calls=%async_computation.3 | async-start | bytes 7471104 | tf_op jit(solution)/shard_map/all_to_all | solution.py:15
  230.2 40.8 %all-to-all-done.3 = bf16[16,128,912]{1,2,0:T(8,128)(2,1)} async-done(((bf16[16,128,912]{1,2,0:T(8,128)(2,1)}), bf16[16,128,912]{1,2,0:T(8,128)(2,1)}, u32[]{:S(2)}, u32[]{:S(2)}) %all-to-all-start.3) | async-done | bytes 3735584 | tf_op jit(solution)/shard_map/all_to_all | solution.py:15
  271.0 2.6 convert_reduce_fusion.1
  276.8 2.4 multiply_convert_fusion.1
  280.3 2.3 broadcast_in_dim.16
  282.6 6.5 %all-to-all-start.1 = ((bf16[16,128,896]{2,1,0:T(8,128)(2,1)}), bf16[16,128,896]{2,1,0:T(8,128)(2,1)}, u32[]{:S(2)}, u32[]{:S(2)}) async-start(bf16[16,128,896]{2,1,0:T(8,128)(2,1)} %broadcast_in_dim.16), calls=%async_computation.1 | async-start | bytes 7340032 | tf_op jit(solution)/shard_map/all_to_all | solution.py:21
  289.9 41.6 %all-to-all-done.1 = bf16[16,128,896]{2,1,0:T(8,128)(2,1)} async-done(((bf16[16,128,896]{2,1,0:T(8,128)(2,1)}), bf16[16,128,896]{2,1,0:T(8,128)(2,1)}, u32[]{:S(2)}, u32[]{:S(2)}) %all-to-all-start.1) | async-done | bytes 3670048 | tf_op jit(solution)/shard_map/all_to_all | solution.py:21
  331.5 2.7 broadcast_in_dim.19
  334.1 8.0 %all-to-all-start.4 = ((bf16[16,2,2,16,896]{4,1,3,2,0:T(2,128)(2,1)}), bf16[16,2,2,16,896]{4,1,3,2,0:T(2,128)(2,1)}, u32[]{:S(2)}, u32[]{:S(2)}) async-start(bf16[16,2,2,16,896]{4,1,3,2,0:T(2,128)(2,1)} %broadcast_in_dim.19), calls=%async_computation.4 | async-start | bytes 3670016 | tf_op jit(solution)/shard_map/all_to_all | solution.py:21
  342.8 3.2 convolution_convert_fusion.4
  346.3 4.7 convolution_convert_fusion.3
  352.7 12.4 %all-to-all-done.4 = bf16[16,2,2,16,896]{4,1,3,2,0:T(2,128)(2,1)} async-done(((bf16[16,2,2,16,896]{4,1,3,2,0:T(2,128)(2,1)}), bf16[16,2,2,16,896]{4,1,3,2,0:T(2,128)(2,1)}, u32[]{:S(2)}, u32[]{:S(2)}) %all-to-all-start.4) | async-done | bytes 1835040 | tf_op jit(solution)/shard_map/all_to_all | solution.py:21
  365.0 4.6 all-to-all-start.2
  373.2 4.0 copy.103
  377.2 5.0 %reshape.250 = bf16[32,2,16,896]{3,0,2,1:T(8,128)(2,1)} reshape(bf16[16,2,2,16,896]{4,1,0,3,2:T(2,128)(2,1)} %copy.103) | data formatting | bytes 3670016 | tf_op jit(solution)/shard_map/reshape | solution.py:22
  386.6 33.8 %all-to-all-done.2 = bf16[16,128,528]{1,2,0:T(8,128)(2,1)} async-done(((bf16[16,128,528]{1,2,0:T(8,128)(2,1)}), bf16[16,128,528]{1,2,0:T(8,128)(2,1)}, u32[]{:S(2)}, u32[]{:S(2)}) %all-to-all-start.2) | async-done | bytes 2162720 | tf_op jit(solution)/shard_map/all_to_all | solution.py:15
  422.3 16.6 %all-gather = f32[2048,48]{0,1:T(8,128)S(1)} all-gather(f32[128,48]{0,1:T(8,128)S(1)} %pad_maximum_fusion.2), channel_id=2, replica_groups=mesh['dp'=16,'tensor'=16] {'tensor'}, dimensions={0}, use_global_device_ids=true | all-gather | bytes 417792 | tf_op jit(solution)/shard_map/all_gather | solution.py:170
  439.1 22.2 %all_gather.19 = bf16[2048,48]{0,1:T(8,128)(2,1)S(1)} all-gather(bf16[128,48]{0,1:T(8,128)(2,1)S(1)} %pad_maximum_fusion.3), channel_id=1, replica_groups=mesh['dp'=16,'tensor'=16] {'dp'}, dimensions={0}, use_global_device_ids=true | all-gather | bytes 208896 | tf_op jit(solution)/shard_map/all_gather | solution.py:212
  462.6 3.5 convolution_bitcast_fusion
  (113 shorter events, 39.1 us)
Async XLA Ops:
  7.2 215.5 %copy-start = (bf16[64,896,16]{1,2,0:T(8,128)(2,1)S(1)}, bf16[64,896,16]{1,2,0:T(8,128)(2,1)}, u32[]{:S(2)}) copy-start(bf16[64,896,16]{1,2,0:T(8,128)(2,1)} %param.23) | copy-start | bytes 5505028
  7.2 45.0 %all-gather.4.cloned.1.call-start = ((), (), s32[]{:S(2)}) async-start(), calls=%async_computation.5 | async-start | bytes 2228224 | tf_op jit(solution)/shard_map/all_gather | solution.py:63
  54.4 2.8 copy-start.13
  57.2 3.9 copy-start.2
  57.2 3.9 copy-start.14
  67.2 8.1 %copy-start.11 = (bf16[64,16,512]{2,1,0:T(8,128)(2,1)S(1)}, bf16[64,16,512]{2,1,0:T(8,128)(2,1)}, u32[]{:S(2)}) copy-start(bf16[64,16,512]{2,1,0:T(8,128)(2,1)} %param.20) | copy-start | bytes 3145732
  67.2 131.7 %all-to-all-start = ((bf16[16,128,1824]{1,2,0:T(8,128)(2,1)}), bf16[16,128,1824]{1,2,0:T(8,128)(2,1)}, u32[]{:S(2)}, u32[]{:S(2)}) async-start(bf16[16,128,1824]{1,2,0:T(8,128)(2,1)} %copy_bitcast_fusion), calls=%async_computation | async-start | bytes 14942208 | tf_op jit(solution)/shard_map/all_to_all | solution.py:15
  74.6 40.5 %all-gather.6.cloned.1.call-start = ((), (), s32[]{:S(2)}) async-start(), calls=%async_computation.6 | async-start | bytes 2228224 | tf_op jit(solution)/shard_map/all_gather | solution.py:65
  198.9 4.4 copy-start.4
  205.8 16.8 %copy-start.12 = (s32[32]{0:T(128)S(1)}, s32[32]{0:T(128)}, u32[]{:S(2)}) copy-start(s32[32]{0:T(128)} %param.24) | copy-start | bytes 388
  205.8 65.2 %all-to-all-start.3 = ((bf16[16,128,912]{1,2,0:T(8,128)(2,1)}), bf16[16,128,912]{1,2,0:T(8,128)(2,1)}, u32[]{:S(2)}, u32[]{:S(2)}) async-start(bf16[16,128,912]{1,2,0:T(8,128)(2,1)} %copy_bitcast_fusion.1), calls=%async_computation.3 | async-start | bytes 7471104 | tf_op jit(solution)/shard_map/all_to_all | solution.py:15
  225.3 48.3 %copy-start.9 = (bf16[2,16,896]{2,1,0:T(8,128)(2,1)}, bf16[2,16,896]{2,1,0:T(8,128)(2,1)S(1)}, u32[]{:S(2)}) copy-start(bf16[2,16,896]{2,1,0:T(8,128)(2,1)S(1)} %gather_fusion.2) | copy-start | bytes 172036
  227.4 2.8 copy-start.7
  282.6 6.5 %copy-start.6 = (bf16[128,896]{0,1:T(8,128)(2,1)S(1)}, bf16[128,896]{0,1:T(8,128)(2,1)}, u32[]{:S(2)}) copy-start(bf16[128,896]{0,1:T(8,128)(2,1)} %get-tuple-element.41) | copy-start | bytes 688132
  282.6 48.9 %all-to-all-start.1 = ((bf16[16,128,896]{2,1,0:T(8,128)(2,1)}), bf16[16,128,896]{2,1,0:T(8,128)(2,1)}, u32[]{:S(2)}, u32[]{:S(2)}) async-start(bf16[16,128,896]{2,1,0:T(8,128)(2,1)} %broadcast_in_dim.16), calls=%async_computation.1 | async-start | bytes 7340032 | tf_op jit(solution)/shard_map/all_to_all | solution.py:21
  334.1 30.9 %all-to-all-start.4 = ((bf16[16,2,2,16,896]{4,1,3,2,0:T(2,128)(2,1)}), bf16[16,2,2,16,896]{4,1,3,2,0:T(2,128)(2,1)}, u32[]{:S(2)}, u32[]{:S(2)}) async-start(bf16[16,2,2,16,896]{4,1,3,2,0:T(2,128)(2,1)} %broadcast_in_dim.19), calls=%async_computation.4 | async-start | bytes 3670016 | tf_op jit(solution)/shard_map/all_to_all | solution.py:21
  350.9 18.7 %copy-start.1 = (s32[64]{0:T(128)S(1)}, s32[64]{0:T(128)}, u32[]{:S(2)}) copy-start(s32[64]{0:T(128)} %param.25) | copy-start | bytes 772
  350.9 21.7 %copy-start.10 = (bf16[2,16,896]{2,1,0:T(8,128)(2,1)S(1)}, bf16[2,16,896]{2,1,0:T(8,128)(2,1)}, u32[]{:S(2)}) copy-start(bf16[2,16,896]{2,1,0:T(8,128)(2,1)} %copy-done.9) | copy-start | bytes 172036
  352.7 20.3 %copy-start.8 = (bf16[2,16,896]{2,1,0:T(8,128)(2,1)S(1)}, bf16[2,16,896]{2,1,0:T(8,128)(2,1)}, u32[]{:S(2)}) copy-start(bf16[2,16,896]{2,1,0:T(8,128)(2,1)} %copy-done.7) | copy-start | bytes 172036
  365.0 55.3 %all-to-all-start.2 = ((bf16[16,128,528]{1,2,0:T(8,128)(2,1)}), bf16[16,128,528]{1,2,0:T(8,128)(2,1)}, u32[]{:S(2)}, u32[]{:S(2)}) async-start(bf16[16,128,528]{1,2,0:T(8,128)(2,1)} %copy_bitcast_fusion.2), calls=%async_computation.2 | async-start | bytes 4325376 | tf_op jit(solution)/shard_map/all_to_all | solution.py:15
  462.6 3.6 copy-start.3
  466.1 2.3 copy-start.5
Sparse Core Ops, SparseCore 0:
  9.8 42.3 all-gather.3
  77.2 37.7 all-gather.5

commit v3 on v2

--- a/solution.py
+++ b/solution.py
@@ -20,6 +20,26 @@
     count = lax.axis_size(axis)
     got = lax.all_to_all(jnp.broadcast_to(x[None], (count,) + x.shape), axis, 0, 0, tiled=False)
     return got.reshape((count * x.shape[0],) + x.shape[1:])
+
+
+TENSOR = ("tz", "tc")
+
+
+def gather_tensor(x):
+    along_z = lax.all_gather(x, "tz", axis=0, tiled=False)
+    both = lax.all_gather(along_z, "tc", axis=1, tiled=False)
+    return both.reshape((-1,) + x.shape[1:])
+
+
+def scatter_sum_tensor(x):
+    count_z = lax.axis_size("tz")
+    count_c = lax.axis_size("tc")
+    pieces = x.astype(jnp.bfloat16).reshape(
+        (count_z, count_c, x.shape[0] // (count_z * count_c)) + x.shape[1:]
+    )
+    pair = lax.all_to_all(pieces, "tc", 1, 1, tiled=False).astype(jnp.float32).sum(1)
+    got = lax.all_to_all(pair.astype(jnp.bfloat16), "tz", 0, 0, tiled=False)
+    return got.astype(jnp.float32).sum(0)
 
 
 def shards(
@@ -39,9 +59,9 @@
 ):
     highest = lax.Precision.HIGHEST
     dp_count = lax.axis_size("dp")
-    tensor_count = lax.axis_size("tensor")
+    tensor_count = lax.axis_size("tz") * lax.axis_size("tc")
     dp_index = lax.axis_index("dp")
-    tensor_index = lax.axis_index("tensor")
+    tensor_index = lax.axis_index("tz") * lax.axis_size("tc") + lax.axis_index("tc")
     rows_in = tokens.shape[0]
     feat_here = tokens.shape[1]
     width_here = gate_weight.shape[1]
@@ -60,9 +80,9 @@
     token_tenants = jnp.broadcast_to(tenants[:, None], (blocks_all, BLOCK)).reshape(every_token_row)
     held_tenants = tensor_index * tenants_here + jnp.arange(tenants_here, dtype=jnp.int32)
     token_onehot = (token_tenants[:, None] == held_tenants[None, :]).astype(jnp.bfloat16)
-    all_inputs = lax.all_gather(tokens, "tensor", axis=0, tiled=True)
+    all_inputs = gather_tensor(tokens)
     cotangent = lax.optimization_barrier((all_inputs, cotangent))[1]
-    all_cot = lax.all_gather(cotangent, "tensor", axis=0, tiled=True)
+    all_cot = gather_tensor(cotangent)
 
     gate_part = jnp.dot(all_inputs, gate_weight, preferred_element_type=jnp.float32)
     up_part = jnp.dot(all_inputs, up_weight, preferred_element_type=jnp.float32)
@@ -109,11 +129,10 @@
         down_in[tenants],
         preferred_element_type=jnp.float32,
     ).reshape(every_token_row, rank_width)
-    down_sums = scatter_sum(
+    down_sums = scatter_sum_tensor(
         jnp.concatenate(
             [out_part.astype(jnp.bfloat16), down_rank_part.astype(jnp.bfloat16)], axis=1
-        ),
-        "tensor",
+        )
     )
     out_sum = down_sums[:, :feat_here]
     down_rank_flat = down_sums[:, feat_here:].astype(jnp.bfloat16)
@@ -176,7 +195,7 @@
             ],
             axis=1,
         ),
-        "tensor",
+        TENSOR,
         axis=0,
         tiled=False,
     )
@@ -269,28 +288,30 @@
 
 
 def solution(mesh):
+    devices = mesh.devices.reshape(mesh.shape["dp"], mesh.shape["tensor"] // 2, 2)
+    split_mesh = jax.sharding.Mesh(devices, ("dp",) + TENSOR)
     in_specs = (
-        P("tensor", "dp"),
-        P("tensor", "dp"),
-        P("dp", "tensor"),
-        P("dp", "tensor"),
-        P("tensor", "dp"),
+        P(TENSOR, "dp"),
+        P(TENSOR, "dp"),
+        P("dp", TENSOR),
+        P("dp", TENSOR),
+        P(TENSOR, "dp"),
         P(None, "dp", None),
         P(None, "dp", None),
         P(None, None, "dp"),
-        P(None, None, "tensor"),
-        P(None, None, "tensor"),
-        P(None, "tensor", None),
+        P(None, None, TENSOR),
+        P(None, None, TENSOR),
+        P(None, TENSOR, None),
         P(),
         P(),
     )
     out_specs = (
-        P("tensor", "dp"),
-        P("tensor", "dp", None),
-        P("tensor", "dp", None),
-        P("tensor", None, "dp"),
-        P("dp", None, "tensor"),
-        P("dp", None, "tensor"),
-        P("dp", "tensor", None),
-    )
-    return jax.shard_map(shards, mesh=mesh, in_specs=in_specs, out_specs=out_specs, check_vma=False)
+        P(TENSOR, "dp"),
+        P(TENSOR, "dp", None),
+        P(TENSOR, "dp", None),
+        P(TENSOR, None, "dp"),
+        P("dp", None, TENSOR),
+        P("dp", None, TENSOR),
+        P("dp", TENSOR, None),
+    )
+    return jax.shard_map(shards, mesh=split_mesh, in_specs=in_specs, out_specs=out_specs, check_vma=False)

time: 478 us -> 500 us (1.046)
  local copies, waits for them, and re-layouts: 38.4 us -> 49.6 us
  blocking collectives: 38.8 us -> 44.4 us
    all_to_all x3 -> x2, waiting for transfers between devices: 150 us -> 103 us  [scatter_sum(): got = lax.all_to_all(pieces, axis, 0, 0, tiled=False)]
    all_gather x2 -> x4, waiting for transfers between devices: 79.1 us -> 112 us  [the longest x2 84.7 us: gather_tensor(): along_z = lax.all_gather(x, 'tz', axis=0, tiled=False)]
    all_to_all x2, waiting for transfers between devices: 53.9 us -> 63.1 us  [gather_rows(): lax.all_to_all(jnp.broadcast_to(x[None], (count,) + x.shape), axis, 0, 0,...]
    all_to_all x3 -> x2, starting transfers between devices: 28.8 us -> 19.7 us  [scatter_sum(): got = lax.all_to_all(pieces, axis, 0, 0, tiled=False)]
    all_to_all x0 -> x1, waiting for transfers between devices: none -> 8.93 us  [scatter_sum_tensor(): got = lax.all_to_all(pair.astype(jnp.bfloat16), 'tz', 0, 0, tiled=False)]
    reshape x0 -> x2, local copies, waits for them, and re-layouts: none -> 8.05 us  [scatter_sum_tensor(): x.astype(jnp.bfloat16)]
    all_to_all x0 -> x1, starting transfers between devices: none -> 6.58 us  [scatter_sum_tensor(): got = lax.all_to_all(pair.astype(jnp.bfloat16), 'tz', 0, 0, tiled=False)]
    all_to_all x0 -> x1, blocking collectives: none -> 6.35 us  [scatter_sum_tensor(): lax.all_to_all(pieces, 'tc', 1, 1, tiled=False).astype(jnp.float32).sum(1)]
  transfers between devices with their start and end apart: 7 -> 9, of which waited for: 7 -> 9; matrix products, arithmetic and copies ran while one was open for 10% -> 9% of each run, Pallas kernels for 0% -> 0%
where the time goes in v3:
time: 500 us; the launch traced here: 499 us
  waiting for transfers between devices  288 us (58%)
  local copies, waits for them, and re-layouts  49.6 us (10%)
  blocking collectives  44.4 us (9%)
  starting transfers between devices  40.7 us (8%)
  matrix products  38.2 us (8%)
  other arithmetic  23.4 us (5%)
  between operations  14.3 us (3%)
    all_to_all x2, waiting for transfers between devices, scatter_sum(): got = lax.all_to_all(pieces, axis, 0, 0, tiled=False)  103 us
    all_gather x2, waiting for transfers between devices, gather_tensor(): along_z = lax.all_gather(x, 'tz', axis=0, tiled=False)  84.7 us
    all_to_all x2, waiting for transfers between devices, gather_rows(): lax.all_to_all(jnp.broadcast_to(x[None], (count,) + x.shape), axis, 0, 0,...  63.1 us
    all_gather x2, waiting for transfers between devices, gather_tensor(): both = lax.all_gather(along_z, 'tc', axis=1, tiled=False)  27.3 us
    all_gather x1, blocking collectives, shards(): lax.all_gather(jnp.concatenate([gate_backward.astype(jnp.bfloat16), up_ba...  22.2 us
    all_to_all x2, starting transfers between devices, scatter_sum(): got = lax.all_to_all(pieces, axis, 0, 0, tiled=False)  19.7 us
    all_gather x1, blocking collectives, shards(): lax.all_gather(jnp.concatenate([gate_backward_piece.reshape(group_rows, r...  15.9 us
    all_to_all x2, starting transfers between devices, gather_rows(): lax.all_to_all(jnp.broadcast_to(x[None], (count,) + x.shape), axis, 0, 0,...  14.2 us
  transfers between devices with their start and end apart: 9, of which 9 were waited for; matrix products, arithmetic and copies ran while one was open for 9% of the time, Pallas kernels for 0%

profile of v3, /device:TPU:8, one launch (start us, length us, event | category | flops | bytes accessed | tf_op | source)
XLA Modules:
  0.0 498.7 jit_solution(3002956575827205365)
XLA Ops:
  8.0 43.1 %all-gather.10.cloned.1.call-done = bf16[1024,512]{1,0:T(8,128)(2,1)} async-done(((bf16[128,512]{1,0:T(8,128)(2,1)}), bf16[1024,512]{1,0:T(8,128)(2,1)}) %all-gather.10.cloned.1.call-update) | async-done | bytes 1048592 | tf_op jit(solution)/shard_map/all_gather | solution.py:29
  55.4 11.8 %all-gather.12.cloned.1.call-done = bf16[8,256,512]{2,1,0:T(8,128)(2,1)} async-done(((bf16[8,128,512]{2,1,0:T(8,128)(2,1)}), bf16[8,256,512]{2,1,0:T(8,128)(2,1)}) %all-gather.12.cloned.1.call-update) | async-done | bytes 2097168 | tf_op jit(solution)/shard_map/all_gather | solution.py:30
  72.3 3.9 convolution_convert_fusion.1
  78.3 3.9 copy_bitcast_fusion
  82.2 7.4 %all-to-all-start = ((bf16[16,128,1824]{1,2,0:T(8,128)(2,1)}), bf16[16,128,1824]{1,2,0:T(8,128)(2,1)}, u32[]{:S(2)}, u32[]{:S(2)}) async-start(bf16[16,128,1824]{1,2,0:T(8,128)(2,1)} %copy_bitcast_fusion), calls=%async_computation | async-start | bytes 14942208 | tf_op jit(solution)/shard_map/all_to_all | solution.py:15
  90.4 41.5 %all-gather.14.cloned.1.call-done = bf16[1024,512]{1,0:T(8,128)(2,1)} async-done(((bf16[128,512]{1,0:T(8,128)(2,1)}), bf16[1024,512]{1,0:T(8,128)(2,1)}) %all-gather.14.cloned.1.call-update) | async-done | bytes 1048592 | tf_op jit(solution)/shard_map/all_gather | solution.py:29
  132.6 15.5 %all-gather.16.cloned.1.call-done = bf16[8,256,512]{2,1,0:T(8,128)(2,1)} async-done(((bf16[8,128,512]{2,1,0:T(8,128)(2,1)}), bf16[8,256,512]{2,1,0:T(8,128)(2,1)}) %all-gather.16.cloned.1.call-update) | async-done | bytes 2097168 | tf_op jit(solution)/shard_map/all_gather | solution.py:30
  150.6 3.9 convolution_convert_fusion
  156.8 62.3 %all-to-all-done = bf16[16,128,1824]{1,2,0:T(8,128)(2,1)} async-done(((bf16[16,128,1824]{1,2,0:T(8,128)(2,1)}), bf16[16,128,1824]{1,2,0:T(8,128)(2,1)}, u32[]{:S(2)}, u32[]{:S(2)}) %all-to-all-start) | async-done | bytes 7471136 | tf_op jit(solution)/shard_map/all_to_all | solution.py:15
  219.1 4.4 convert_reduce_fusion
  223.5 2.5 copy_bitcast_fusion.1
  226.0 12.3 %all-to-all-start.4 = ((bf16[16,128,912]{1,2,0:T(8,128)(2,1)}), bf16[16,128,912]{1,2,0:T(8,128)(2,1)}, u32[]{:S(2)}, u32[]{:S(2)}) async-start(bf16[16,128,912]{1,2,0:T(8,128)(2,1)} %copy_bitcast_fusion.1), calls=%async_computation.4 | async-start | bytes 7471104 | tf_op jit(solution)/shard_map/all_to_all | solution.py:15
  246.5 40.3 %all-to-all-done.4 = bf16[16,128,912]{1,2,0:T(8,128)(2,1)} async-done(((bf16[16,128,912]{1,2,0:T(8,128)(2,1)}), bf16[16,128,912]{1,2,0:T(8,128)(2,1)}, u32[]{:S(2)}, u32[]{:S(2)}) %all-to-all-start.4) | async-done | bytes 3735584 | tf_op jit(solution)/shard_map/all_to_all | solution.py:15
  286.8 2.6 convert_reduce_fusion.1
  297.4 6.6 %all-to-all-start.1 = ((bf16[16,128,896]{2,1,0:T(8,128)(2,1)}), bf16[16,128,896]{2,1,0:T(8,128)(2,1)}, u32[]{:S(2)}, u32[]{:S(2)}) async-start(bf16[16,128,896]{2,1,0:T(8,128)(2,1)} %broadcast_in_dim.16), calls=%async_computation.1 | async-start | bytes 7340032 | tf_op jit(solution)/shard_map/all_to_all | solution.py:21
  306.7 40.7 %all-to-all-done.1 = bf16[16,128,896]{2,1,0:T(8,128)(2,1)} async-done(((bf16[16,128,896]{2,1,0:T(8,128)(2,1)}), bf16[16,128,896]{2,1,0:T(8,128)(2,1)}, u32[]{:S(2)}, u32[]{:S(2)}) %all-to-all-start.1) | async-done | bytes 3670048 | tf_op jit(solution)/shard_map/all_to_all | solution.py:21
  347.3 6.0 %convolution_convert_fusion.3 = bf16[2048,512]{0,1:T(8,128)(2,1)} fusion(bf16[2048,896]{1,0:T(8,128)(2,1)} %bitcast.7, bf16[896,512]{1,0:T(8,128)(2,1)} %param.17), kind=kOutput, calls=%fused_computation.18 | convolution fusion | flops 1880096768 | bytes 6684672 | tf_op jit(solution)/shard_map/dot_general | solution.py:125
  353.3 3.2 convolution_convert_fusion.4
  356.8 3.2 pad_maximum_fusion.1
  360.0 6.2 %reshape.256 = bf16[8,2,128,528]{2,1,0,3:T(2,128)(2,1)} reshape(bf16[2048,528]{0,1:T(8,128)(2,1)} %pad_maximum_fusion.1) | data formatting | bytes 4325376 | tf_op jit(solution)/shard_map/reshape | solution.py:37
  368.1 6.4 %all_to_all.30 = bf16[8,2,128,528]{2,0,3,1:T(8,128)(2,1)} all-to-all(bf16[8,2,128,528]{2,0,3,1:T(8,128)(2,1)S(1)} %copy.88), channel_id=1, replica_groups=mesh['dp'=16,'tz'=8,'tc'=2] {'tc'}, dimensions={1} | all-to-all | bytes 4325376 | tf_op jit(solution)/shard_map/all_to_all | solution.py:40
  374.4 2.7 broadcast_in_dim.19
  377.1 7.6 %all-to-all-start.5 = ((bf16[16,2,2,16,896]{4,1,3,2,0:T(2,128)(2,1)}), bf16[16,2,2,16,896]{4,1,3,2,0:T(2,128)(2,1)}, u32[]{:S(2)}, u32[]{:S(2)}) async-start(bf16[16,2,2,16,896]{4,1,3,2,0:T(2,128)(2,1)} %broadcast_in_dim.19), calls=%async_computation.5 | async-start | bytes 3670016 | tf_op jit(solution)/shard_map/all_to_all | solution.py:21
  384.8 2.8 reduce_sum.49
  388.7 22.5 %all-to-all-done.5 = bf16[16,2,2,16,896]{4,1,3,2,0:T(2,128)(2,1)} async-done(((bf16[16,2,2,16,896]{4,1,3,2,0:T(2,128)(2,1)}), bf16[16,2,2,16,896]{4,1,3,2,0:T(2,128)(2,1)}, u32[]{:S(2)}, u32[]{:S(2)}) %all-to-all-start.5) | async-done | bytes 1835040 | tf_op jit(solution)/shard_map/all_to_all | solution.py:21
  411.1 6.6 %all-to-all-start.3 = ((bf16[8,128,528]{1,2,0:T(8,128)(2,1)}), bf16[8,128,528]{1,2,0:T(8,128)(2,1)S(1)}, u32[]{:S(2)}, u32[]{:S(2)}) async-start(bf16[8,128,528]{1,2,0:T(8,128)(2,1)} %copy.90), calls=%async_computation.3 | async-start | bytes 2162688 | tf_op jit(solution)/shard_map/all_to_all | solution.py:41
  423.0 4.1 copy.105
  427.1 5.0 reshape.268
  436.4 8.9 %all-to-all-done.3 = bf16[8,128,528]{1,2,0:T(8,128)(2,1)S(1)} async-done(((bf16[8,128,528]{1,2,0:T(8,128)(2,1)}), bf16[8,128,528]{1,2,0:T(8,128)(2,1)S(1)}, u32[]{:S(2)}, u32[]{:S(2)}) %all-to-all-start.3) | async-done | bytes 1081376 | tf_op jit(solution)/shard_map/all_to_all | solution.py:41
  445.5 15.9 %all-gather.4 = f32[2048,48]{0,1:T(8,128)S(1)} all-gather(f32[128,48]{0,1:T(8,128)S(1)} %pad_maximum_fusion.3), channel_id=6, replica_groups=mesh['dp'=16,'tz'=8,'tc'=2] {'tz','tc'}, dimensions={0}, use_global_device_ids=true | all-gather | bytes 417792 | tf_op jit(solution)/shard_map/all_gather | solution.py:189
  461.6 22.2 %all_gather.43 = bf16[2048,48]{0,1:T(8,128)(2,1)S(1)} all-gather(bf16[128,48]{0,1:T(8,128)(2,1)S(1)} %pad_maximum_fusion.4), channel_id=1, replica_groups=mesh['dp'=16,'tz'=8,'tc'=2] {'dp'}, dimensions={0}, use_global_device_ids=true | all-gather | bytes 208896 | tf_op jit(solution)/shard_map/all_gather | solution.py:231
  487.5 3.5 convolution_bitcast_fusion
  (138 shorter events, 55.0 us)
Async XLA Ops:
  7.2 231.8 %copy-start = (bf16[64,896,16]{1,2,0:T(8,128)(2,1)S(1)}, bf16[64,896,16]{1,2,0:T(8,128)(2,1)}, u32[]{:S(2)}) copy-start(bf16[64,896,16]{1,2,0:T(8,128)(2,1)} %param.23) | copy-start | bytes 5505028
  7.2 43.9 %all-gather.10.cloned.1.call-start = ((), (), s32[]{:S(2)}) async-start(), calls=%async_computation.6 | async-start | bytes 1179648 | tf_op jit(solution)/shard_map/all_gather | solution.py:29
  7.9 59.3 %all-gather.12.cloned.1.call-start = ((), (), s32[]{:S(2)}) async-start(), calls=%async_computation.7 | async-start | bytes 3145728 | tf_op jit(solution)/shard_map/all_gather | solution.py:30
  69.5 2.8 copy-start.20
  72.3 3.9 copy-start.2
  72.3 3.9 copy-start.21
  82.2 49.7 %copy-start.11 = (bf16[64,16,512]{2,1,0:T(8,128)(2,1)S(1)}, bf16[64,16,512]{2,1,0:T(8,128)(2,1)}, u32[]{:S(2)}) copy-start(bf16[64,16,512]{2,1,0:T(8,128)(2,1)} %param.20) | copy-start | bytes 3145732
  82.2 136.9 %all-to-all-start = ((bf16[16,128,1824]{1,2,0:T(8,128)(2,1)}), bf16[16,128,1824]{1,2,0:T(8,128)(2,1)}, u32[]{:S(2)}, u32[]{:S(2)}) async-start(bf16[16,128,1824]{1,2,0:T(8,128)(2,1)} %copy_bitcast_fusion), calls=%async_computation | async-start | bytes 14942208 | tf_op jit(solution)/shard_map/all_to_all | solution.py:15
  89.6 42.3 %all-gather.14.cloned.1.call-start = ((), (), s32[]{:S(2)}) async-start(), calls=%async_computation.8 | async-start | bytes 1179648 | tf_op jit(solution)/shard_map/all_gather | solution.py:29
  90.4 57.7 %all-gather.16.cloned.1.call-start = ((), (), s32[]{:S(2)}) async-start(), calls=%async_computation.9 | async-start | bytes 3145728 | tf_op jit(solution)/shard_map/all_gather | solution.py:30
  219.1 4.4 copy-start.4
  226.0 12.3 %copy-start.18 = (s32[32]{0:T(128)S(1)}, s32[32]{0:T(128)}, u32[]{:S(2)}) copy-start(s32[32]{0:T(128)} %param.24) | copy-start | bytes 388
  226.0 60.8 %all-to-all-start.4 = ((bf16[16,128,912]{1,2,0:T(8,128)(2,1)}), bf16[16,128,912]{1,2,0:T(8,128)(2,1)}, u32[]{:S(2)}, u32[]{:S(2)}) async-start(bf16[16,128,912]{1,2,0:T(8,128)(2,1)} %copy_bitcast_fusion.1), calls=%async_computation.4 | async-start | bytes 7471104 | tf_op jit(solution)/shard_map/all_to_all | solution.py:15
  241.6 47.8 %copy-start.9 = (bf16[2,16,896]{2,1,0:T(8,128)(2,1)}, bf16[2,16,896]{2,1,0:T(8,128)(2,1)S(1)}, u32[]{:S(2)}) copy-start(bf16[2,16,896]{2,1,0:T(8,128)(2,1)S(1)} %gather_fusion.2) | copy-start | bytes 172036
  243.7 2.8 copy-start.7
  297.4 49.9 %all-to-all-start.1 = ((bf16[16,128,896]{2,1,0:T(8,128)(2,1)}), bf16[16,128,896]{2,1,0:T(8,128)(2,1)}, u32[]{:S(2)}, u32[]{:S(2)}) async-start(bf16[16,128,896]{2,1,0:T(8,128)(2,1)} %broadcast_in_dim.16), calls=%async_computation.1 | async-start | bytes 7340032 | tf_op jit(solution)/shard_map/all_to_all | solution.py:21
  304.0 0.9 copy-start.6
  377.1 34.0 %all-to-all-start.5 = ((bf16[16,2,2,16,896]{4,1,3,2,0:T(2,128)(2,1)}), bf16[16,2,2,16,896]{4,1,3,2,0:T(2,128)(2,1)}, u32[]{:S(2)}, u32[]{:S(2)}) async-start(bf16[16,2,2,16,896]{4,1,3,2,0:T(2,128)(2,1)} %broadcast_in_dim.19), calls=%async_computation.5 | async-start | bytes 3670016 | tf_op jit(solution)/shard_map/all_to_all | solution.py:21
  384.7 33.0 %copy-start.1 = (s32[64]{0:T(128)S(1)}, s32[64]{0:T(128)}, u32[]{:S(2)}) copy-start(s32[64]{0:T(128)} %param.25) | copy-start | bytes 772
  384.7 35.2 %copy-start.19 = (s32[2]{0:T(128)S(1)}, s32[2]{0:T(128)}, u32[]{:S(2)}) copy-start(s32[2]{0:T(128)} %get-tuple-element.54) | copy-start | bytes 28
  384.7 37.7 %copy-start.10 = (bf16[2,16,896]{2,1,0:T(8,128)(2,1)S(1)}, bf16[2,16,896]{2,1,0:T(8,128)(2,1)}, u32[]{:S(2)}) copy-start(bf16[2,16,896]{2,1,0:T(8,128)(2,1)} %copy-done.9) | copy-start | bytes 172036
  384.7 38.0 %copy-start.8 = (bf16[2,16,896]{2,1,0:T(8,128)(2,1)S(1)}, bf16[2,16,896]{2,1,0:T(8,128)(2,1)}, u32[]{:S(2)}) copy-start(bf16[2,16,896]{2,1,0:T(8,128)(2,1)} %copy-done.7) | copy-start | bytes 172036
  411.1 34.2 %all-to-all-start.3 = ((bf16[8,128,528]{1,2,0:T(8,128)(2,1)}), bf16[8,128,528]{1,2,0:T(8,128)(2,1)S(1)}, u32[]{:S(2)}, u32[]{:S(2)}) async-start(bf16[8,128,528]{1,2,0:T(8,128)(2,1)} %copy.90), calls=%async_computation.3 | async-start | bytes 2162688 | tf_op jit(solution)/shard_map/all_to_all | solution.py:41
  417.7 0.7 copy-start.16
  418.4 0.5 copy-start.14
  423.0 9.0 %copy-start.15 = (s32[32]{0:T(128)S(1)}, s32[32]{0:T(128)}, u32[]{:S(2)}) copy-start(s32[32]{0:T(128)} %copy-done.14) | copy-start | bytes 388
  423.0 9.0 %copy-start.17 = (s32[4]{0:T(128)S(1)}, s32[4]{0:T(128)}, u32[]{:S(2)}) copy-start(s32[4]{0:T(128)} %copy-done.16) | copy-start | bytes 52
  445.4 38.5 %copy-start.3 = (bf16[8,256,512]{2,1,0:T(8,128)(2,1)S(1)}, bf16[8,256,512]{2,1,0:T(8,128)(2,1)}, u32[]{:S(2)}) copy-start(bf16[8,256,512]{2,1,0:T(8,128)(2,1)} %all-gather.12.cloned.1.call-done) | copy-start | bytes 6291460
  461.5 24.8 %copy-start.12 = (bf16[2,16,512]{2,1,0:T(8,128)(2,1)S(1)}, bf16[2,16,512]{2,1,0:T(8,128)(2,1)}, u32[]{:S(2)}) copy-start(bf16[2,16,512]{2,1,0:T(8,128)(2,1)} %gather_fusion.5) | copy-start | bytes 98308
  483.9 3.6 copy-start.13
  487.5 3.5 copy-start.5
Sparse Core Ops, SparseCore 0:
  9.8 41.2 all-gather.9
  52.9 14.2 all-gather.11
  92.2 39.6 all-gather.13
  133.6 14.4 all-gather.15

commit v4 on v2

--- a/solution.py
+++ b/solution.py
@@ -102,31 +102,6 @@
     hidden = (jax.nn.silu(gate_complete) * up_complete).astype(jnp.bfloat16)
     all_hidden = gather_rows(hidden, "dp")
 
-    out_part = jnp.dot(all_hidden, down_weight, preferred_element_type=jnp.float32)
-    down_rank_part = jnp.einsum(
-        "btf,bfr->btr",
-        all_hidden.reshape(blocks_all, BLOCK, width_here),
-        down_in[tenants],
-        preferred_element_type=jnp.float32,
-    ).reshape(every_token_row, rank_width)
-    down_sums = scatter_sum(
-        jnp.concatenate(
-            [out_part.astype(jnp.bfloat16), down_rank_part.astype(jnp.bfloat16)], axis=1
-        ),
-        "tensor",
-    )
-    out_sum = down_sums[:, :feat_here]
-    down_rank_flat = down_sums[:, feat_here:].astype(jnp.bfloat16)
-    down_rank_second = down_rank_flat.reshape(blocks_in, BLOCK, rank_width)
-    down_raise = down_out[input_tenants]
-    mixed = (
-        out_sum
-        + adapter_scale
-        * jnp.einsum(
-            "vmn,vnx->vmx", down_rank_second, down_raise, preferred_element_type=jnp.float32
-        ).reshape(rows_in, feat_here)
-    ).astype(jnp.bfloat16)
-
     hidden_grad_part = lax.dot_general(
         all_cot, down_weight, (((1,), (1,)), ((), ())), preferred_element_type=jnp.float32
     )
@@ -167,23 +142,47 @@
     up_backward_piece = adapter_scale * jnp.einsum(
         "yae,yve->yav", up_gradient, up_raise, preferred_element_type=jnp.float32
     )
-    rank_partials = lax.all_gather(
-        jnp.concatenate(
-            [
-                gate_backward_piece.reshape(group_rows, rank_width),
-                up_backward_piece.reshape(group_rows, rank_width),
-                down_rank_flat.astype(jnp.float32),
-            ],
-            axis=1,
-        ),
-        "tensor",
-        axis=0,
-        tiled=False,
-    )
-    back_rank_sums = rank_partials[:, :, : 2 * rank_width].sum(0)
-    gate_backward = back_rank_sums[:, :rank_width]
-    up_backward = back_rank_sums[:, rank_width:]
-    all_down_rank = rank_partials[:, :, 2 * rank_width :].reshape(every_token_row, rank_width)
+
+    out_part = jnp.dot(all_hidden, down_weight, preferred_element_type=jnp.float32)
+    down_rank_part = jnp.einsum(
+        "btf,bfr->btr",
+        all_hidden.reshape(blocks_all, BLOCK, width_here),
+        down_in[tenants],
+        preferred_element_type=jnp.float32,
+    ).reshape(every_token_row, rank_width)
+    rank_back_pieces = jnp.concatenate(
+        [
+            gate_backward_piece.reshape(group_rows, rank_width),
+            up_backward_piece.reshape(group_rows, rank_width),
+        ],
+        axis=1,
+    ).astype(jnp.bfloat16)
+    down_pieces = jnp.concatenate(
+        [out_part.astype(jnp.bfloat16), down_rank_part.astype(jnp.bfloat16)], axis=1
+    ).reshape(tensor_count, rows_in, feat_here + rank_width)
+    down_pieces = jnp.concatenate(
+        [
+            down_pieces,
+            jnp.broadcast_to(rank_back_pieces[None], (tensor_count, group_rows, 2 * rank_width)),
+        ],
+        axis=2,
+    )
+    down_sums = scatter_sum(down_pieces.reshape(tensor_count * rows_in, -1), "tensor")
+    out_sum = down_sums[:, :feat_here]
+    down_rank_flat = down_sums[:, feat_here : feat_here + rank_width].astype(jnp.bfloat16)
+    gate_backward = down_sums[:, feat_here + rank_width : feat_here + 2 * rank_width]
+    up_backward = down_sums[:, feat_here + 2 * rank_width :]
+    down_rank_second = down_rank_flat.reshape(blocks_in, BLOCK, rank_width)
+    down_raise = down_out[input_tenants]
+    mixed = (
+        out_sum
+        + adapter_scale
+        * jnp.einsum(
+            "vmn,vnx->vmx", down_rank_second, down_raise, preferred_element_type=jnp.float32
+        ).reshape(rows_in, feat_here)
+    ).astype(jnp.bfloat16)
+
+    all_down_rank = lax.all_gather(down_rank_flat, "tensor", axis=0, tiled=True)
     rank_weighted = (token_onehot[:, :, None] * all_down_rank[:, None, :]).reshape(
         every_token_row, tenants_here * rank_width
     )
@@ -198,10 +197,22 @@
     up_raise_block_list = adapter_scale * jnp.einsum(
         "yap,yau->ypu", up_rank_second, up_gradient, preferred_element_type=jnp.float32
     )
-    all_raise_blocks = gather_rows(
-        jnp.stack([gate_raise_block_list, up_raise_block_list], axis=1).astype(jnp.bfloat16),
-        "dp",
-    ).astype(jnp.float32)
+    raise_stack = jnp.stack([gate_raise_block_list, up_raise_block_list], axis=1).astype(
+        jnp.bfloat16
+    )
+    backs = jnp.concatenate(
+        [gate_backward.astype(jnp.bfloat16), up_backward.astype(jnp.bfloat16), group_down_back],
+        axis=1,
+    )
+    all_joined = gather_rows(
+        jnp.concatenate([raise_stack.reshape(-1), backs.reshape(-1)])[None], "dp"
+    )
+    all_raise_blocks = (
+        all_joined[:, : raise_stack.size]
+        .reshape((dp_count * blocks_group,) + raise_stack.shape[1:])
+        .astype(jnp.float32)
+    )
+    all_backs = all_joined[:, raise_stack.size :].reshape(every_token_row, 3 * rank_width)
     own_slots = dp_index * slots_here + jnp.arange(slots_here, dtype=jnp.int32)
     block_onehot = (own_slots[:, None] == owners[tenants][None, :]).astype(jnp.float32)
     grad_gate_out = jnp.einsum(
@@ -209,19 +220,6 @@
     )
     grad_up_out = jnp.einsum("sb,brf->srf", block_onehot, all_raise_blocks[:, 1], precision=highest)
 
-    all_backs = lax.all_gather(
-        jnp.concatenate(
-            [
-                gate_backward.astype(jnp.bfloat16),
-                up_backward.astype(jnp.bfloat16),
-                group_down_back,
-            ],
-            axis=1,
-        ),
-        "dp",
-        axis=0,
-        tiled=True,
-    )
     all_gate_back = all_backs[:, :rank_width]
     all_up_back = all_backs[:, rank_width : 2 * rank_width]
     all_down_back = all_backs[:, 2 * rank_width :]

time: 478 us -> 499 us (1.044)
  blocking collectives: 38.8 us -> 15.8 us
  other arithmetic: 20.4 us -> 36.6 us
  local copies, waits for them, and re-layouts: 38.4 us -> 54 us
  waiting for transfers between devices: 284 us -> 295 us
    all_gather x2 -> x1, blocking collectives: 38.8 us -> 15.8 us  [shards(): all_down_rank = lax.all_gather(down_rank_flat, 'tensor', axis=0, tiled=True)]
    all_to_all x3, waiting for transfers between devices: 150 us -> 169 us  [scatter_sum(): got = lax.all_to_all(pieces, axis, 0, 0, tiled=False)]
    unnamed x35 -> x36, local copies, waits for them, and re-layouts: 2.38 us -> 19.9 us
    broadcast_in_dim x0 -> x1, other arithmetic: none -> 14.3 us  [gather_rows(): jnp.broadcast_to(x[None], (count,) + x.shape)]
    all_to_all x2, waiting for transfers between devices: 53.9 us -> 46.3 us  [gather_rows(): lax.all_to_all(jnp.broadcast_to(x[None], (count,) + x.shape), axis, 0, 0,...]
  transfers between devices with their start and end apart: 7 -> 7, of which waited for: 7 -> 7; matrix products, arithmetic and copies ran while one was open for 10% -> 6% of each run, Pallas kernels for 0% -> 0%
where the time goes in v4:
time: 499 us; the launch traced here: 497 us
  waiting for transfers between devices  295 us (59%)
  local copies, waits for them, and re-layouts  54 us (11%)
  starting transfers between devices  43.7 us (9%)
  matrix products  37.4 us (7%)
  other arithmetic  36.6 us (7%)
  blocking collectives  15.8 us (3%)
  between operations  14.6 us (3%)
    all_to_all x3, waiting for transfers between devices, scatter_sum(): got = lax.all_to_all(pieces, axis, 0, 0, tiled=False)  169 us
    all_to_all x2, waiting for transfers between devices, gather_rows(): lax.all_to_all(jnp.broadcast_to(x[None], (count,) + x.shape), axis, 0, 0,...  46.3 us
    all_gather x1, waiting for transfers between devices, shards(): all_inputs = lax.all_gather(tokens, 'tensor', axis=0, tiled=True)  40 us
    all_gather x1, waiting for transfers between devices, shards(): all_cot = lax.all_gather(cotangent, 'tensor', axis=0, tiled=True)  39.1 us
    all_to_all x3, starting transfers between devices, scatter_sum(): got = lax.all_to_all(pieces, axis, 0, 0, tiled=False)  29.3 us
    unnamed x36, local copies, waits for them, and re-layouts  19.9 us
    all_gather x1, blocking collectives, shards(): all_down_rank = lax.all_gather(down_rank_flat, 'tensor', axis=0, tiled=True)  15.8 us
    all_to_all x2, starting transfers between devices, gather_rows(): lax.all_to_all(jnp.broadcast_to(x[None], (count,) + x.shape), axis, 0, 0,...  14.3 us
  transfers between devices with their start and end apart: 7, of which 7 were waited for; matrix products, arithmetic and copies ran while one was open for 6% of the time, Pallas kernels for 0%

profile of v4, /device:TPU:8, one launch (start us, length us, event | category | flops | bytes accessed | tf_op | source)
XLA Modules:
  0.0 497.4 jit_solution(16767779722942689592)
XLA Ops:
  12.2 40.0 %all-gather.3.cloned.1.call-done = bf16[2048,512]{1,0:T(8,128)(2,1)} async-done(((bf16[128,512]{1,0:T(8,128)(2,1)}), bf16[2048,512]{1,0:T(8,128)(2,1)}) %all-gather.3.cloned.1.call-update) | async-done | bytes 2097168 | tf_op jit(solution)/shard_map/all_gather | solution.py:63
  54.7 2.3 fusion.3
  57.2 3.9 convolution_convert_fusion.1
  63.3 3.9 copy_bitcast_fusion
  67.2 7.4 %all-to-all-start = ((bf16[16,128,1824]{1,2,0:T(8,128)(2,1)}), bf16[16,128,1824]{1,2,0:T(8,128)(2,1)}, u32[]{:S(2)}, u32[]{:S(2)}) async-start(bf16[16,128,1824]{1,2,0:T(8,128)(2,1)} %copy_bitcast_fusion), calls=%async_computation | async-start | bytes 14942208 | tf_op jit(solution)/shard_map/all_to_all | solution.py:15
  75.9 39.1 %all-gather.5.cloned.1.call-done = bf16[2048,512]{1,0:T(8,128)(2,1)} async-done(((bf16[128,512]{1,0:T(8,128)(2,1)}), bf16[2048,512]{1,0:T(8,128)(2,1)}) %all-gather.5.cloned.1.call-update) | async-done | bytes 2097168 | tf_op jit(solution)/shard_map/all_gather | solution.py:65
  117.5 3.9 convolution_convert_fusion
  121.4 2.3 pad_maximum_fusion
  123.7 75.0 %all-to-all-done = bf16[16,128,1824]{1,2,0:T(8,128)(2,1)} async-done(((bf16[16,128,1824]{1,2,0:T(8,128)(2,1)}), bf16[16,128,1824]{1,2,0:T(8,128)(2,1)}, u32[]{:S(2)}, u32[]{:S(2)}) %all-to-all-start) | async-done | bytes 7471136 | tf_op jit(solution)/shard_map/all_to_all | solution.py:15
  198.8 4.4 convert_reduce_fusion
  203.2 2.5 copy_bitcast_fusion.1
  205.7 17.3 %all-to-all-start.2 = ((bf16[16,128,912]{1,2,0:T(8,128)(2,1)}), bf16[16,128,912]{1,2,0:T(8,128)(2,1)}, u32[]{:S(2)}, u32[]{:S(2)}) async-start(bf16[16,128,912]{1,2,0:T(8,128)(2,1)} %copy_bitcast_fusion.1), calls=%async_computation.2 | async-start | bytes 7471104 | tf_op jit(solution)/shard_map/all_to_all | solution.py:15
  230.5 40.8 %all-to-all-done.2 = bf16[16,128,912]{1,2,0:T(8,128)(2,1)} async-done(((bf16[16,128,912]{1,2,0:T(8,128)(2,1)}), bf16[16,128,912]{1,2,0:T(8,128)(2,1)}, u32[]{:S(2)}, u32[]{:S(2)}) %all-to-all-start.2) | async-done | bytes 3735584 | tf_op jit(solution)/shard_map/all_to_all | solution.py:15
  271.4 2.6 convert_reduce_fusion.1
  277.1 2.4 multiply_convert_fusion.1
  280.6 2.3 broadcast_in_dim.18
  282.9 6.4 %all-to-all-start.1 = ((bf16[16,128,896]{2,1,0:T(8,128)(2,1)}), bf16[16,128,896]{2,1,0:T(8,128)(2,1)}, u32[]{:S(2)}, u32[]{:S(2)}) async-start(bf16[16,128,896]{2,1,0:T(8,128)(2,1)} %broadcast_in_dim.18), calls=%async_computation.1 | async-start | bytes 7340032 | tf_op jit(solution)/shard_map/all_to_all | solution.py:21
  291.1 40.5 %all-to-all-done.1 = bf16[16,128,896]{2,1,0:T(8,128)(2,1)} async-done(((bf16[16,128,896]{2,1,0:T(8,128)(2,1)}), bf16[16,128,896]{2,1,0:T(8,128)(2,1)}, u32[]{:S(2)}, u32[]{:S(2)}) %all-to-all-start.1) | async-done | bytes 3670048 | tf_op jit(solution)/shard_map/all_to_all | solution.py:21
  331.6 6.0 %convolution_convert_fusion.3 = bf16[2048,512]{0,1:T(8,128)(2,1)} fusion(bf16[2048,896]{1,0:T(8,128)(2,1)} %bitcast.5, bf16[896,512]{1,0:T(8,128)(2,1)} %param.17), kind=kOutput, calls=%fused_computation.19 | convolution fusion | flops 1880096768 | bytes 6684672 | tf_op jit(solution)/shard_map/dot_general | solution.py:146
  337.6 3.2 convolution_convert_fusion.4
  344.7 4.7 all-to-all-start.3
  349.9 52.7 %all-to-all-done.3 = bf16[16,128,560]{1,2,0:T(8,128)(2,1)} async-done(((bf16[16,128,560]{1,2,0:T(8,128)(2,1)}), bf16[16,128,560]{1,2,0:T(8,128)(2,1)}, u32[]{:S(2)}, u32[]{:S(2)}) %all-to-all-start.3) | async-done | bytes 2293792 | tf_op jit(solution)/shard_map/all_to_all | solution.py:15
  404.9 4.0 broadcast_in_dim.22
  409.4 14.3 %reduce = bf16[16,63488]{1,0:T(8,128)(2,1)} reduce(bf16[16,1,63488]{2,1,0:T(2,128)(2,1)} %broadcast_in_dim.22, bf16[]{:T(256)} %broadcast.136), dimensions={1}, to_apply=%broadcast_in_dim.22.reduce_sub_computation | reduce | bytes 4063234 | tf_op jit(solution)/shard_map/broadcast_in_dim | solution.py:21
  423.7 3.9 reshape.316
  427.6 8.0 %all-to-all-start.4 = ((bf16[16,2,31744]{2,1,0:T(2,128)(2,1)}), bf16[16,2,31744]{2,1,0:T(2,128)(2,1)}, u32[]{:S(2)}, u32[]{:S(2)}) async-start(bf16[16,2,31744]{2,1,0:T(2,128)(2,1)} %reshape.316), calls=%async_computation.4 | async-start | bytes 4063232 | tf_op jit(solution)/shard_map/all_to_all | solution.py:21
  439.8 15.8 %all_gather.11 = bf16[2048,16]{0,1:T(8,128)(2,1)S(1)} all-gather(bf16[128,16]{0,1:T(8,128)(2,1)S(1)} %slice.100), channel_id=1, replica_groups=mesh['dp'=16,'tensor'=16] {'tensor'}, dimensions={0}, use_global_device_ids=true | all-gather | bytes 69632 | tf_op jit(solution)/shard_map/all_gather | solution.py:185
  455.6 2.7 fusion.5
  458.3 5.8 %all-to-all-done.4 = bf16[16,2,31744]{2,1,0:T(2,128)(2,1)} async-done(((bf16[16,2,31744]{2,1,0:T(2,128)(2,1)}), bf16[16,2,31744]{2,1,0:T(2,128)(2,1)}, u32[]{:S(2)}, u32[]{:S(2)}) %all-to-all-start.4) | async-done | bytes 2031648 | tf_op jit(solution)/shard_map/all_to_all | solution.py:21
  464.1 10.2 %reshape.317 = bf16[16,1,63488]{2,1,0:T(2,128)(2,1)} reshape(bf16[16,2,31744]{2,1,0:T(2,128)(2,1)} %all-to-all-done.4) | data formatting | bytes 4063232
  474.3 3.3 copy.153
  484.8 3.5 convolution_bitcast_fusion
  (127 shorter events, 47.8 us)
Async XLA Ops:
  7.2 215.8 %copy-start = (bf16[64,896,16]{1,2,0:T(8,128)(2,1)S(1)}, bf16[64,896,16]{1,2,0:T(8,128)(2,1)}, u32[]{:S(2)}) copy-start(bf16[64,896,16]{1,2,0:T(8,128)(2,1)} %param.23) | copy-start | bytes 5505028
  7.2 45.0 %all-gather.3.cloned.1.call-start = ((), (), s32[]{:S(2)}) async-start(), calls=%async_computation.5 | async-start | bytes 2228224 | tf_op jit(solution)/shard_map/all_gather | solution.py:63
  54.4 2.8 copy-start.13
  57.2 3.9 copy-start.3
  57.2 3.9 copy-start.14
  67.2 8.1 %copy-start.11 = (bf16[64,16,512]{2,1,0:T(8,128)(2,1)S(1)}, bf16[64,16,512]{2,1,0:T(8,128)(2,1)}, u32[]{:S(2)}) copy-start(bf16[64,16,512]{2,1,0:T(8,128)(2,1)} %param.20) | copy-start | bytes 3145732
  67.2 131.6 %all-to-all-start = ((bf16[16,128,1824]{1,2,0:T(8,128)(2,1)}), bf16[16,128,1824]{1,2,0:T(8,128)(2,1)}, u32[]{:S(2)}, u32[]{:S(2)}) async-start(bf16[16,128,1824]{1,2,0:T(8,128)(2,1)} %copy_bitcast_fusion), calls=%async_computation | async-start | bytes 14942208 | tf_op jit(solution)/shard_map/all_to_all | solution.py:15
  74.6 40.5 %all-gather.5.cloned.1.call-start = ((), (), s32[]{:S(2)}) async-start(), calls=%async_computation.6 | async-start | bytes 2228224 | tf_op jit(solution)/shard_map/all_gather | solution.py:65
  198.8 4.4 copy-start.5
  205.7 17.3 %copy-start.12 = (s32[32]{0:T(128)S(1)}, s32[32]{0:T(128)}, u32[]{:S(2)}) copy-start(s32[32]{0:T(128)} %param.24) | copy-start | bytes 388
  205.7 65.7 %all-to-all-start.2 = ((bf16[16,128,912]{1,2,0:T(8,128)(2,1)}), bf16[16,128,912]{1,2,0:T(8,128)(2,1)}, u32[]{:S(2)}, u32[]{:S(2)}) async-start(bf16[16,128,912]{1,2,0:T(8,128)(2,1)} %copy_bitcast_fusion.1), calls=%async_computation.2 | async-start | bytes 7471104 | tf_op jit(solution)/shard_map/all_to_all | solution.py:15
  225.7 48.3 %copy-start.9 = (bf16[2,16,896]{2,1,0:T(8,128)(2,1)}, bf16[2,16,896]{2,1,0:T(8,128)(2,1)S(1)}, u32[]{:S(2)}) copy-start(bf16[2,16,896]{2,1,0:T(8,128)(2,1)S(1)} %gather_fusion.2) | copy-start | bytes 172036
  227.8 2.8 copy-start.7
  282.9 48.7 %all-to-all-start.1 = ((bf16[16,128,896]{2,1,0:T(8,128)(2,1)}), bf16[16,128,896]{2,1,0:T(8,128)(2,1)}, u32[]{:S(2)}, u32[]{:S(2)}) async-start(bf16[16,128,896]{2,1,0:T(8,128)(2,1)} %broadcast_in_dim.18), calls=%async_computation.1 | async-start | bytes 7340032 | tf_op jit(solution)/shard_map/all_to_all | solution.py:21
  289.3 0.9 copy-start.6
  289.3 1.3 copy-start.10
  289.3 1.6 copy-start.8
  344.7 57.9 %all-to-all-start.3 = ((bf16[16,128,560]{1,2,0:T(8,128)(2,1)}), bf16[16,128,560]{1,2,0:T(8,128)(2,1)}, u32[]{:S(2)}, u32[]{:S(2)}) async-start(bf16[16,128,560]{1,2,0:T(8,128)(2,1)} %pad_maximum_fusion.1), calls=%async_computation.3 | async-start | bytes 4587520 | tf_op jit(solution)/shard_map/all_to_all | solution.py:15
  423.7 11.8 %copy-start.2 = (s32[64]{0:T(128)S(1)}, s32[64]{0:T(128)}, u32[]{:S(2)}) copy-start(s32[64]{0:T(128)} %param.25) | copy-start | bytes 772
  427.6 36.5 %all-to-all-start.4 = ((bf16[16,2,31744]{2,1,0:T(2,128)(2,1)}), bf16[16,2,31744]{2,1,0:T(2,128)(2,1)}, u32[]{:S(2)}, u32[]{:S(2)}) async-start(bf16[16,2,31744]{2,1,0:T(2,128)(2,1)} %reshape.316), calls=%async_computation.4 | async-start | bytes 4063232 | tf_op jit(solution)/shard_map/all_to_all | solution.py:21
  484.8 3.5 copy-start.4
  484.8 5.8 %copy-start.1 = (bf16[64,896,16]{1,2,0:T(8,128)(2,1)S(1)}, bf16[64,896,16]{1,2,0:T(8,128)(2,1)}, u32[]{:S(2)}) copy-start(bf16[64,896,16]{1,2,0:T(8,128)(2,1)} %param.23) | copy-start | bytes 5505028
Sparse Core Ops, SparseCore 0:
  9.8 42.3 all-gather.2
  77.2 37.7 all-gather.4

commit v5 on v4

--- a/solution.py
+++ b/solution.py
@@ -204,15 +204,22 @@
         [gate_backward.astype(jnp.bfloat16), up_backward.astype(jnp.bfloat16), group_down_back],
         axis=1,
     )
+    raise_rows = raise_stack.reshape(-1, width_here)
+    back_rows = -(-backs.size // (8 * width_here)) * 8
+    backs_padded = jnp.pad(backs.reshape(-1), (0, back_rows * width_here - backs.size))
     all_joined = gather_rows(
-        jnp.concatenate([raise_stack.reshape(-1), backs.reshape(-1)])[None], "dp"
-    )
+        jnp.concatenate([raise_rows, backs_padded.reshape(back_rows, width_here)], axis=0), "dp"
+    ).reshape(dp_count, -1, width_here)
     all_raise_blocks = (
-        all_joined[:, : raise_stack.size]
+        all_joined[:, : raise_rows.shape[0]]
         .reshape((dp_count * blocks_group,) + raise_stack.shape[1:])
         .astype(jnp.float32)
     )
-    all_backs = all_joined[:, raise_stack.size :].reshape(every_token_row, 3 * rank_width)
+    all_backs = (
+        all_joined[:, raise_rows.shape[0] :]
+        .reshape(dp_count, -1)[:, : backs.size]
+        .reshape(every_token_row, 3 * rank_width)
+    )
     own_slots = dp_index * slots_here + jnp.arange(slots_here, dtype=jnp.int32)
     block_onehot = (own_slots[:, None] == owners[tenants][None, :]).astype(jnp.float32)
     grad_gate_out = jnp.einsum(

time: 499 us -> 465 us (0.932)
  local copies, waits for them, and re-layouts: 54 us -> 34.6 us
  other arithmetic: 36.6 us -> 22.3 us
    unnamed x36 -> x30, local copies, waits for them, and re-layouts: 19.9 us -> 2.5 us
    broadcast_in_dim x1 -> x0, other arithmetic: 14.3 us -> none  [gather_rows(): jnp.broadcast_to(x[None], (count,) + x.shape)]
  transfers between devices with their start and end apart: 7 -> 7, of which waited for: 7 -> 7; matrix products, arithmetic and copies ran while one was open for 6% -> 7% of each run, Pallas kernels for 0% -> 0%
where the time goes in v5:
time: 465 us; the launch traced here: 464 us
  waiting for transfers between devices  295 us (63%)
  starting transfers between devices  43.1 us (9%)
  matrix products  38.3 us (8%)
  local copies, waits for them, and re-layouts  34.6 us (7%)
  other arithmetic  22.3 us (5%)
  blocking collectives  15.9 us (3%)
  between operations  14.6 us (3%)
    all_to_all x3, waiting for transfers between devices, scatter_sum(): got = lax.all_to_all(pieces, axis, 0, 0, tiled=False)  169 us
    all_to_all x2, waiting for transfers between devices, gather_rows(): lax.all_to_all(jnp.broadcast_to(x[None], (count,) + x.shape), axis, 0, 0,...  45.7 us
    all_gather x1, waiting for transfers between devices, shards(): all_inputs = lax.all_gather(tokens, 'tensor', axis=0, tiled=True)  40 us
    all_gather x1, waiting for transfers between devices, shards(): all_cot = lax.all_gather(cotangent, 'tensor', axis=0, tiled=True)  39.1 us
    all_to_all x3, starting transfers between devices, scatter_sum(): got = lax.all_to_all(pieces, axis, 0, 0, tiled=False)  28.8 us
    all_gather x1, blocking collectives, shards(): all_down_rank = lax.all_gather(down_rank_flat, 'tensor', axis=0, tiled=True)  15.9 us
    all_to_all x2, starting transfers between devices, gather_rows(): lax.all_to_all(jnp.broadcast_to(x[None], (count,) + x.shape), axis, 0, 0,...  14.3 us
  transfers between devices with their start and end apart: 7, of which 7 were waited for; matrix products, arithmetic and copies ran while one was open for 7% of the time, Pallas kernels for 0%

profile of v5, /device:TPU:8, one launch (start us, length us, event | category | flops | bytes accessed | tf_op | source)
XLA Modules:
  0.0 464.0 jit_solution(6410173804098847509)
XLA Ops:
  12.2 40.0 %all-gather.3.cloned.1.call-done = bf16[2048,512]{1,0:T(8,128)(2,1)} async-done(((bf16[128,512]{1,0:T(8,128)(2,1)}), bf16[2048,512]{1,0:T(8,128)(2,1)}) %all-gather.3.cloned.1.call-update) | async-done | bytes 2097168 | tf_op jit(solution)/shard_map/all_gather | solution.py:63
  52.2 2.2 fusion.3
  54.7 2.3 fusion.4
  57.2 3.9 convolution_convert_fusion.1
  61.1 2.2 convolution_convert_fusion.2
  63.3 3.9 copy_bitcast_fusion
  67.2 7.4 %all-to-all-start = ((bf16[16,128,1824]{1,2,0:T(8,128)(2,1)}), bf16[16,128,1824]{1,2,0:T(8,128)(2,1)}, u32[]{:S(2)}, u32[]{:S(2)}) async-start(bf16[16,128,1824]{1,2,0:T(8,128)(2,1)} %copy_bitcast_fusion), calls=%async_computation | async-start | bytes 14942208 | tf_op jit(solution)/shard_map/all_to_all | solution.py:15
  75.9 39.1 %all-gather.5.cloned.1.call-done = bf16[2048,512]{1,0:T(8,128)(2,1)} async-done(((bf16[128,512]{1,0:T(8,128)(2,1)}), bf16[2048,512]{1,0:T(8,128)(2,1)}) %all-gather.5.cloned.1.call-update) | async-done | bytes 2097168 | tf_op jit(solution)/shard_map/all_gather | solution.py:65
  115.0 2.2 fusion.2
  117.5 3.9 convolution_convert_fusion
  121.4 2.3 pad_maximum_fusion
  123.8 75.1 %all-to-all-done = bf16[16,128,1824]{1,2,0:T(8,128)(2,1)} async-done(((bf16[16,128,1824]{1,2,0:T(8,128)(2,1)}), bf16[16,128,1824]{1,2,0:T(8,128)(2,1)}, u32[]{:S(2)}, u32[]{:S(2)}) %all-to-all-start) | async-done | bytes 7471136 | tf_op jit(solution)/shard_map/all_to_all | solution.py:15
  198.9 4.4 convert_reduce_fusion
  203.3 2.5 copy_bitcast_fusion.1
  205.8 16.8 %all-to-all-start.2 = ((bf16[16,128,912]{1,2,0:T(8,128)(2,1)}), bf16[16,128,912]{1,2,0:T(8,128)(2,1)}, u32[]{:S(2)}, u32[]{:S(2)}) async-start(bf16[16,128,912]{1,2,0:T(8,128)(2,1)} %copy_bitcast_fusion.1), calls=%async_computation.2 | async-start | bytes 7471104 | tf_op jit(solution)/shard_map/all_to_all | solution.py:15
  223.2 2.1 gather_fusion.2
  225.3 2.1 gather_fusion.3
  230.2 40.8 %all-to-all-done.2 = bf16[16,128,912]{1,2,0:T(8,128)(2,1)} async-done(((bf16[16,128,912]{1,2,0:T(8,128)(2,1)}), bf16[16,128,912]{1,2,0:T(8,128)(2,1)}, u32[]{:S(2)}, u32[]{:S(2)}) %all-to-all-start.2) | async-done | bytes 3735584 | tf_op jit(solution)/shard_map/all_to_all | solution.py:15
  271.0 2.6 convert_reduce_fusion.1
  276.8 2.4 multiply_convert_fusion.1
  280.3 2.3 broadcast_in_dim.18
  282.6 6.4 %all-to-all-start.1 = ((bf16[16,128,896]{2,1,0:T(8,128)(2,1)}), bf16[16,128,896]{2,1,0:T(8,128)(2,1)}, u32[]{:S(2)}, u32[]{:S(2)}) async-start(bf16[16,128,896]{2,1,0:T(8,128)(2,1)} %broadcast_in_dim.18), calls=%async_computation.1 | async-start | bytes 7340032 | tf_op jit(solution)/shard_map/all_to_all | solution.py:21
  291.6 39.7 %all-to-all-done.1 = bf16[16,128,896]{2,1,0:T(8,128)(2,1)} async-done(((bf16[16,128,896]{2,1,0:T(8,128)(2,1)}), bf16[16,128,896]{2,1,0:T(8,128)(2,1)}, u32[]{:S(2)}, u32[]{:S(2)}) %all-to-all-start.1) | async-done | bytes 3670048 | tf_op jit(solution)/shard_map/all_to_all | solution.py:21
  331.3 6.0 %convolution_convert_fusion.3 = bf16[2048,512]{0,1:T(8,128)(2,1)} fusion(bf16[2048,896]{1,0:T(8,128)(2,1)} %bitcast.5, bf16[896,512]{1,0:T(8,128)(2,1)} %param.17), kind=kOutput, calls=%fused_computation.19 | convolution fusion | flops 1880096768 | bytes 6684672 | tf_op jit(solution)/shard_map/dot_general | solution.py:146
  337.4 3.2 convolution_convert_fusion.4
  344.4 4.6 all-to-all-start.3
  349.3 53.2 %all-to-all-done.3 = bf16[16,128,560]{1,2,0:T(8,128)(2,1)} async-done(((bf16[16,128,560]{1,2,0:T(8,128)(2,1)}), bf16[16,128,560]{1,2,0:T(8,128)(2,1)}, u32[]{:S(2)}, u32[]{:S(2)}) %all-to-all-start.3) | async-done | bytes 2293792 | tf_op jit(solution)/shard_map/all_to_all | solution.py:15
  406.4 8.0 %all-to-all-start.4 = ((bf16[16,72,896]{2,1,0:T(8,128)(2,1)}), bf16[16,72,896]{2,1,0:T(8,128)(2,1)}, u32[]{:S(2)}, u32[]{:S(2)}) async-start(bf16[16,72,896]{2,1,0:T(8,128)(2,1)} %broadcast_in_dim.22), calls=%async_computation.4 | async-start | bytes 4128768 | tf_op jit(solution)/shard_map/all_to_all | solution.py:21
  418.6 15.9 %all_gather.11 = bf16[2048,16]{0,1:T(8,128)(2,1)S(1)} all-gather(bf16[128,16]{0,1:T(8,128)(2,1)S(1)} %slice.104), channel_id=1, replica_groups=mesh['dp'=16,'tensor'=16] {'tensor'}, dimensions={0}, use_global_device_ids=true | all-gather | bytes 69632 | tf_op jit(solution)/shard_map/all_gather | solution.py:185
  434.5 2.7 fusion.5
  437.2 5.9 %all-to-all-done.4 = bf16[16,72,896]{2,1,0:T(8,128)(2,1)} async-done(((bf16[16,72,896]{2,1,0:T(8,128)(2,1)}), bf16[16,72,896]{2,1,0:T(8,128)(2,1)}, u32[]{:S(2)}, u32[]{:S(2)}) %all-to-all-start.4) | async-done | bytes 2064416 | tf_op jit(solution)/shard_map/all_to_all | solution.py:21
  451.4 3.5 convolution_bitcast_fusion
  (120 shorter events, 39.8 us)
Async XLA Ops:
  7.2 215.5 %copy-start = (bf16[64,896,16]{1,2,0:T(8,128)(2,1)S(1)}, bf16[64,896,16]{1,2,0:T(8,128)(2,1)}, u32[]{:S(2)}) copy-start(bf16[64,896,16]{1,2,0:T(8,128)(2,1)} %param.23) | copy-start | bytes 5505028
  7.2 45.0 %all-gather.3.cloned.1.call-start = ((), (), s32[]{:S(2)}) async-start(), calls=%async_computation.5 | async-start | bytes 2228224 | tf_op jit(solution)/shard_map/all_gather | solution.py:63
  54.4 2.8 copy-start.11
  57.2 3.9 copy-start.2
  57.2 3.9 copy-start.12
  67.2 8.1 %copy-start.9 = (bf16[64,16,512]{2,1,0:T(8,128)(2,1)S(1)}, bf16[64,16,512]{2,1,0:T(8,128)(2,1)}, u32[]{:S(2)}) copy-start(bf16[64,16,512]{2,1,0:T(8,128)(2,1)} %param.20) | copy-start | bytes 3145732
  67.2 131.7 %all-to-all-start = ((bf16[16,128,1824]{1,2,0:T(8,128)(2,1)}), bf16[16,128,1824]{1,2,0:T(8,128)(2,1)}, u32[]{:S(2)}, u32[]{:S(2)}) async-start(bf16[16,128,1824]{1,2,0:T(8,128)(2,1)} %copy_bitcast_fusion), calls=%async_computation | async-start | bytes 14942208 | tf_op jit(solution)/shard_map/all_to_all | solution.py:15
  74.6 40.5 %all-gather.5.cloned.1.call-start = ((), (), s32[]{:S(2)}) async-start(), calls=%async_computation.6 | async-start | bytes 2228224 | tf_op jit(solution)/shard_map/all_gather | solution.py:65
  198.9 4.4 copy-start.4
  205.8 16.8 %copy-start.10 = (s32[32]{0:T(128)S(1)}, s32[32]{0:T(128)}, u32[]{:S(2)}) copy-start(s32[32]{0:T(128)} %param.24) | copy-start | bytes 388
  205.8 65.2 %all-to-all-start.2 = ((bf16[16,128,912]{1,2,0:T(8,128)(2,1)}), bf16[16,128,912]{1,2,0:T(8,128)(2,1)}, u32[]{:S(2)}, u32[]{:S(2)}) async-start(bf16[16,128,912]{1,2,0:T(8,128)(2,1)} %copy_bitcast_fusion.1), calls=%async_computation.2 | async-start | bytes 7471104 | tf_op jit(solution)/shard_map/all_to_all | solution.py:15
  225.3 48.3 %copy-start.8 = (bf16[2,16,896]{2,1,0:T(8,128)(2,1)}, bf16[2,16,896]{2,1,0:T(8,128)(2,1)S(1)}, u32[]{:S(2)}) copy-start(bf16[2,16,896]{2,1,0:T(8,128)(2,1)S(1)} %gather_fusion.2) | copy-start | bytes 172036
  227.4 2.8 copy-start.6
  282.6 48.7 %all-to-all-start.1 = ((bf16[16,128,896]{2,1,0:T(8,128)(2,1)}), bf16[16,128,896]{2,1,0:T(8,128)(2,1)}, u32[]{:S(2)}, u32[]{:S(2)}) async-start(bf16[16,128,896]{2,1,0:T(8,128)(2,1)} %broadcast_in_dim.18), calls=%async_computation.1 | async-start | bytes 7340032 | tf_op jit(solution)/shard_map/all_to_all | solution.py:21
  289.0 0.9 copy-start.5
  289.0 2.4 copy-start.7
  344.4 58.2 %all-to-all-start.3 = ((bf16[16,128,560]{1,2,0:T(8,128)(2,1)}), bf16[16,128,560]{1,2,0:T(8,128)(2,1)}, u32[]{:S(2)}, u32[]{:S(2)}) async-start(bf16[16,128,560]{1,2,0:T(8,128)(2,1)} %pad_maximum_fusion.1), calls=%async_computation.3 | async-start | bytes 4587520 | tf_op jit(solution)/shard_map/all_to_all | solution.py:15
  404.5 9.8 %copy-start.1 = (s32[64]{0:T(128)S(1)}, s32[64]{0:T(128)}, u32[]{:S(2)}) copy-start(s32[64]{0:T(128)} %param.25) | copy-start | bytes 772
  406.4 36.8 %all-to-all-start.4 = ((bf16[16,72,896]{2,1,0:T(8,128)(2,1)}), bf16[16,72,896]{2,1,0:T(8,128)(2,1)}, u32[]{:S(2)}, u32[]{:S(2)}) async-start(bf16[16,72,896]{2,1,0:T(8,128)(2,1)} %broadcast_in_dim.22), calls=%async_computation.4 | async-start | bytes 4128768 | tf_op jit(solution)/shard_map/all_to_all | solution.py:21
  451.4 3.5 copy-start.3
Sparse Core Ops, SparseCore 0:
  9.8 42.3 all-gather.2
  77.2 37.7 all-gather.4

commit v6 on v5

--- a/solution.py
+++ b/solution.py
@@ -9,11 +9,14 @@
 adapter_scale = 0.5
 
 
-def scatter_sum(x, axis):
+def exchange_pieces(x, axis):
     count = lax.axis_size(axis)
     pieces = x.astype(jnp.bfloat16).reshape((count, x.shape[0] // count) + x.shape[1:])
-    got = lax.all_to_all(pieces, axis, 0, 0, tiled=False)
-    return got.astype(jnp.float32).sum(0)
+    return lax.all_to_all(pieces, axis, 0, 0, tiled=False)
+
+
+def scatter_sum(x, axis):
+    return exchange_pieces(x, axis).astype(jnp.float32).sum(0)
 
 
 def gather_rows(x, axis):
@@ -73,7 +76,7 @@
     up_rank_part = jnp.einsum(
         "btk,bkr->btr", input_blocks, up_in[tenants], preferred_element_type=jnp.float32
     ).reshape(every_token_row, rank_width)
-    forward_sums = scatter_sum(
+    forward_got = exchange_pieces(
         jnp.concatenate(
             [
                 gate_part.astype(jnp.bfloat16),
@@ -85,6 +88,7 @@
         ),
         "dp",
     )
+    forward_sums = forward_got.astype(jnp.float32).sum(0)
     gate_total_sum = forward_sums[:, :width_here]
     up_total_sum = forward_sums[:, width_here : 2 * width_here]
     gate_rank = forward_sums[:, 2 * width_here : 2 * width_here + rank_width]
@@ -114,7 +118,7 @@
     back_pieces = jnp.concatenate(
         [hidden_grad_part.astype(jnp.bfloat16), down_back_part.astype(jnp.bfloat16)], axis=1
     )
-    forward_sums, back_pieces = lax.optimization_barrier((forward_sums, back_pieces))
+    forward_got, back_pieces = lax.optimization_barrier((forward_got, back_pieces))
     back_sums = scatter_sum(back_pieces, "dp")
     hidden_grad_sum = back_sums[:, :width_here]
     group_down_back = back_sums[:, width_here:].astype(jnp.bfloat16)

time: 465 us -> 463 us (level)
  transfers between devices with their start and end apart: 7 -> 7, of which waited for: 7 -> 7; matrix products, arithmetic and copies ran while one was open for 7% -> 8% of each run, Pallas kernels for 0% -> 0%
where the time goes in v6:
time: 463 us; the launch traced here: 462 us
  waiting for transfers between devices  291 us (63%)
  starting transfers between devices  43.2 us (9%)
  matrix products  38.2 us (8%)
  local copies, waits for them, and re-layouts  36.6 us (8%)
  other arithmetic  22.1 us (5%)
  blocking collectives  15.9 us (3%)
  between operations  14.6 us (3%)
    all_to_all x3, waiting for transfers between devices, exchange_pieces(): return lax.all_to_all(pieces, axis, 0, 0, tiled=False)  165 us
    all_to_all x2, waiting for transfers between devices, gather_rows(): lax.all_to_all(jnp.broadcast_to(x[None], (count,) + x.shape), axis, 0, 0,...  45.6 us
    all_gather x1, waiting for transfers between devices, shards(): all_inputs = lax.all_gather(tokens, 'tensor', axis=0, tiled=True)  40 us
    all_gather x1, waiting for transfers between devices, shards(): all_cot = lax.all_gather(cotangent, 'tensor', axis=0, tiled=True)  39.1 us
    all_to_all x3, starting transfers between devices, exchange_pieces(): return lax.all_to_all(pieces, axis, 0, 0, tiled=False)  28.8 us
    all_gather x1, blocking collectives, shards(): all_down_rank = lax.all_gather(down_rank_flat, 'tensor', axis=0, tiled=True)  15.9 us
    all_to_all x2, starting transfers between devices, gather_rows(): lax.all_to_all(jnp.broadcast_to(x[None], (count,) + x.shape), axis, 0, 0,...  14.3 us
  transfers between devices with their start and end apart: 7, of which 7 were waited for; matrix products, arithmetic and copies ran while one was open for 8% of the time, Pallas kernels for 0%

profile of v6, /device:TPU:8, one launch (start us, length us, event | category | flops | bytes accessed | tf_op | source)
XLA Modules:
  0.0 461.7 jit_solution(18328511936901871741)
XLA Ops:
  12.2 40.0 %all-gather.3.cloned.1.call-done = bf16[2048,512]{1,0:T(8,128)(2,1)} async-done(((bf16[128,512]{1,0:T(8,128)(2,1)}), bf16[2048,512]{1,0:T(8,128)(2,1)}) %all-gather.3.cloned.1.call-update) | async-done | bytes 2097168 | tf_op jit(solution)/shard_map/all_gather | solution.py:66
  52.2 2.2 fusion.3
  54.7 2.3 fusion.4
  57.2 3.9 convolution_convert_fusion.1
  61.1 2.2 convolution_convert_fusion.2
  63.3 3.9 copy_bitcast_fusion
  67.2 7.4 %all-to-all-start = ((bf16[16,128,1824]{1,2,0:T(8,128)(2,1)}), bf16[16,128,1824]{1,2,0:T(8,128)(2,1)}, u32[]{:S(2)}, u32[]{:S(2)}) async-start(bf16[16,128,1824]{1,2,0:T(8,128)(2,1)} %copy_bitcast_fusion), calls=%async_computation | async-start | bytes 14942208 | tf_op jit(solution)/shard_map/all_to_all | solution.py:15
  75.9 39.1 %all-gather.5.cloned.1.call-done = bf16[2048,512]{1,0:T(8,128)(2,1)} async-done(((bf16[128,512]{1,0:T(8,128)(2,1)}), bf16[2048,512]{1,0:T(8,128)(2,1)}) %all-gather.5.cloned.1.call-update) | async-done | bytes 2097168 | tf_op jit(solution)/shard_map/all_gather | solution.py:68
  115.0 2.2 fusion.2
  117.5 3.9 convolution_convert_fusion
  121.4 2.3 pad_maximum_fusion
  123.7 75.1 %all-to-all-done = bf16[16,128,1824]{1,2,0:T(8,128)(2,1)} async-done(((bf16[16,128,1824]{1,2,0:T(8,128)(2,1)}), bf16[16,128,1824]{1,2,0:T(8,128)(2,1)}, u32[]{:S(2)}, u32[]{:S(2)}) %all-to-all-start) | async-done | bytes 7471136 | tf_op jit(solution)/shard_map/all_to_all | solution.py:15
  198.9 4.6 %copy_bitcast_fusion.1 = bf16[16,128,912]{1,2,0:T(8,128)(2,1)} fusion(bf16[2048,912]{0,1:T(8,128)(2,1)} %pad_maximum_fusion), kind=kLoop, calls=%fused_computation.14 | loop fusion | bytes 7471104 | tf_op jit(solution)/shard_map/reshape | solution.py:14
  203.5 16.8 %all-to-all-start.2 = ((bf16[16,128,912]{1,2,0:T(8,128)(2,1)}), bf16[16,128,912]{1,2,0:T(8,128)(2,1)}, u32[]{:S(2)}, u32[]{:S(2)}) async-start(bf16[16,128,912]{1,2,0:T(8,128)(2,1)} %copy_bitcast_fusion.1), calls=%async_computation.2 | async-start | bytes 7471104 | tf_op jit(solution)/shard_map/all_to_all | solution.py:15
  221.0 2.1 gather_fusion.2
  223.1 2.1 gather_fusion.3
  225.2 4.2 convert_reduce_fusion
  232.1 36.6 %all-to-all-done.2 = bf16[16,128,912]{1,2,0:T(8,128)(2,1)} async-done(((bf16[16,128,912]{1,2,0:T(8,128)(2,1)}), bf16[16,128,912]{1,2,0:T(8,128)(2,1)}, u32[]{:S(2)}, u32[]{:S(2)}) %all-to-all-start.2) | async-done | bytes 3735584 | tf_op jit(solution)/shard_map/all_to_all | solution.py:15
  268.8 2.6 convert_reduce_fusion.1
  274.5 2.4 multiply_convert_fusion.1
  278.0 2.3 broadcast_in_dim.18
  280.3 6.4 %all-to-all-start.1 = ((bf16[16,128,896]{2,1,0:T(8,128)(2,1)}), bf16[16,128,896]{2,1,0:T(8,128)(2,1)}, u32[]{:S(2)}, u32[]{:S(2)}) async-start(bf16[16,128,896]{2,1,0:T(8,128)(2,1)} %broadcast_in_dim.18), calls=%async_computation.1 | async-start | bytes 7340032 | tf_op jit(solution)/shard_map/all_to_all | solution.py:24
  289.3 39.7 %all-to-all-done.1 = bf16[16,128,896]{2,1,0:T(8,128)(2,1)} async-done(((bf16[16,128,896]{2,1,0:T(8,128)(2,1)}), bf16[16,128,896]{2,1,0:T(8,128)(2,1)}, u32[]{:S(2)}, u32[]{:S(2)}) %all-to-all-start.1) | async-done | bytes 3670048 | tf_op jit(solution)/shard_map/all_to_all | solution.py:24
  329.0 6.0 %convolution_convert_fusion.3 = bf16[2048,512]{0,1:T(8,128)(2,1)} fusion(bf16[2048,896]{1,0:T(8,128)(2,1)} %bitcast.5, bf16[896,512]{1,0:T(8,128)(2,1)} %param.17), kind=kOutput, calls=%fused_computation.19 | convolution fusion | flops 1880096768 | bytes 6684672 | tf_op jit(solution)/shard_map/dot_general | solution.py:150
  335.0 3.2 convolution_convert_fusion.4
  342.0 4.6 all-to-all-start.3
  347.0 53.2 %all-to-all-done.3 = bf16[16,128,560]{1,2,0:T(8,128)(2,1)} async-done(((bf16[16,128,560]{1,2,0:T(8,128)(2,1)}), bf16[16,128,560]{1,2,0:T(8,128)(2,1)}, u32[]{:S(2)}, u32[]{:S(2)}) %all-to-all-start.3) | async-done | bytes 2293792 | tf_op jit(solution)/shard_map/all_to_all | solution.py:15
  404.0 8.0 %all-to-all-start.4 = ((bf16[16,72,896]{2,1,0:T(8,128)(2,1)}), bf16[16,72,896]{2,1,0:T(8,128)(2,1)}, u32[]{:S(2)}, u32[]{:S(2)}) async-start(bf16[16,72,896]{2,1,0:T(8,128)(2,1)} %broadcast_in_dim.22), calls=%async_computation.4 | async-start | bytes 4128768 | tf_op jit(solution)/shard_map/all_to_all | solution.py:24
  416.3 15.9 %all_gather.11 = bf16[2048,16]{0,1:T(8,128)(2,1)S(1)} all-gather(bf16[128,16]{0,1:T(8,128)(2,1)S(1)} %slice.104), channel_id=1, replica_groups=mesh['dp'=16,'tensor'=16] {'tensor'}, dimensions={0}, use_global_device_ids=true | all-gather | bytes 69632 | tf_op jit(solution)/shard_map/all_gather | solution.py:189
  432.2 2.7 fusion.5
  434.9 6.0 %all-to-all-done.4 = bf16[16,72,896]{2,1,0:T(8,128)(2,1)} async-done(((bf16[16,72,896]{2,1,0:T(8,128)(2,1)}), bf16[16,72,896]{2,1,0:T(8,128)(2,1)}, u32[]{:S(2)}, u32[]{:S(2)}) %all-to-all-start.4) | async-done | bytes 2064416 | tf_op jit(solution)/shard_map/all_to_all | solution.py:24
  449.0 3.5 convolution_bitcast_fusion
  (118 shorter events, 39.7 us)
Async XLA Ops:
  7.2 213.2 %copy-start = (bf16[64,896,16]{1,2,0:T(8,128)(2,1)S(1)}, bf16[64,896,16]{1,2,0:T(8,128)(2,1)}, u32[]{:S(2)}) copy-start(bf16[64,896,16]{1,2,0:T(8,128)(2,1)} %param.23) | copy-start | bytes 5505028
  7.2 45.0 %all-gather.3.cloned.1.call-start = ((), (), s32[]{:S(2)}) async-start(), calls=%async_computation.5 | async-start | bytes 2228224 | tf_op jit(solution)/shard_map/all_gather | solution.py:66
  54.4 2.8 copy-start.10
  57.2 3.9 copy-start.2
  57.2 3.9 copy-start.11
  67.2 8.1 %copy-start.8 = (bf16[64,16,512]{2,1,0:T(8,128)(2,1)S(1)}, bf16[64,16,512]{2,1,0:T(8,128)(2,1)}, u32[]{:S(2)}) copy-start(bf16[64,16,512]{2,1,0:T(8,128)(2,1)} %param.20) | copy-start | bytes 3145732
  67.2 131.7 %all-to-all-start = ((bf16[16,128,1824]{1,2,0:T(8,128)(2,1)}), bf16[16,128,1824]{1,2,0:T(8,128)(2,1)}, u32[]{:S(2)}, u32[]{:S(2)}) async-start(bf16[16,128,1824]{1,2,0:T(8,128)(2,1)} %copy_bitcast_fusion), calls=%async_computation | async-start | bytes 14942208 | tf_op jit(solution)/shard_map/all_to_all | solution.py:15
  74.6 40.5 %all-gather.5.cloned.1.call-start = ((), (), s32[]{:S(2)}) async-start(), calls=%async_computation.6 | async-start | bytes 2228224 | tf_op jit(solution)/shard_map/all_gather | solution.py:68
  203.5 16.8 %copy-start.9 = (s32[32]{0:T(128)S(1)}, s32[32]{0:T(128)}, u32[]{:S(2)}) copy-start(s32[32]{0:T(128)} %param.24) | copy-start | bytes 388
  203.5 65.2 %all-to-all-start.2 = ((bf16[16,128,912]{1,2,0:T(8,128)(2,1)}), bf16[16,128,912]{1,2,0:T(8,128)(2,1)}, u32[]{:S(2)}, u32[]{:S(2)}) async-start(bf16[16,128,912]{1,2,0:T(8,128)(2,1)} %copy_bitcast_fusion.1), calls=%async_computation.2 | async-start | bytes 7471104 | tf_op jit(solution)/shard_map/all_to_all | solution.py:15
  223.0 6.5 %copy-start.7 = (bf16[2,16,896]{2,1,0:T(8,128)(2,1)}, bf16[2,16,896]{2,1,0:T(8,128)(2,1)S(1)}, u32[]{:S(2)}) copy-start(bf16[2,16,896]{2,1,0:T(8,128)(2,1)S(1)} %gather_fusion.2) | copy-start | bytes 172036
  225.1 5.7 %copy-start.5 = (bf16[2,16,896]{2,1,0:T(8,128)(2,1)}, bf16[2,16,896]{2,1,0:T(8,128)(2,1)S(1)}, u32[]{:S(2)}) copy-start(bf16[2,16,896]{2,1,0:T(8,128)(2,1)S(1)} %gather_fusion.3) | copy-start | bytes 172036
  280.3 48.7 %all-to-all-start.1 = ((bf16[16,128,896]{2,1,0:T(8,128)(2,1)}), bf16[16,128,896]{2,1,0:T(8,128)(2,1)}, u32[]{:S(2)}, u32[]{:S(2)}) async-start(bf16[16,128,896]{2,1,0:T(8,128)(2,1)} %broadcast_in_dim.18), calls=%async_computation.1 | async-start | bytes 7340032 | tf_op jit(solution)/shard_map/all_to_all | solution.py:24
  286.7 0.9 copy-start.4
  286.7 2.4 copy-start.6
  342.0 58.2 %all-to-all-start.3 = ((bf16[16,128,560]{1,2,0:T(8,128)(2,1)}), bf16[16,128,560]{1,2,0:T(8,128)(2,1)}, u32[]{:S(2)}, u32[]{:S(2)}) async-start(bf16[16,128,560]{1,2,0:T(8,128)(2,1)} %pad_maximum_fusion.1), calls=%async_computation.3 | async-start | bytes 4587520 | tf_op jit(solution)/shard_map/all_to_all | solution.py:15
  402.2 9.8 %copy-start.1 = (s32[64]{0:T(128)S(1)}, s32[64]{0:T(128)}, u32[]{:S(2)}) copy-start(s32[64]{0:T(128)} %param.25) | copy-start | bytes 772
  404.0 36.8 %all-to-all-start.4 = ((bf16[16,72,896]{2,1,0:T(8,128)(2,1)}), bf16[16,72,896]{2,1,0:T(8,128)(2,1)}, u32[]{:S(2)}, u32[]{:S(2)}) async-start(bf16[16,72,896]{2,1,0:T(8,128)(2,1)} %broadcast_in_dim.22), calls=%async_computation.4 | async-start | bytes 4128768 | tf_op jit(solution)/shard_map/all_to_all | solution.py:24
  449.0 3.5 copy-start.3
Sparse Core Ops, SparseCore 0:
  9.8 42.3 all-gather.2
  77.2 37.7 all-gather.4

commit v7 on v6

--- a/solution.py
+++ b/solution.py
@@ -63,9 +63,9 @@
     token_tenants = jnp.broadcast_to(tenants[:, None], (blocks_all, BLOCK)).reshape(every_token_row)
     held_tenants = tensor_index * tenants_here + jnp.arange(tenants_here, dtype=jnp.int32)
     token_onehot = (token_tenants[:, None] == held_tenants[None, :]).astype(jnp.bfloat16)
-    all_inputs = lax.all_gather(tokens, "tensor", axis=0, tiled=True)
+    all_inputs = gather_rows(tokens, "tensor")
     cotangent = lax.optimization_barrier((all_inputs, cotangent))[1]
-    all_cot = lax.all_gather(cotangent, "tensor", axis=0, tiled=True)
+    all_cot = gather_rows(cotangent, "tensor")
 
     gate_part = jnp.dot(all_inputs, gate_weight, preferred_element_type=jnp.float32)
     up_part = jnp.dot(all_inputs, up_weight, preferred_element_type=jnp.float32)

time: 463 us -> 506 us (1.093)
  blocking collectives: 15.9 us -> 74 us
  waiting for transfers between devices: 291 us -> 275 us
  between operations: 14.6 us -> 1.18 us
  starting transfers between devices: 43.2 us -> 51.8 us
    all_gather x2 -> x0, waiting for transfers between devices: 79.1 us -> none  [the longest x1 40 us: shards(): all_inputs = lax.all_gather(tokens, 'tensor', axis=0, tiled=True)]
    all_to_all x0 -> x1, blocking collectives: none -> 58.1 us  [gather_rows(): lax.all_to_all(jnp.broadcast_to(x[None], (count,) + x.shape), axis, 0, 0,...]
    all_to_all x3, waiting for transfers between devices: 165 us -> 200 us  [exchange_pieces(): return lax.all_to_all(pieces, axis, 0, 0, tiled=False)]
    all_to_all x2 -> x3, waiting for transfers between devices: 45.6 us -> 75.5 us  [gather_rows(): lax.all_to_all(jnp.broadcast_to(x[None], (count,) + x.shape), axis, 0, 0,...]
    all_to_all x3, starting transfers between devices: 28.8 us -> 33.9 us  [exchange_pieces(): return lax.all_to_all(pieces, axis, 0, 0, tiled=False)]
    all_to_all x2 -> x3, starting transfers between devices: 14.3 us -> 17.9 us  [gather_rows(): lax.all_to_all(jnp.broadcast_to(x[None], (count,) + x.shape), axis, 0, 0,...]
  transfers between devices with their start and end apart: 7 -> 6, of which waited for: 7 -> 6; matrix products, arithmetic and copies ran while one was open for 8% -> 10% of each run, Pallas kernels for 0% -> 0%
where the time goes in v7:
time: 506 us; the launch traced here: 505 us
  waiting for transfers between devices  275 us (54%)
  blocking collectives  74 us (15%)
  starting transfers between devices  51.8 us (10%)
  matrix products  41.3 us (8%)
  local copies, waits for them, and re-layouts  39.4 us (8%)
  other arithmetic  21.5 us (4%)
    all_to_all x3, waiting for transfers between devices, exchange_pieces(): return lax.all_to_all(pieces, axis, 0, 0, tiled=False)  200 us
    all_to_all x3, waiting for transfers between devices, gather_rows(): lax.all_to_all(jnp.broadcast_to(x[None], (count,) + x.shape), axis, 0, 0,...  75.5 us
    all_to_all x1, blocking collectives, gather_rows(): lax.all_to_all(jnp.broadcast_to(x[None], (count,) + x.shape), axis, 0, 0,...  58.1 us
    all_to_all x3, starting transfers between devices, exchange_pieces(): return lax.all_to_all(pieces, axis, 0, 0, tiled=False)  33.9 us
    all_to_all x3, starting transfers between devices, gather_rows(): lax.all_to_all(jnp.broadcast_to(x[None], (count,) + x.shape), axis, 0, 0,...  17.9 us
    all_gather x1, blocking collectives, shards(): all_down_rank = lax.all_gather(down_rank_flat, 'tensor', axis=0, tiled=True)  15.9 us
  transfers between devices with their start and end apart: 6, of which 6 were waited for; matrix products, arithmetic and copies ran while one was open for 10% of the time, Pallas kernels for 0%

profile of v7, /device:TPU:8, one launch (start us, length us, event | category | flops | bytes accessed | tf_op | source)
XLA Modules:
  0.0 504.5 jit_solution(6630775170100928872)
XLA Ops:
  1.9 58.1 %all_to_all.35 = bf16[16,128,512]{2,1,0:T(8,128)(2,1)} all-to-all(bf16[16,128,512]{2,1,0:T(8,128)(2,1)S(1)} %broadcast_in_dim.20), channel_id=1, replica_groups=mesh['dp'=16,'tensor'=16] {'tensor'}, dimensions={0} | all-to-all | bytes 4194304 | tf_op jit(solution)/shard_map/all_to_all | solution.py:24
  61.5 4.4 all-to-all-start.3
  69.6 2.2 fusion.1
  72.1 2.3 fusion.2
  74.7 3.9 convolution_convert_fusion.1
  80.7 3.9 copy_bitcast_fusion
  84.6 30.6 %all-to-all-done.3 = bf16[16,128,512]{2,1,0:T(8,128)(2,1)} async-done(((bf16[16,128,512]{2,1,0:T(8,128)(2,1)}), bf16[16,128,512]{2,1,0:T(8,128)(2,1)}, u32[]{:S(2)}, u32[]{:S(2)}) %all-to-all-start.3) | async-done | bytes 2097184 | tf_op jit(solution)/shard_map/all_to_all | solution.py:24
  115.2 7.4 %all-to-all-start.1 = ((bf16[16,128,1824]{1,2,0:T(8,128)(2,1)}), bf16[16,128,1824]{1,2,0:T(8,128)(2,1)}, u32[]{:S(2)}, u32[]{:S(2)}) async-start(bf16[16,128,1824]{1,2,0:T(8,128)(2,1)} %copy_bitcast_fusion), calls=%async_computation.1 | async-start | bytes 14942208 | tf_op jit(solution)/shard_map/all_to_all | solution.py:15
  123.2 2.2 fusion
  125.7 3.9 convolution_convert_fusion
  129.6 2.3 pad_maximum_fusion
  131.9 111.1 %all-to-all-done.1 = bf16[16,128,1824]{1,2,0:T(8,128)(2,1)} async-done(((bf16[16,128,1824]{1,2,0:T(8,128)(2,1)}), bf16[16,128,1824]{1,2,0:T(8,128)(2,1)}, u32[]{:S(2)}, u32[]{:S(2)}) %all-to-all-start.1) | async-done | bytes 7471136 | tf_op jit(solution)/shard_map/all_to_all | solution.py:15
  243.0 4.7 copy_bitcast_fusion.1
  247.7 19.1 %all-to-all-start.4 = ((bf16[16,128,912]{1,2,0:T(8,128)(2,1)}), bf16[16,128,912]{1,2,0:T(8,128)(2,1)}, u32[]{:S(2)}, u32[]{:S(2)}) async-start(bf16[16,128,912]{1,2,0:T(8,128)(2,1)} %copy_bitcast_fusion.1), calls=%async_computation.4 | async-start | bytes 7471104 | tf_op jit(solution)/shard_map/all_to_all | solution.py:15
  271.6 4.2 convert_reduce_fusion
  278.5 35.6 %all-to-all-done.4 = bf16[16,128,912]{1,2,0:T(8,128)(2,1)} async-done(((bf16[16,128,912]{1,2,0:T(8,128)(2,1)}), bf16[16,128,912]{1,2,0:T(8,128)(2,1)}, u32[]{:S(2)}, u32[]{:S(2)}) %all-to-all-start.4) | async-done | bytes 3735584 | tf_op jit(solution)/shard_map/all_to_all | solution.py:15
  314.1 2.6 convert_reduce_fusion.1
  319.8 2.4 multiply_convert_fusion.1
  323.3 2.4 broadcast_in_dim.23
  325.7 5.7 %all-to-all-start.2 = ((bf16[16,128,896]{2,1,0:T(8,128)(2,1)}), bf16[16,128,896]{2,1,0:T(8,128)(2,1)}, u32[]{:S(2)}, u32[]{:S(2)}) async-start(bf16[16,128,896]{2,1,0:T(8,128)(2,1)} %broadcast_in_dim.23), calls=%async_computation.2 | async-start | bytes 7340032 | tf_op jit(solution)/shard_map/all_to_all | solution.py:24
  334.0 39.0 %all-to-all-done.2 = bf16[16,128,896]{2,1,0:T(8,128)(2,1)} async-done(((bf16[16,128,896]{2,1,0:T(8,128)(2,1)}), bf16[16,128,896]{2,1,0:T(8,128)(2,1)}, u32[]{:S(2)}, u32[]{:S(2)}) %all-to-all-start.2) | async-done | bytes 3670048 | tf_op jit(solution)/shard_map/all_to_all | solution.py:24
  373.0 6.0 %convolution_convert_fusion.3 = bf16[2048,512]{0,1:T(8,128)(2,1)} fusion(bf16[2048,896]{1,0:T(8,128)(2,1)} %bitcast.6, bf16[896,512]{1,0:T(8,128)(2,1)} %param.17), kind=kOutput, calls=%fused_computation.19 | convolution fusion | flops 1880096768 | bytes 6684672 | tf_op jit(solution)/shard_map/dot_general | solution.py:150
  379.0 3.2 convolution_convert_fusion.4
  386.1 7.4 %all-to-all-start.5 = ((bf16[16,128,560]{1,2,0:T(8,128)(2,1)}), bf16[16,128,560]{1,2,0:T(8,128)(2,1)}, u32[]{:S(2)}, u32[]{:S(2)}) async-start(bf16[16,128,560]{1,2,0:T(8,128)(2,1)} %pad_maximum_fusion.1), calls=%async_computation.5 | async-start | bytes 4587520 | tf_op jit(solution)/shard_map/all_to_all | solution.py:15
  393.9 53.2 %all-to-all-done.5 = bf16[16,128,560]{1,2,0:T(8,128)(2,1)} async-done(((bf16[16,128,560]{1,2,0:T(8,128)(2,1)}), bf16[16,128,560]{1,2,0:T(8,128)(2,1)}, u32[]{:S(2)}, u32[]{:S(2)}) %all-to-all-start.5) | async-done | bytes 2293792 | tf_op jit(solution)/shard_map/all_to_all | solution.py:15
  450.9 7.8 %all-to-all-start.6 = ((bf16[16,72,896]{2,1,0:T(8,128)(2,1)}), bf16[16,72,896]{2,1,0:T(8,128)(2,1)}, u32[]{:S(2)}, u32[]{:S(2)}) async-start(bf16[16,72,896]{2,1,0:T(8,128)(2,1)} %broadcast_in_dim.28), calls=%async_computation.6 | async-start | bytes 4128768 | tf_op jit(solution)/shard_map/all_to_all | solution.py:24
  463.0 15.9 %all_gather.3 = bf16[2048,16]{0,1:T(8,128)(2,1)S(1)} all-gather(bf16[128,16]{0,1:T(8,128)(2,1)S(1)} %slice.104), channel_id=1, replica_groups=mesh['dp'=16,'tensor'=16] {'tensor'}, dimensions={0}, use_global_device_ids=true | all-gather | bytes 69632 | tf_op jit(solution)/shard_map/all_gather | solution.py:189
  478.9 2.7 convolution_multiply_fusion.4
  481.6 5.9 %all-to-all-done.6 = bf16[16,72,896]{2,1,0:T(8,128)(2,1)} async-done(((bf16[16,72,896]{2,1,0:T(8,128)(2,1)}), bf16[16,72,896]{2,1,0:T(8,128)(2,1)}, u32[]{:S(2)}, u32[]{:S(2)}) %all-to-all-start.6) | async-done | bytes 2064416 | tf_op jit(solution)/shard_map/all_to_all | solution.py:24
  495.7 2.7 fusion.39
  498.4 2.7 fusion.38
  501.2 3.4 convolution_bitcast_fusion
  (117 shorter events, 44.3 us)
Async XLA Ops:
  0.6 266.2 %copy-start = (bf16[64,896,16]{1,2,0:T(8,128)(2,1)S(1)}, bf16[64,896,16]{1,2,0:T(8,128)(2,1)}, u32[]{:S(2)}) copy-start(bf16[64,896,16]{1,2,0:T(8,128)(2,1)} %param.23) | copy-start | bytes 5505028
  0.6 59.4 %copy-start.8 = (bf16[128,512]{1,0:T(8,128)(2,1)S(1)}, bf16[128,512]{1,0:T(8,128)(2,1)}, u32[]{:S(2)}) copy-start(bf16[128,512]{1,0:T(8,128)(2,1)} %param.14) | copy-start | bytes 393220
  60.0 5.9 %copy-start.9 = (s32[32]{0:T(128)S(1)}, s32[32]{0:T(128)}, u32[]{:S(2)}) copy-start(s32[32]{0:T(128)} %param.24) | copy-start | bytes 388
  61.5 53.7 %all-to-all-start.3 = ((bf16[16,128,512]{2,1,0:T(8,128)(2,1)}), bf16[16,128,512]{2,1,0:T(8,128)(2,1)}, u32[]{:S(2)}, u32[]{:S(2)}) async-start(bf16[16,128,512]{2,1,0:T(8,128)(2,1)} %broadcast_in_dim.24), calls=%async_computation.3 | async-start | bytes 4194304 | tf_op jit(solution)/shard_map/all_to_all | solution.py:24
  71.9 2.8 copy-start.10
  74.7 3.9 copy-start.2
  74.7 3.9 copy-start.11
  84.6 38.0 %copy-start.7 = (bf16[64,16,512]{2,1,0:T(8,128)(2,1)S(1)}, bf16[64,16,512]{2,1,0:T(8,128)(2,1)}, u32[]{:S(2)}) copy-start(bf16[64,16,512]{2,1,0:T(8,128)(2,1)} %param.20) | copy-start | bytes 3145732
  115.2 127.8 %all-to-all-start.1 = ((bf16[16,128,1824]{1,2,0:T(8,128)(2,1)}), bf16[16,128,1824]{1,2,0:T(8,128)(2,1)}, u32[]{:S(2)}, u32[]{:S(2)}) async-start(bf16[16,128,1824]{1,2,0:T(8,128)(2,1)} %copy_bitcast_fusion), calls=%async_computation.1 | async-start | bytes 14942208 | tf_op jit(solution)/shard_map/all_to_all | solution.py:15
  247.7 66.4 %all-to-all-start.4 = ((bf16[16,128,912]{1,2,0:T(8,128)(2,1)}), bf16[16,128,912]{1,2,0:T(8,128)(2,1)}, u32[]{:S(2)}, u32[]{:S(2)}) async-start(bf16[16,128,912]{1,2,0:T(8,128)(2,1)} %copy_bitcast_fusion.1), calls=%async_computation.4 | async-start | bytes 7471104 | tf_op jit(solution)/shard_map/all_to_all | solution.py:15
  269.5 6.5 %copy-start.6 = (bf16[2,16,896]{2,1,0:T(8,128)(2,1)}, bf16[2,16,896]{2,1,0:T(8,128)(2,1)S(1)}, u32[]{:S(2)}) copy-start(bf16[2,16,896]{2,1,0:T(8,128)(2,1)S(1)} %gather_fusion.2) | copy-start | bytes 172036
  271.6 5.7 %copy-start.4 = (bf16[2,16,896]{2,1,0:T(8,128)(2,1)}, bf16[2,16,896]{2,1,0:T(8,128)(2,1)S(1)}, u32[]{:S(2)}) copy-start(bf16[2,16,896]{2,1,0:T(8,128)(2,1)S(1)} %gather_fusion.3) | copy-start | bytes 172036
  325.7 47.4 %all-to-all-start.2 = ((bf16[16,128,896]{2,1,0:T(8,128)(2,1)}), bf16[16,128,896]{2,1,0:T(8,128)(2,1)}, u32[]{:S(2)}, u32[]{:S(2)}) async-start(bf16[16,128,896]{2,1,0:T(8,128)(2,1)} %broadcast_in_dim.23), calls=%async_computation.2 | async-start | bytes 7340032 | tf_op jit(solution)/shard_map/all_to_all | solution.py:24
  331.4 0.9 copy-start.3
  331.4 2.4 copy-start.5
  386.1 61.0 %all-to-all-start.5 = ((bf16[16,128,560]{1,2,0:T(8,128)(2,1)}), bf16[16,128,560]{1,2,0:T(8,128)(2,1)}, u32[]{:S(2)}, u32[]{:S(2)}) async-start(bf16[16,128,560]{1,2,0:T(8,128)(2,1)} %pad_maximum_fusion.1), calls=%async_computation.5 | async-start | bytes 4587520 | tf_op jit(solution)/shard_map/all_to_all | solution.py:15
  449.1 9.6 %copy-start.1 = (s32[64]{0:T(128)S(1)}, s32[64]{0:T(128)}, u32[]{:S(2)}) copy-start(s32[64]{0:T(128)} %param.25) | copy-start | bytes 772
  450.9 36.6 %all-to-all-start.6 = ((bf16[16,72,896]{2,1,0:T(8,128)(2,1)}), bf16[16,72,896]{2,1,0:T(8,128)(2,1)}, u32[]{:S(2)}, u32[]{:S(2)}) async-start(bf16[16,72,896]{2,1,0:T(8,128)(2,1)} %broadcast_in_dim.28), calls=%async_computation.6 | async-start | bytes 4128768 | tf_op jit(solution)/shard_map/all_to_all | solution.py:24

commit v8 on v6

--- a/solution.py
+++ b/solution.py
@@ -118,7 +118,7 @@
     back_pieces = jnp.concatenate(
         [hidden_grad_part.astype(jnp.bfloat16), down_back_part.astype(jnp.bfloat16)], axis=1
     )
-    forward_got, back_pieces = lax.optimization_barrier((forward_got, back_pieces))
+    all_hidden, back_pieces = lax.optimization_barrier((all_hidden, back_pieces))
     back_sums = scatter_sum(back_pieces, "dp")
     hidden_grad_sum = back_sums[:, :width_here]
     group_down_back = back_sums[:, width_here:].astype(jnp.bfloat16)

time: 463 us -> 469 us (1.013)
  local copies, waits for them, and re-layouts: 36.6 us -> 41.3 us
    all_to_all x3, waiting for transfers between devices: 165 us -> 205 us  [exchange_pieces(): return lax.all_to_all(pieces, axis, 0, 0, tiled=False)]
    all_gather x1, waiting for transfers between devices: 39.1 us -> 0.02 us  [shards(): all_cot = lax.all_gather(cotangent, 'tensor', axis=0, tiled=True)]
    all_to_all x2, starting transfers between devices: 14.3 us -> 25 us  [gather_rows(): lax.all_to_all(jnp.broadcast_to(x[None], (count,) + x.shape), axis, 0, 0,...]
    all_to_all x3, starting transfers between devices: 28.8 us -> 18.1 us  [exchange_pieces(): return lax.all_to_all(pieces, axis, 0, 0, tiled=False)]
  transfers between devices with their start and end apart: 7 -> 7, of which waited for: 7 -> 6; matrix products, arithmetic and copies ran while one was open for 8% -> 11% of each run, Pallas kernels for 0% -> 0%
where the time goes in v8:
time: 469 us; the launch traced here: 468 us
  waiting for transfers between devices  289 us (62%)
  starting transfers between devices  43.2 us (9%)
  local copies, waits for them, and re-layouts  41.3 us (9%)
  matrix products  39.4 us (8%)
  other arithmetic  24.5 us (5%)
  blocking collectives  15.8 us (3%)
  between operations  14.6 us (3%)
    all_to_all x3, waiting for transfers between devices, exchange_pieces(): return lax.all_to_all(pieces, axis, 0, 0, tiled=False)  205 us
    all_to_all x2, waiting for transfers between devices, gather_rows(): lax.all_to_all(jnp.broadcast_to(x[None], (count,) + x.shape), axis, 0, 0,...  43.3 us
    all_gather x1, waiting for transfers between devices, shards(): all_inputs = lax.all_gather(tokens, 'tensor', axis=0, tiled=True)  40 us
    all_to_all x2, starting transfers between devices, gather_rows(): lax.all_to_all(jnp.broadcast_to(x[None], (count,) + x.shape), axis, 0, 0,...  25 us
    all_to_all x3, starting transfers between devices, exchange_pieces(): return lax.all_to_all(pieces, axis, 0, 0, tiled=False)  18.1 us
    all_gather x1, blocking collectives, shards(): all_down_rank = lax.all_gather(down_rank_flat, 'tensor', axis=0, tiled=True)  15.8 us
  transfers between devices with their start and end apart: 7, of which 6 were waited for; matrix products, arithmetic and copies ran while one was open for 11% of the time, Pallas kernels for 0%

profile of v8, /device:TPU:8, one launch (start us, length us, event | category | flops | bytes accessed | tf_op | source)
XLA Modules:
  0.0 467.7 jit_solution(2562274837054436296)
XLA Ops:
  12.2 40.0 %all-gather.3.cloned.1.call-done = bf16[2048,512]{1,0:T(8,128)(2,1)} async-done(((bf16[128,512]{1,0:T(8,128)(2,1)}), bf16[2048,512]{1,0:T(8,128)(2,1)}) %all-gather.3.cloned.1.call-update) | async-done | bytes 2097168 | tf_op jit(solution)/shard_map/all_gather | solution.py:66
  52.2 2.2 fusion.8
  54.7 2.3 fusion.9
  57.2 3.9 convolution_convert_fusion.1
  61.1 2.2 convolution_convert_fusion.2
  63.3 3.9 copy_bitcast_fusion
  67.1 7.4 %all-to-all-start = ((bf16[16,128,1824]{1,2,0:T(8,128)(2,1)}), bf16[16,128,1824]{1,2,0:T(8,128)(2,1)}, u32[]{:S(2)}, u32[]{:S(2)}) async-start(bf16[16,128,1824]{1,2,0:T(8,128)(2,1)} %copy_bitcast_fusion), calls=%async_computation | async-start | bytes 14942208 | tf_op jit(solution)/shard_map/all_to_all | solution.py:15
  75.3 2.1 gather_fusion.2
  77.3 2.1 gather_fusion.3
  79.4 119.3 %all-to-all-done = bf16[16,128,1824]{1,2,0:T(8,128)(2,1)} async-done(((bf16[16,128,1824]{1,2,0:T(8,128)(2,1)}), bf16[16,128,1824]{1,2,0:T(8,128)(2,1)}, u32[]{:S(2)}, u32[]{:S(2)}) %all-to-all-start) | async-done | bytes 7471136 | tf_op jit(solution)/shard_map/all_to_all | solution.py:15
  198.7 4.2 convert_reduce_fusion
  210.5 3.3 broadcast_in_dim.18
  213.9 17.1 %all-to-all-start.1 = ((bf16[16,128,896]{2,1,0:T(8,128)(2,1)}), bf16[16,128,896]{2,1,0:T(8,128)(2,1)}, u32[]{:S(2)}, u32[]{:S(2)}) async-start(bf16[16,128,896]{2,1,0:T(8,128)(2,1)} %broadcast_in_dim.18), calls=%async_computation.1 | async-start | bytes 7340032 | tf_op jit(solution)/shard_map/all_to_all | solution.py:24
  232.8 2.2 fusion.7
  235.3 3.9 convolution_convert_fusion
  239.2 2.3 pad_maximum_fusion
  241.6 37.1 %all-to-all-done.1 = bf16[16,128,896]{2,1,0:T(8,128)(2,1)} async-done(((bf16[16,128,896]{2,1,0:T(8,128)(2,1)}), bf16[16,128,896]{2,1,0:T(8,128)(2,1)}, u32[]{:S(2)}, u32[]{:S(2)}) %all-to-all-start.1) | async-done | bytes 3670048 | tf_op jit(solution)/shard_map/all_to_all | solution.py:24
  278.6 4.6 copy_bitcast_fusion.1
  283.2 6.2 %all-to-all-start.2 = ((bf16[16,128,912]{1,2,0:T(8,128)(2,1)}), bf16[16,128,912]{1,2,0:T(8,128)(2,1)}, u32[]{:S(2)}, u32[]{:S(2)}) async-start(bf16[16,128,912]{1,2,0:T(8,128)(2,1)} %copy_bitcast_fusion.1), calls=%async_computation.2 | async-start | bytes 7471104 | tf_op jit(solution)/shard_map/all_to_all | solution.py:15
  290.7 3.2 convolution_convert_fusion.4
  294.2 4.7 convolution_convert_fusion.3
  300.6 32.2 %all-to-all-done.2 = bf16[16,128,912]{1,2,0:T(8,128)(2,1)} async-done(((bf16[16,128,912]{1,2,0:T(8,128)(2,1)}), bf16[16,128,912]{1,2,0:T(8,128)(2,1)}, u32[]{:S(2)}, u32[]{:S(2)}) %all-to-all-start.2) | async-done | bytes 3735584 | tf_op jit(solution)/shard_map/all_to_all | solution.py:15
  332.8 2.6 convert_reduce_fusion.1
  339.4 2.3 multiply_convert_fusion.1
  345.1 3.2 pad_maximum_fusion.1
  348.4 4.5 all-to-all-start.3
  353.2 53.1 %all-to-all-done.3 = bf16[16,128,560]{1,2,0:T(8,128)(2,1)} async-done(((bf16[16,128,560]{1,2,0:T(8,128)(2,1)}), bf16[16,128,560]{1,2,0:T(8,128)(2,1)}, u32[]{:S(2)}, u32[]{:S(2)}) %all-to-all-start.3) | async-done | bytes 2293792 | tf_op jit(solution)/shard_map/all_to_all | solution.py:15
  410.1 7.9 %all-to-all-start.4 = ((bf16[16,72,896]{2,1,0:T(8,128)(2,1)}), bf16[16,72,896]{2,1,0:T(8,128)(2,1)}, u32[]{:S(2)}, u32[]{:S(2)}) async-start(bf16[16,72,896]{2,1,0:T(8,128)(2,1)} %broadcast_in_dim.22), calls=%async_computation.4 | async-start | bytes 4128768 | tf_op jit(solution)/shard_map/all_to_all | solution.py:24
  422.2 15.8 %all_gather.11 = bf16[2048,16]{0,1:T(8,128)(2,1)S(1)} all-gather(bf16[128,16]{0,1:T(8,128)(2,1)S(1)} %slice.104), channel_id=1, replica_groups=mesh['dp'=16,'tensor'=16] {'tensor'}, dimensions={0}, use_global_device_ids=true | all-gather | bytes 69632 | tf_op jit(solution)/shard_map/all_gather | solution.py:189
  438.0 2.7 fusion.10
  440.7 6.2 %all-to-all-done.4 = bf16[16,72,896]{2,1,0:T(8,128)(2,1)} async-done(((bf16[16,72,896]{2,1,0:T(8,128)(2,1)}), bf16[16,72,896]{2,1,0:T(8,128)(2,1)}, u32[]{:S(2)}, u32[]{:S(2)}) %all-to-all-start.4) | async-done | bytes 2064416 | tf_op jit(solution)/shard_map/all_to_all | solution.py:24
  455.0 3.5 fusion.4
  (118 shorter events, 45.1 us)
Async XLA Ops:
  7.2 282.3 %copy-start = (bf16[64,896,16]{1,2,0:T(8,128)(2,1)S(1)}, bf16[64,896,16]{1,2,0:T(8,128)(2,1)}, u32[]{:S(2)}) copy-start(bf16[64,896,16]{1,2,0:T(8,128)(2,1)} %param.23) | copy-start | bytes 5505028
  7.2 45.0 %all-gather.3.cloned.1.call-start = ((), (), s32[]{:S(2)}) async-start(), calls=%async_computation.5 | async-start | bytes 2228224 | tf_op jit(solution)/shard_map/all_gather | solution.py:66
  54.4 2.8 copy-start.10
  57.2 3.9 copy-start.2
  57.2 3.9 copy-start.11
  67.1 7.4 %copy-start.9 = (s32[32]{0:T(128)S(1)}, s32[32]{0:T(128)}, u32[]{:S(2)}) copy-start(s32[32]{0:T(128)} %param.24) | copy-start | bytes 388
  67.1 131.6 %all-to-all-start = ((bf16[16,128,1824]{1,2,0:T(8,128)(2,1)}), bf16[16,128,1824]{1,2,0:T(8,128)(2,1)}, u32[]{:S(2)}, u32[]{:S(2)}) async-start(bf16[16,128,1824]{1,2,0:T(8,128)(2,1)} %copy_bitcast_fusion), calls=%async_computation | async-start | bytes 14942208 | tf_op jit(solution)/shard_map/all_to_all | solution.py:15
  74.5 158.3 %all-gather.5.cloned.1.call-start = ((), (), s32[]{:S(2)}) async-start(), calls=%async_computation.6 | async-start | bytes 2228224 | tf_op jit(solution)/shard_map/all_gather | solution.py:68
  77.3 125.8 %copy-start.8 = (bf16[2,16,896]{2,1,0:T(8,128)(2,1)}, bf16[2,16,896]{2,1,0:T(8,128)(2,1)S(1)}, u32[]{:S(2)}) copy-start(bf16[2,16,896]{2,1,0:T(8,128)(2,1)S(1)} %gather_fusion.2) | copy-start | bytes 172036
  79.4 126.0 %copy-start.7 = (bf16[2,16,896]{2,1,0:T(8,128)(2,1)}, bf16[2,16,896]{2,1,0:T(8,128)(2,1)S(1)}, u32[]{:S(2)}) copy-start(bf16[2,16,896]{2,1,0:T(8,128)(2,1)S(1)} %gather_fusion.3) | copy-start | bytes 172036
  202.9 10.9 %copy-start.4 = (f32[128,1824]{0,1:T(8,128)}, f32[128,1824]{0,1:T(8,128)S(1)}, u32[]{:S(2)}) copy-start(f32[128,1824]{0,1:T(8,128)S(1)} %convert_reduce_fusion) | copy-start | bytes 2801668
  213.9 64.8 %all-to-all-start.1 = ((bf16[16,128,896]{2,1,0:T(8,128)(2,1)}), bf16[16,128,896]{2,1,0:T(8,128)(2,1)}, u32[]{:S(2)}, u32[]{:S(2)}) async-start(bf16[16,128,896]{2,1,0:T(8,128)(2,1)} %broadcast_in_dim.18), calls=%async_computation.1 | async-start | bytes 7340032 | tf_op jit(solution)/shard_map/all_to_all | solution.py:24
  283.2 49.6 %all-to-all-start.2 = ((bf16[16,128,912]{1,2,0:T(8,128)(2,1)}), bf16[16,128,912]{1,2,0:T(8,128)(2,1)}, u32[]{:S(2)}, u32[]{:S(2)}) async-start(bf16[16,128,912]{1,2,0:T(8,128)(2,1)} %copy_bitcast_fusion.1), calls=%async_computation.2 | async-start | bytes 7471104 | tf_op jit(solution)/shard_map/all_to_all | solution.py:15
  300.6 38.8 %copy-start.5 = (f32[128,1824]{0,1:T(8,128)S(1)}, f32[128,1824]{0,1:T(8,128)}, u32[]{:S(2)}) copy-start(f32[128,1824]{0,1:T(8,128)} %copy-done.4) | copy-start | bytes 2801668
  335.4 0.8 copy-start.6
  348.4 57.9 %all-to-all-start.3 = ((bf16[16,128,560]{1,2,0:T(8,128)(2,1)}), bf16[16,128,560]{1,2,0:T(8,128)(2,1)}, u32[]{:S(2)}, u32[]{:S(2)}) async-start(bf16[16,128,560]{1,2,0:T(8,128)(2,1)} %pad_maximum_fusion.1), calls=%async_computation.3 | async-start | bytes 4587520 | tf_op jit(solution)/shard_map/all_to_all | solution.py:15
  408.3 9.7 %copy-start.1 = (s32[64]{0:T(128)S(1)}, s32[64]{0:T(128)}, u32[]{:S(2)}) copy-start(s32[64]{0:T(128)} %param.25) | copy-start | bytes 772
  410.1 36.8 %all-to-all-start.4 = ((bf16[16,72,896]{2,1,0:T(8,128)(2,1)}), bf16[16,72,896]{2,1,0:T(8,128)(2,1)}, u32[]{:S(2)}, u32[]{:S(2)}) async-start(bf16[16,72,896]{2,1,0:T(8,128)(2,1)} %broadcast_in_dim.22), calls=%async_computation.4 | async-start | bytes 4128768 | tf_op jit(solution)/shard_map/all_to_all | solution.py:24
  455.0 3.6 copy-start.3
Sparse Core Ops, SparseCore 0:
  9.8 42.3 all-gather.2
  77.1 37.7 all-gather.4

commit v9 on v6

--- a/solution.py
+++ b/solution.py
@@ -186,7 +186,7 @@
         ).reshape(rows_in, feat_here)
     ).astype(jnp.bfloat16)
 
-    all_down_rank = lax.all_gather(down_rank_flat, "tensor", axis=0, tiled=True)
+    all_down_rank = gather_rows(down_rank_flat, "tensor")
     rank_weighted = (token_onehot[:, :, None] * all_down_rank[:, None, :]).reshape(
         every_token_row, tenants_here * rank_width
     )

time: 463 us -> 477 us (1.030)
  waiting for transfers between devices: 291 us -> 315 us
  blocking collectives: 15.9 us -> 0 us
  starting transfers between devices: 43.2 us -> 48.1 us
    all_to_all x2 -> x3, waiting for transfers between devices: 45.6 us -> 70.2 us  [gather_rows(): lax.all_to_all(jnp.broadcast_to(x[None], (count,) + x.shape), axis, 0, 0,...]
    all_gather x1 -> x0, blocking collectives: 15.9 us -> none  [shards(): all_down_rank = lax.all_gather(down_rank_flat, 'tensor', axis=0, tiled=True)]
    all_to_all x2 -> x3, starting transfers between devices: 14.3 us -> 18.9 us  [gather_rows(): lax.all_to_all(jnp.broadcast_to(x[None], (count,) + x.shape), axis, 0, 0,...]
  transfers between devices with their start and end apart: 7 -> 8, of which waited for: 7 -> 8; matrix products, arithmetic and copies ran while one was open for 8% -> 7% of each run, Pallas kernels for 0% -> 0%
where the time goes in v9:
time: 477 us; the launch traced here: 475 us
  waiting for transfers between devices  315 us (66%)
  starting transfers between devices  48.1 us (10%)
  matrix products  38.2 us (8%)
  local copies, waits for them, and re-layouts  37.3 us (8%)
  other arithmetic  22.1 us (5%)
  between operations  14.6 us (3%)
    all_to_all x3, waiting for transfers between devices, exchange_pieces(): return lax.all_to_all(pieces, axis, 0, 0, tiled=False)  164 us
    all_to_all x3, waiting for transfers between devices, gather_rows(): lax.all_to_all(jnp.broadcast_to(x[None], (count,) + x.shape), axis, 0, 0,...  70.2 us
    all_gather x1, waiting for transfers between devices, shards(): all_inputs = lax.all_gather(tokens, 'tensor', axis=0, tiled=True)  40 us
    all_gather x1, waiting for transfers between devices, shards(): all_cot = lax.all_gather(cotangent, 'tensor', axis=0, tiled=True)  39.1 us
    all_to_all x3, starting transfers between devices, exchange_pieces(): return lax.all_to_all(pieces, axis, 0, 0, tiled=False)  29.1 us
    all_to_all x3, starting transfers between devices, gather_rows(): lax.all_to_all(jnp.broadcast_to(x[None], (count,) + x.shape), axis, 0, 0,...  18.9 us
  transfers between devices with their start and end apart: 8, of which 8 were waited for; matrix products, arithmetic and copies ran while one was open for 7% of the time, Pallas kernels for 0%

profile of v9, /device:TPU:8, one launch (start us, length us, event | category | flops | bytes accessed | tf_op | source)
XLA Modules:
  0.0 475.0 jit_solution(6537656613292415950)
XLA Ops:
  12.2 40.0 %all-gather.3.cloned.1.call-done = bf16[2048,512]{1,0:T(8,128)(2,1)} async-done(((bf16[128,512]{1,0:T(8,128)(2,1)}), bf16[2048,512]{1,0:T(8,128)(2,1)}) %all-gather.3.cloned.1.call-update) | async-done | bytes 2097168 | tf_op jit(solution)/shard_map/all_gather | solution.py:66
  52.2 2.2 fusion.3
  54.7 2.3 fusion.4
  57.2 3.9 convolution_convert_fusion.1
  61.1 2.2 convolution_convert_fusion.2
  63.3 3.9 copy_bitcast_fusion
  67.2 7.4 %all-to-all-start = ((bf16[16,128,1824]{1,2,0:T(8,128)(2,1)}), bf16[16,128,1824]{1,2,0:T(8,128)(2,1)}, u32[]{:S(2)}, u32[]{:S(2)}) async-start(bf16[16,128,1824]{1,2,0:T(8,128)(2,1)} %copy_bitcast_fusion), calls=%async_computation | async-start | bytes 14942208 | tf_op jit(solution)/shard_map/all_to_all | solution.py:15
  75.9 39.1 %all-gather.5.cloned.1.call-done = bf16[2048,512]{1,0:T(8,128)(2,1)} async-done(((bf16[128,512]{1,0:T(8,128)(2,1)}), bf16[2048,512]{1,0:T(8,128)(2,1)}) %all-gather.5.cloned.1.call-update) | async-done | bytes 2097168 | tf_op jit(solution)/shard_map/all_gather | solution.py:68
  115.0 2.2 fusion.2
  117.5 3.9 convolution_convert_fusion
  121.4 2.3 pad_maximum_fusion
  123.7 75.0 %all-to-all-done = bf16[16,128,1824]{1,2,0:T(8,128)(2,1)} async-done(((bf16[16,128,1824]{1,2,0:T(8,128)(2,1)}), bf16[16,128,1824]{1,2,0:T(8,128)(2,1)}, u32[]{:S(2)}, u32[]{:S(2)}) %all-to-all-start) | async-done | bytes 7471136 | tf_op jit(solution)/shard_map/all_to_all | solution.py:15
  198.8 4.6 copy_bitcast_fusion.1
  203.4 17.3 %all-to-all-start.2 = ((bf16[16,128,912]{1,2,0:T(8,128)(2,1)}), bf16[16,128,912]{1,2,0:T(8,128)(2,1)}, u32[]{:S(2)}, u32[]{:S(2)}) async-start(bf16[16,128,912]{1,2,0:T(8,128)(2,1)} %copy_bitcast_fusion.1), calls=%async_computation.2 | async-start | bytes 7471104 | tf_op jit(solution)/shard_map/all_to_all | solution.py:15
  223.4 2.1 gather_fusion.3
  225.5 4.2 convert_reduce_fusion
  232.5 36.6 %all-to-all-done.2 = bf16[16,128,912]{1,2,0:T(8,128)(2,1)} async-done(((bf16[16,128,912]{1,2,0:T(8,128)(2,1)}), bf16[16,128,912]{1,2,0:T(8,128)(2,1)}, u32[]{:S(2)}, u32[]{:S(2)}) %all-to-all-start.2) | async-done | bytes 3735584 | tf_op jit(solution)/shard_map/all_to_all | solution.py:15
  269.1 2.6 convert_reduce_fusion.1
  274.8 2.4 multiply_convert_fusion.1
  278.3 2.3 broadcast_in_dim.20
  280.7 6.4 %all-to-all-start.1 = ((bf16[16,128,896]{2,1,0:T(8,128)(2,1)}), bf16[16,128,896]{2,1,0:T(8,128)(2,1)}, u32[]{:S(2)}, u32[]{:S(2)}) async-start(bf16[16,128,896]{2,1,0:T(8,128)(2,1)} %broadcast_in_dim.20), calls=%async_computation.1 | async-start | bytes 7340032 | tf_op jit(solution)/shard_map/all_to_all | solution.py:24
  289.7 39.7 %all-to-all-done.1 = bf16[16,128,896]{2,1,0:T(8,128)(2,1)} async-done(((bf16[16,128,896]{2,1,0:T(8,128)(2,1)}), bf16[16,128,896]{2,1,0:T(8,128)(2,1)}, u32[]{:S(2)}, u32[]{:S(2)}) %all-to-all-start.1) | async-done | bytes 3670048 | tf_op jit(solution)/shard_map/all_to_all | solution.py:24
  329.4 6.0 %convolution_convert_fusion.3 = bf16[2048,512]{0,1:T(8,128)(2,1)} fusion(bf16[2048,896]{1,0:T(8,128)(2,1)} %bitcast.5, bf16[896,512]{1,0:T(8,128)(2,1)} %param.17), kind=kOutput, calls=%fused_computation.19 | convolution fusion | flops 1880096768 | bytes 6684672 | tf_op jit(solution)/shard_map/dot_general | solution.py:150
  335.4 3.2 convolution_convert_fusion.4
  342.4 4.4 all-to-all-start.3
  348.0 52.4 %all-to-all-done.3 = bf16[16,128,560]{1,2,0:T(8,128)(2,1)} async-done(((bf16[16,128,560]{1,2,0:T(8,128)(2,1)}), bf16[16,128,560]{1,2,0:T(8,128)(2,1)}, u32[]{:S(2)}, u32[]{:S(2)}) %all-to-all-start.3) | async-done | bytes 2293792 | tf_op jit(solution)/shard_map/all_to_all | solution.py:15
  403.0 4.6 all-to-all-start.5
  408.0 7.5 %all-to-all-done.5 = bf16[16,128,16]{1,2,0:T(8,128)(2,1)S(1)} async-done(((bf16[16,128,16]{1,2,0:T(8,128)(2,1)}), bf16[16,128,16]{1,2,0:T(8,128)(2,1)S(1)}, u32[]{:S(2)}, u32[]{:S(2)}) %all-to-all-start.5) | async-done | bytes 65568 | tf_op jit(solution)/shard_map/all_to_all | solution.py:24
  416.9 8.0 %all-to-all-start.4 = ((bf16[16,72,896]{2,1,0:T(8,128)(2,1)}), bf16[16,72,896]{2,1,0:T(8,128)(2,1)}, u32[]{:S(2)}, u32[]{:S(2)}) async-start(bf16[16,72,896]{2,1,0:T(8,128)(2,1)} %broadcast_in_dim.24), calls=%async_computation.4 | async-start | bytes 4128768 | tf_op jit(solution)/shard_map/all_to_all | solution.py:24
  428.4 2.7 fusion.5
  431.1 23.0 %all-to-all-done.4 = bf16[16,72,896]{2,1,0:T(8,128)(2,1)} async-done(((bf16[16,72,896]{2,1,0:T(8,128)(2,1)}), bf16[16,72,896]{2,1,0:T(8,128)(2,1)}, u32[]{:S(2)}, u32[]{:S(2)}) %all-to-all-start.4) | async-done | bytes 2064416 | tf_op jit(solution)/shard_map/all_to_all | solution.py:24
  462.3 3.5 convolution_bitcast_fusion
  (121 shorter events, 42.4 us)
Async XLA Ops:
  7.2 213.6 %copy-start = (bf16[64,896,16]{1,2,0:T(8,128)(2,1)S(1)}, bf16[64,896,16]{1,2,0:T(8,128)(2,1)}, u32[]{:S(2)}) copy-start(bf16[64,896,16]{1,2,0:T(8,128)(2,1)} %param.23) | copy-start | bytes 5505028
  7.2 45.0 %all-gather.3.cloned.1.call-start = ((), (), s32[]{:S(2)}) async-start(), calls=%async_computation.6 | async-start | bytes 2228224 | tf_op jit(solution)/shard_map/all_gather | solution.py:66
  54.4 2.8 copy-start.10
  57.2 3.9 copy-start.2
  57.2 3.9 copy-start.11
  67.2 8.1 %copy-start.8 = (bf16[64,16,512]{2,1,0:T(8,128)(2,1)S(1)}, bf16[64,16,512]{2,1,0:T(8,128)(2,1)}, u32[]{:S(2)}) copy-start(bf16[64,16,512]{2,1,0:T(8,128)(2,1)} %param.20) | copy-start | bytes 3145732
  67.2 131.6 %all-to-all-start = ((bf16[16,128,1824]{1,2,0:T(8,128)(2,1)}), bf16[16,128,1824]{1,2,0:T(8,128)(2,1)}, u32[]{:S(2)}, u32[]{:S(2)}) async-start(bf16[16,128,1824]{1,2,0:T(8,128)(2,1)} %copy_bitcast_fusion), calls=%async_computation | async-start | bytes 14942208 | tf_op jit(solution)/shard_map/all_to_all | solution.py:15
  74.6 40.5 %all-gather.5.cloned.1.call-start = ((), (), s32[]{:S(2)}) async-start(), calls=%async_computation.7 | async-start | bytes 2228224 | tf_op jit(solution)/shard_map/all_gather | solution.py:68
  203.4 17.3 %copy-start.9 = (s32[32]{0:T(128)S(1)}, s32[32]{0:T(128)}, u32[]{:S(2)}) copy-start(s32[32]{0:T(128)} %param.24) | copy-start | bytes 388
  203.4 65.7 %all-to-all-start.2 = ((bf16[16,128,912]{1,2,0:T(8,128)(2,1)}), bf16[16,128,912]{1,2,0:T(8,128)(2,1)}, u32[]{:S(2)}, u32[]{:S(2)}) async-start(bf16[16,128,912]{1,2,0:T(8,128)(2,1)} %copy_bitcast_fusion.1), calls=%async_computation.2 | async-start | bytes 7471104 | tf_op jit(solution)/shard_map/all_to_all | solution.py:15
  223.4 6.5 %copy-start.7 = (bf16[2,16,896]{2,1,0:T(8,128)(2,1)}, bf16[2,16,896]{2,1,0:T(8,128)(2,1)S(1)}, u32[]{:S(2)}) copy-start(bf16[2,16,896]{2,1,0:T(8,128)(2,1)S(1)} %gather_fusion.2) | copy-start | bytes 172036
  225.5 5.7 %copy-start.5 = (bf16[2,16,896]{2,1,0:T(8,128)(2,1)}, bf16[2,16,896]{2,1,0:T(8,128)(2,1)S(1)}, u32[]{:S(2)}) copy-start(bf16[2,16,896]{2,1,0:T(8,128)(2,1)S(1)} %gather_fusion.3) | copy-start | bytes 172036
  280.7 48.7 %all-to-all-start.1 = ((bf16[16,128,896]{2,1,0:T(8,128)(2,1)}), bf16[16,128,896]{2,1,0:T(8,128)(2,1)}, u32[]{:S(2)}, u32[]{:S(2)}) async-start(bf16[16,128,896]{2,1,0:T(8,128)(2,1)} %broadcast_in_dim.20), calls=%async_computation.1 | async-start | bytes 7340032 | tf_op jit(solution)/shard_map/all_to_all | solution.py:24
  287.0 0.9 copy-start.4
  287.0 2.4 copy-start.6
  340.9 6.0 %copy-start.1 = (s32[64]{0:T(128)S(1)}, s32[64]{0:T(128)}, u32[]{:S(2)}) copy-start(s32[64]{0:T(128)} %param.25) | copy-start | bytes 772
  342.4 57.9 %all-to-all-start.3 = ((bf16[16,128,560]{1,2,0:T(8,128)(2,1)}), bf16[16,128,560]{1,2,0:T(8,128)(2,1)}, u32[]{:S(2)}, u32[]{:S(2)}) async-start(bf16[16,128,560]{1,2,0:T(8,128)(2,1)} %pad_maximum_fusion.1), calls=%async_computation.3 | async-start | bytes 4587520 | tf_op jit(solution)/shard_map/all_to_all | solution.py:15
  403.0 12.4 %all-to-all-start.5 = ((bf16[16,128,16]{1,2,0:T(8,128)(2,1)}), bf16[16,128,16]{1,2,0:T(8,128)(2,1)S(1)}, u32[]{:S(2)}, u32[]{:S(2)}) async-start(bf16[16,128,16]{1,2,0:T(8,128)(2,1)} %broadcast_in_dim.25), calls=%async_computation.5 | async-start | bytes 131072 | tf_op jit(solution)/shard_map/all_to_all | solution.py:24
  416.9 37.2 %all-to-all-start.4 = ((bf16[16,72,896]{2,1,0:T(8,128)(2,1)}), bf16[16,72,896]{2,1,0:T(8,128)(2,1)}, u32[]{:S(2)}, u32[]{:S(2)}) async-start(bf16[16,72,896]{2,1,0:T(8,128)(2,1)} %broadcast_in_dim.24), calls=%async_computation.4 | async-start | bytes 4128768 | tf_op jit(solution)/shard_map/all_to_all | solution.py:24
  462.3 3.5 copy-start.3
Sparse Core Ops, SparseCore 0:
  9.8 42.3 all-gather.2
  77.2 37.7 all-gather.4

commit v10 on v8

--- a/solution.py
+++ b/solution.py
@@ -76,23 +76,22 @@
     up_rank_part = jnp.einsum(
         "btk,bkr->btr", input_blocks, up_in[tenants], preferred_element_type=jnp.float32
     ).reshape(every_token_row, rank_width)
-    forward_got = exchange_pieces(
+    gate_got = exchange_pieces(
         jnp.concatenate(
-            [
-                gate_part.astype(jnp.bfloat16),
-                up_part.astype(jnp.bfloat16),
-                gate_rank_part.astype(jnp.bfloat16),
-                up_rank_part.astype(jnp.bfloat16),
-            ],
-            axis=1,
+            [gate_part.astype(jnp.bfloat16), gate_rank_part.astype(jnp.bfloat16)], axis=1
         ),
         "dp",
     )
-    forward_sums = forward_got.astype(jnp.float32).sum(0)
-    gate_total_sum = forward_sums[:, :width_here]
-    up_total_sum = forward_sums[:, width_here : 2 * width_here]
-    gate_rank = forward_sums[:, 2 * width_here : 2 * width_here + rank_width]
-    up_rank = forward_sums[:, 2 * width_here + rank_width :]
+    up_got = exchange_pieces(
+        jnp.concatenate([up_part.astype(jnp.bfloat16), up_rank_part.astype(jnp.bfloat16)], axis=1),
+        "dp",
+    )
+    gate_sums = gate_got.astype(jnp.float32).sum(0)
+    up_sums = up_got.astype(jnp.float32).sum(0)
+    gate_total_sum = gate_sums[:, :width_here]
+    up_total_sum = up_sums[:, :width_here]
+    gate_rank = gate_sums[:, width_here:]
+    up_rank = up_sums[:, width_here:]
     gate_rank_second = gate_rank.astype(jnp.bfloat16).reshape(blocks_group, BLOCK, rank_width)
     up_rank_second = up_rank.astype(jnp.bfloat16).reshape(blocks_group, BLOCK, rank_width)
     gate_raise = gate_out[group_tenants]
@@ -118,7 +117,7 @@
     back_pieces = jnp.concatenate(
         [hidden_grad_part.astype(jnp.bfloat16), down_back_part.astype(jnp.bfloat16)], axis=1
     )
-    all_hidden, back_pieces = lax.optimization_barrier((all_hidden, back_pieces))
+    gate_got, up_got, back_pieces = lax.optimization_barrier((gate_got, up_got, back_pieces))
     back_sums = scatter_sum(back_pieces, "dp")
     hidden_grad_sum = back_sums[:, :width_here]
     group_down_back = back_sums[:, width_here:].astype(jnp.bfloat16)

time: 469 us -> 431 us (0.919)
  waiting for transfers between devices: 289 us -> 253 us
  local copies, waits for them, and re-layouts: 41.3 us -> 35.5 us
    all_to_all x3 -> x4, waiting for transfers between devices: 205 us -> 162 us  [exchange_pieces(): return lax.all_to_all(pieces, axis, 0, 0, tiled=False)]
    all_to_all x3 -> x4, starting transfers between devices: 18.1 us -> 32.3 us  [exchange_pieces(): return lax.all_to_all(pieces, axis, 0, 0, tiled=False)]
    all_to_all x2, starting transfers between devices: 25 us -> 14.5 us  [gather_rows(): lax.all_to_all(jnp.broadcast_to(x[None], (count,) + x.shape), axis, 0, 0,...]
  transfers between devices with their start and end apart: 7 -> 8, of which waited for: 6 -> 7; matrix products, arithmetic and copies ran while one was open for 11% -> 10% of each run, Pallas kernels for 0% -> 0%
where the time goes in v10:
time: 431 us; the launch traced here: 429 us
  waiting for transfers between devices  253 us (59%)
  starting transfers between devices  46.9 us (11%)
  matrix products  39.8 us (9%)
  local copies, waits for them, and re-layouts  35.5 us (8%)
  other arithmetic  23.7 us (5%)
  blocking collectives  16 us (4%)
  between operations  14.5 us (3%)
    all_to_all x4, waiting for transfers between devices, exchange_pieces(): return lax.all_to_all(pieces, axis, 0, 0, tiled=False)  162 us
    all_to_all x2, waiting for transfers between devices, gather_rows(): lax.all_to_all(jnp.broadcast_to(x[None], (count,) + x.shape), axis, 0, 0,...  47.7 us
    all_gather x1, waiting for transfers between devices, shards(): all_inputs = lax.all_gather(tokens, 'tensor', axis=0, tiled=True)  41.7 us
    all_to_all x4, starting transfers between devices, exchange_pieces(): return lax.all_to_all(pieces, axis, 0, 0, tiled=False)  32.3 us
    all_gather x1, blocking collectives, shards(): all_down_rank = lax.all_gather(down_rank_flat, 'tensor', axis=0, tiled=True)  16 us
    all_to_all x2, starting transfers between devices, gather_rows(): lax.all_to_all(jnp.broadcast_to(x[None], (count,) + x.shape), axis, 0, 0,...  14.5 us
  transfers between devices with their start and end apart: 8, of which 7 were waited for; matrix products, arithmetic and copies ran while one was open for 10% of the time, Pallas kernels for 0%

profile of v10, /device:TPU:8, one launch (start us, length us, event | category | flops | bytes accessed | tf_op | source)
XLA Modules:
  0.0 429.3 jit_solution(9791714073575079307)
XLA Ops:
  10.5 41.7 %all-gather.3.cloned.1.call-done = bf16[2048,512]{1,0:T(8,128)(2,1)} async-done(((bf16[128,512]{1,0:T(8,128)(2,1)}), bf16[2048,512]{1,0:T(8,128)(2,1)}) %all-gather.3.cloned.1.call-update) | async-done | bytes 2097168 | tf_op jit(solution)/shard_map/all_gather | solution.py:66
  52.2 2.2 fusion.3
  54.7 3.7 convolution_convert_fusion.2
  58.4 2.3 copy_bitcast_fusion.2
  60.7 7.4 %all-to-all-start = ((bf16[16,128,912]{1,2,0:T(8,128)(2,1)}), bf16[16,128,912]{1,2,0:T(8,128)(2,1)}, u32[]{:S(2)}, u32[]{:S(2)}) async-start(bf16[16,128,912]{1,2,0:T(8,128)(2,1)} %copy_bitcast_fusion.2), calls=%async_computation | async-start | bytes 7471104 | tf_op jit(solution)/shard_map/all_to_all | solution.py:15
  69.4 2.2 fusion.4
  71.9 3.9 convolution_convert_fusion.1
  78.0 39.6 %all-to-all-done = bf16[16,128,912]{1,2,0:T(8,128)(2,1)} async-done(((bf16[16,128,912]{1,2,0:T(8,128)(2,1)}), bf16[16,128,912]{1,2,0:T(8,128)(2,1)}, u32[]{:S(2)}, u32[]{:S(2)}) %all-to-all-start) | async-done | bytes 3735584 | tf_op jit(solution)/shard_map/all_to_all | solution.py:15
  117.6 14.0 %all-to-all-start.1 = ((bf16[16,128,912]{1,2,0:T(8,128)(2,1)}), bf16[16,128,912]{1,2,0:T(8,128)(2,1)}, u32[]{:S(2)}, u32[]{:S(2)}) async-start(bf16[16,128,912]{1,2,0:T(8,128)(2,1)} %copy_bitcast_fusion.1), calls=%async_computation.1 | async-start | bytes 7471104 | tf_op jit(solution)/shard_map/all_to_all | solution.py:15
  132.2 2.2 fusion.2
  134.7 3.9 convolution_convert_fusion
  138.6 2.4 pad_maximum_fusion
  141.0 39.0 %all-to-all-done.1 = bf16[16,128,912]{1,2,0:T(8,128)(2,1)} async-done(((bf16[16,128,912]{1,2,0:T(8,128)(2,1)}), bf16[16,128,912]{1,2,0:T(8,128)(2,1)}, u32[]{:S(2)}, u32[]{:S(2)}) %all-to-all-start.1) | async-done | bytes 3735584 | tf_op jit(solution)/shard_map/all_to_all | solution.py:15
  180.0 4.5 %copy_bitcast_fusion = bf16[16,128,912]{1,2,0:T(8,128)(2,1)} fusion(bf16[2048,912]{0,1:T(8,128)(2,1)} %pad_maximum_fusion), kind=kLoop, calls=%fused_computation.13 | loop fusion | bytes 7471104 | tf_op jit(solution)/shard_map/reshape | solution.py:14
  184.6 6.5 %all-to-all-start.3 = ((bf16[16,128,912]{1,2,0:T(8,128)(2,1)}), bf16[16,128,912]{1,2,0:T(8,128)(2,1)}, u32[]{:S(2)}, u32[]{:S(2)}) async-start(bf16[16,128,912]{1,2,0:T(8,128)(2,1)} %copy_bitcast_fusion), calls=%async_computation.3 | async-start | bytes 7471104 | tf_op jit(solution)/shard_map/all_to_all | solution.py:15
  195.9 2.6 convert_reduce_fusion.1
  199.9 2.6 convert_reduce_fusion.2
  203.9 30.5 %all-to-all-done.3 = bf16[16,128,912]{1,2,0:T(8,128)(2,1)} async-done(((bf16[16,128,912]{1,2,0:T(8,128)(2,1)}), bf16[16,128,912]{1,2,0:T(8,128)(2,1)}, u32[]{:S(2)}, u32[]{:S(2)}) %all-to-all-start.3) | async-done | bytes 3735584 | tf_op jit(solution)/shard_map/all_to_all | solution.py:15
  234.3 2.6 convert_reduce_fusion
  240.2 2.4 multiply_convert_fusion.2
  243.6 2.4 broadcast_in_dim.18
  246.0 7.9 %all-to-all-start.2 = ((bf16[16,128,896]{2,1,0:T(8,128)(2,1)}), bf16[16,128,896]{2,1,0:T(8,128)(2,1)}, u32[]{:S(2)}, u32[]{:S(2)}) async-start(bf16[16,128,896]{2,1,0:T(8,128)(2,1)} %broadcast_in_dim.18), calls=%async_computation.2 | async-start | bytes 7340032 | tf_op jit(solution)/shard_map/all_to_all | solution.py:24
  256.5 41.7 %all-to-all-done.2 = bf16[16,128,896]{2,1,0:T(8,128)(2,1)} async-done(((bf16[16,128,896]{2,1,0:T(8,128)(2,1)}), bf16[16,128,896]{2,1,0:T(8,128)(2,1)}, u32[]{:S(2)}, u32[]{:S(2)}) %all-to-all-start.2) | async-done | bytes 3670048 | tf_op jit(solution)/shard_map/all_to_all | solution.py:24
  298.2 6.0 %convolution_convert_fusion.3 = bf16[2048,512]{0,1:T(8,128)(2,1)} fusion(bf16[2048,896]{1,0:T(8,128)(2,1)} %bitcast.5, bf16[896,512]{1,0:T(8,128)(2,1)} %param.17), kind=kOutput, calls=%fused_computation.22 | convolution fusion | flops 1880096768 | bytes 6684672 | tf_op jit(solution)/shard_map/dot_general | solution.py:149
  304.2 3.2 convolution_convert_fusion.4
  311.2 4.5 %all-to-all-start.4 = ((bf16[16,128,560]{1,2,0:T(8,128)(2,1)}), bf16[16,128,560]{1,2,0:T(8,128)(2,1)}, u32[]{:S(2)}, u32[]{:S(2)}) async-start(bf16[16,128,560]{1,2,0:T(8,128)(2,1)} %pad_maximum_fusion.1), calls=%async_computation.4 | async-start | bytes 4587520 | tf_op jit(solution)/shard_map/all_to_all | solution.py:15
  316.0 53.1 %all-to-all-done.4 = bf16[16,128,560]{1,2,0:T(8,128)(2,1)} async-done(((bf16[16,128,560]{1,2,0:T(8,128)(2,1)}), bf16[16,128,560]{1,2,0:T(8,128)(2,1)}, u32[]{:S(2)}, u32[]{:S(2)}) %all-to-all-start.4) | async-done | bytes 2293792 | tf_op jit(solution)/shard_map/all_to_all | solution.py:15
  372.9 6.6 %all-to-all-start.5 = ((bf16[16,72,896]{2,1,0:T(8,128)(2,1)}), bf16[16,72,896]{2,1,0:T(8,128)(2,1)}, u32[]{:S(2)}, u32[]{:S(2)}) async-start(bf16[16,72,896]{2,1,0:T(8,128)(2,1)} %broadcast_in_dim.22), calls=%async_computation.5 | async-start | bytes 4128768 | tf_op jit(solution)/shard_map/all_to_all | solution.py:24
  383.8 16.0 %all_gather.11 = bf16[2048,16]{0,1:T(8,128)(2,1)S(1)} all-gather(bf16[128,16]{0,1:T(8,128)(2,1)S(1)} %slice.104), channel_id=1, replica_groups=mesh['dp'=16,'tensor'=16] {'tensor'}, dimensions={0}, use_global_device_ids=true | all-gather | bytes 69632 | tf_op jit(solution)/shard_map/all_gather | solution.py:188
  399.8 2.7 fusion.5
  402.5 6.0 %all-to-all-done.5 = bf16[16,72,896]{2,1,0:T(8,128)(2,1)} async-done(((bf16[16,72,896]{2,1,0:T(8,128)(2,1)}), bf16[16,72,896]{2,1,0:T(8,128)(2,1)}, u32[]{:S(2)}, u32[]{:S(2)}) %all-to-all-start.5) | async-done | bytes 2064416 | tf_op jit(solution)/shard_map/all_to_all | solution.py:24
  416.7 3.5 convolution_bitcast_fusion
  (120 shorter events, 44.9 us)
Async XLA Ops:
  7.2 184.0 %copy-start = (bf16[64,896,16]{1,2,0:T(8,128)(2,1)S(1)}, bf16[64,896,16]{1,2,0:T(8,128)(2,1)}, u32[]{:S(2)}) copy-start(bf16[64,896,16]{1,2,0:T(8,128)(2,1)} %param.23) | copy-start | bytes 5505028
  7.2 45.0 %all-gather.3.cloned.1.call-start = ((), (), s32[]{:S(2)}) async-start(), calls=%async_computation.6 | async-start | bytes 2228224 | tf_op jit(solution)/shard_map/all_gather | solution.py:66
  8.6 46.1 %copy-start.10 = (bf16[512,896]{1,0:T(8,128)(2,1)S(1)}, bf16[512,896]{1,0:T(8,128)(2,1)}, u32[]{:S(2)}) copy-start(bf16[512,896]{1,0:T(8,128)(2,1)} %param.15) | copy-start | bytes 2752516
  60.7 8.1 %copy-start.3 = (bf16[64,512,16]{1,2,0:T(8,128)(2,1)S(1)}, bf16[64,512,16]{1,2,0:T(8,128)(2,1)}, u32[]{:S(2)}) copy-start(bf16[64,512,16]{1,2,0:T(8,128)(2,1)} %param.19) | copy-start | bytes 3145732
  60.7 56.9 %all-to-all-start = ((bf16[16,128,912]{1,2,0:T(8,128)(2,1)}), bf16[16,128,912]{1,2,0:T(8,128)(2,1)}, u32[]{:S(2)}, u32[]{:S(2)}) async-start(bf16[16,128,912]{1,2,0:T(8,128)(2,1)} %copy_bitcast_fusion.2), calls=%async_computation | async-start | bytes 7471104 | tf_op jit(solution)/shard_map/all_to_all | solution.py:15
  68.1 64.1 %all-gather.5.cloned.1.call-start = ((), (), s32[]{:S(2)}) async-start(), calls=%async_computation.7 | async-start | bytes 2228224 | tf_op jit(solution)/shard_map/all_gather | solution.py:68
  78.0 53.6 %copy-start.8 = (bf16[64,16,512]{2,1,0:T(8,128)(2,1)S(1)}, bf16[64,16,512]{2,1,0:T(8,128)(2,1)}, u32[]{:S(2)}) copy-start(bf16[64,16,512]{2,1,0:T(8,128)(2,1)} %param.20) | copy-start | bytes 3145732
  117.6 62.4 %all-to-all-start.1 = ((bf16[16,128,912]{1,2,0:T(8,128)(2,1)}), bf16[16,128,912]{1,2,0:T(8,128)(2,1)}, u32[]{:S(2)}, u32[]{:S(2)}) async-start(bf16[16,128,912]{1,2,0:T(8,128)(2,1)} %copy_bitcast_fusion.1), calls=%async_computation.1 | async-start | bytes 7471104 | tf_op jit(solution)/shard_map/all_to_all | solution.py:15
  184.6 6.5 %copy-start.9 = (s32[32]{0:T(128)S(1)}, s32[32]{0:T(128)}, u32[]{:S(2)}) copy-start(s32[32]{0:T(128)} %param.24) | copy-start | bytes 388
  184.6 49.8 %all-to-all-start.3 = ((bf16[16,128,912]{1,2,0:T(8,128)(2,1)}), bf16[16,128,912]{1,2,0:T(8,128)(2,1)}, u32[]{:S(2)}, u32[]{:S(2)}) async-start(bf16[16,128,912]{1,2,0:T(8,128)(2,1)} %copy_bitcast_fusion), calls=%async_computation.3 | async-start | bytes 7471104 | tf_op jit(solution)/shard_map/all_to_all | solution.py:15
  193.8 5.1 %copy-start.5 = (bf16[2,16,896]{2,1,0:T(8,128)(2,1)}, bf16[2,16,896]{2,1,0:T(8,128)(2,1)S(1)}, u32[]{:S(2)}) copy-start(bf16[2,16,896]{2,1,0:T(8,128)(2,1)S(1)} %gather_fusion.3) | copy-start | bytes 172036
  195.9 6.7 %copy-start.7 = (bf16[2,16,896]{2,1,0:T(8,128)(2,1)}, bf16[2,16,896]{2,1,0:T(8,128)(2,1)S(1)}, u32[]{:S(2)}) copy-start(bf16[2,16,896]{2,1,0:T(8,128)(2,1)S(1)} %gather_fusion.1) | copy-start | bytes 172036
  246.0 52.2 %all-to-all-start.2 = ((bf16[16,128,896]{2,1,0:T(8,128)(2,1)}), bf16[16,128,896]{2,1,0:T(8,128)(2,1)}, u32[]{:S(2)}, u32[]{:S(2)}) async-start(bf16[16,128,896]{2,1,0:T(8,128)(2,1)} %broadcast_in_dim.18), calls=%async_computation.2 | async-start | bytes 7340032 | tf_op jit(solution)/shard_map/all_to_all | solution.py:24
  253.8 0.9 copy-start.4
  253.8 2.4 copy-start.6
  311.2 57.9 %all-to-all-start.4 = ((bf16[16,128,560]{1,2,0:T(8,128)(2,1)}), bf16[16,128,560]{1,2,0:T(8,128)(2,1)}, u32[]{:S(2)}, u32[]{:S(2)}) async-start(bf16[16,128,560]{1,2,0:T(8,128)(2,1)} %pad_maximum_fusion.1), calls=%async_computation.4 | async-start | bytes 4587520 | tf_op jit(solution)/shard_map/all_to_all | solution.py:15
  371.1 8.5 %copy-start.1 = (s32[64]{0:T(128)S(1)}, s32[64]{0:T(128)}, u32[]{:S(2)}) copy-start(s32[64]{0:T(128)} %param.25) | copy-start | bytes 772
  372.9 35.6 %all-to-all-start.5 = ((bf16[16,72,896]{2,1,0:T(8,128)(2,1)}), bf16[16,72,896]{2,1,0:T(8,128)(2,1)}, u32[]{:S(2)}, u32[]{:S(2)}) async-start(bf16[16,72,896]{2,1,0:T(8,128)(2,1)} %broadcast_in_dim.22), calls=%async_computation.5 | async-start | bytes 4128768 | tf_op jit(solution)/shard_map/all_to_all | solution.py:24
  416.7 3.5 copy-start.2
Sparse Core Ops, SparseCore 0:
  9.8 42.3 all-gather.2
  70.7 37.7 all-gather.4

commit v11 on v10

--- a/solution.py
+++ b/solution.py
@@ -76,16 +76,23 @@
     up_rank_part = jnp.einsum(
         "btk,bkr->btr", input_blocks, up_in[tenants], preferred_element_type=jnp.float32
     ).reshape(every_token_row, rank_width)
+    cut = width_here // 7 * 4
+    gate_head = exchange_pieces(gate_part[:, :cut], "dp")
     gate_got = exchange_pieces(
         jnp.concatenate(
-            [gate_part.astype(jnp.bfloat16), gate_rank_part.astype(jnp.bfloat16)], axis=1
+            [gate_part[:, cut:].astype(jnp.bfloat16), gate_rank_part.astype(jnp.bfloat16)], axis=1
         ),
         "dp",
     )
+    up_head = exchange_pieces(up_part[:, :cut], "dp")
     up_got = exchange_pieces(
-        jnp.concatenate([up_part.astype(jnp.bfloat16), up_rank_part.astype(jnp.bfloat16)], axis=1),
+        jnp.concatenate(
+            [up_part[:, cut:].astype(jnp.bfloat16), up_rank_part.astype(jnp.bfloat16)], axis=1
+        ),
         "dp",
     )
+    gate_got = jnp.concatenate([gate_head, gate_got], axis=2)
+    up_got = jnp.concatenate([up_head, up_got], axis=2)
     gate_sums = gate_got.astype(jnp.float32).sum(0)
     up_sums = up_got.astype(jnp.float32).sum(0)
     gate_total_sum = gate_sums[:, :width_here]

time: 431 us -> 426 us (0.988)
  waiting for transfers between devices: 253 us -> 230 us
  local copies, waits for them, and re-layouts: 35.5 us -> 56.9 us
  other arithmetic: 23.7 us -> 19.1 us
    all_to_all x4 -> x6, waiting for transfers between devices: 162 us -> 139 us  [exchange_pieces(): return lax.all_to_all(pieces, axis, 0, 0, tiled=False)]
    slice x0 -> x5, local copies, waits for them, and re-layouts: none -> 7.25 us  [the longest x1 3.08 us: shards(): gate_head = exchange_pieces(gate_part[:, :cut], 'dp')]
    all_to_all x0 -> x2, local copies, waits for them, and re-layouts: none -> 6.66 us  [exchange_pieces(): return lax.all_to_all(pieces, axis, 0, 0, tiled=False)]
    reshape x1 -> x3, local copies, waits for them, and re-layouts: 4.54 us -> 10.2 us  [exchange_pieces(): x.astype(jnp.bfloat16).reshape((count, x.shape[0] // count) + x.shape[1:])]
    reshape x2 -> x0, other arithmetic: 4.49 us -> none  [exchange_pieces(): x.astype(jnp.bfloat16).reshape((count, x.shape[0] // count) + x.shape[1:])]
    all_to_all x4 -> x6, starting transfers between devices: 32.3 us -> 34.7 us  [exchange_pieces(): return lax.all_to_all(pieces, axis, 0, 0, tiled=False)]
  transfers between devices with their start and end apart: 8 -> 10, of which waited for: 7 -> 9; matrix products, arithmetic and copies ran while one was open for 10% -> 15% of each run, Pallas kernels for 0% -> 0%
where the time goes in v11:
time: 426 us; the launch traced here: 425 us
  waiting for transfers between devices  230 us (54%)
  local copies, waits for them, and re-layouts  56.9 us (13%)
  starting transfers between devices  48.9 us (11%)
  matrix products  39 us (9%)
  other arithmetic  19.1 us (4%)
  blocking collectives  16 us (4%)
  between operations  14.6 us (3%)
    all_to_all x6, waiting for transfers between devices, exchange_pieces(): return lax.all_to_all(pieces, axis, 0, 0, tiled=False)  139 us
    all_to_all x2, waiting for transfers between devices, gather_rows(): lax.all_to_all(jnp.broadcast_to(x[None], (count,) + x.shape), axis, 0, 0,...  47.6 us
    all_gather x1, waiting for transfers between devices, shards(): all_inputs = lax.all_gather(tokens, 'tensor', axis=0, tiled=True)  41.8 us
    all_to_all x6, starting transfers between devices, exchange_pieces(): return lax.all_to_all(pieces, axis, 0, 0, tiled=False)  34.7 us
    all_gather x1, blocking collectives, shards(): all_down_rank = lax.all_gather(down_rank_flat, 'tensor', axis=0, tiled=True)  16 us
    all_to_all x2, starting transfers between devices, gather_rows(): lax.all_to_all(jnp.broadcast_to(x[None], (count,) + x.shape), axis, 0, 0,...  14.2 us
    reshape x3, local copies, waits for them, and re-layouts, exchange_pieces(): x.astype(jnp.bfloat16).reshape((count, x.shape[0] // count) + x.shape[1:])  10.2 us
  transfers between devices with their start and end apart: 10, of which 9 were waited for; matrix products, arithmetic and copies ran while one was open for 15% of the time, Pallas kernels for 0%

profile of v11, /device:TPU:8, one launch (start us, length us, event | category | flops | bytes accessed | tf_op | source)
XLA Modules:
  0.0 424.6 jit_solution(12329702501113977799)
XLA Ops:
  10.4 41.8 %all-gather.3.cloned.1.call-done = bf16[2048,512]{1,0:T(8,128)(2,1)} async-done(((bf16[128,512]{1,0:T(8,128)(2,1)}), bf16[2048,512]{1,0:T(8,128)(2,1)}) %all-gather.3.cloned.1.call-update) | async-done | bytes 2097168 | tf_op jit(solution)/shard_map/all_gather | solution.py:66
  54.7 3.9 convolution_convert_fusion.1
  61.2 3.9 copy.134
  65.0 7.4 %all-to-all-start.3 = ((bf16[16,128,400]{1,2,0:T(8,128)(2,1)}), bf16[16,128,400]{1,2,0:T(8,128)(2,1)}, u32[]{:S(2)}, u32[]{:S(2)}) async-start(bf16[16,128,400]{1,2,0:T(8,128)(2,1)} %copy.134), calls=%async_computation.3 | async-start | bytes 3276800 | tf_op jit(solution)/shard_map/all_to_all | solution.py:15
  75.5 4.2 convolution_convert_fusion.2
  82.2 3.9 copy.129
  86.1 10.4 %all-to-all-done.3 = bf16[16,128,400]{1,2,0:T(8,128)(2,1)} async-done(((bf16[16,128,400]{1,2,0:T(8,128)(2,1)}), bf16[16,128,400]{1,2,0:T(8,128)(2,1)}, u32[]{:S(2)}, u32[]{:S(2)}) %all-to-all-start.3) | async-done | bytes 1638432 | tf_op jit(solution)/shard_map/all_to_all | solution.py:15
  96.5 5.0 %all-to-all-start.1 = ((bf16[16,128,400]{1,2,0:T(8,128)(2,1)}), bf16[16,128,400]{1,2,0:T(8,128)(2,1)S(1)}, u32[]{:S(2)}, u32[]{:S(2)}) async-start(bf16[16,128,400]{1,2,0:T(8,128)(2,1)} %copy.129), calls=%async_computation.1 | async-start | bytes 3276800 | tf_op jit(solution)/shard_map/all_to_all | solution.py:15
  102.2 3.1 slice.121
  105.3 17.9 %all-to-all-done.1 = bf16[16,128,400]{1,2,0:T(8,128)(2,1)S(1)} async-done(((bf16[16,128,400]{1,2,0:T(8,128)(2,1)}), bf16[16,128,400]{1,2,0:T(8,128)(2,1)S(1)}, u32[]{:S(2)}, u32[]{:S(2)}) %all-to-all-start.1) | async-done | bytes 1638432 | tf_op jit(solution)/shard_map/all_to_all | solution.py:15
  123.2 5.6 %all-to-all-start.2 = ((bf16[16,128,512]{2,1,0:T(8,128)(2,1)}), bf16[16,128,512]{2,1,0:T(8,128)(2,1)}, u32[]{:S(2)}, u32[]{:S(2)}) async-start(bf16[16,128,512]{2,1,0:T(8,128)(2,1)} %bitcast.158), calls=%async_computation.2 | async-start | bytes 4194304 | tf_op jit(solution)/shard_map/all_to_all | solution.py:15
  128.8 3.1 slice.117
  131.9 22.7 %all-to-all-done.2 = bf16[16,128,512]{2,1,0:T(8,128)(2,1)} async-done(((bf16[16,128,512]{2,1,0:T(8,128)(2,1)}), bf16[16,128,512]{2,1,0:T(8,128)(2,1)}, u32[]{:S(2)}, u32[]{:S(2)}) %all-to-all-start.2) | async-done | bytes 2097184 | tf_op jit(solution)/shard_map/all_to_all | solution.py:15
  154.6 6.3 %all-to-all-start = ((bf16[16,128,512]{2,1,0:T(8,128)(2,1)}), bf16[16,128,512]{2,1,0:T(8,128)(2,1)}, u32[]{:S(2)}, u32[]{:S(2)}) async-start(bf16[16,128,512]{2,1,0:T(8,128)(2,1)} %bitcast.157), calls=%async_computation | async-start | bytes 4194304 | tf_op jit(solution)/shard_map/all_to_all | solution.py:15
  167.6 3.9 convolution_convert_fusion
  174.5 10.3 %all-to-all-done = bf16[16,128,512]{2,1,0:T(8,128)(2,1)} async-done(((bf16[16,128,512]{2,1,0:T(8,128)(2,1)}), bf16[16,128,512]{2,1,0:T(8,128)(2,1)}, u32[]{:S(2)}, u32[]{:S(2)}) %all-to-all-start) | async-done | bytes 2097184 | tf_op jit(solution)/shard_map/all_to_all | solution.py:15
  184.8 5.8 %all-to-all-start.5 = ((bf16[16,128,912]{1,2,0:T(8,128)(2,1)}), bf16[16,128,912]{1,2,0:T(8,128)(2,1)}, u32[]{:S(2)}, u32[]{:S(2)}) async-start(bf16[16,128,912]{1,2,0:T(8,128)(2,1)} %copy_bitcast_fusion), calls=%async_computation.5 | async-start | bytes 7471104 | tf_op jit(solution)/shard_map/all_to_all | solution.py:15
  196.7 3.7 copy.135
  200.4 2.9 copy.130
  203.3 3.2 convert_reduce_fusion
  210.9 25.0 %all-to-all-done.5 = bf16[16,128,912]{1,2,0:T(8,128)(2,1)} async-done(((bf16[16,128,912]{1,2,0:T(8,128)(2,1)}), bf16[16,128,912]{1,2,0:T(8,128)(2,1)}, u32[]{:S(2)}, u32[]{:S(2)}) %all-to-all-start.5) | async-done | bytes 3735584 | tf_op jit(solution)/shard_map/all_to_all | solution.py:15
  245.8 6.3 %all-to-all-start.4 = ((bf16[16,128,896]{2,1,0:T(8,128)(2,1)}), bf16[16,128,896]{2,1,0:T(8,128)(2,1)}, u32[]{:S(2)}, u32[]{:S(2)}) async-start(bf16[16,128,896]{2,1,0:T(8,128)(2,1)} %broadcast_in_dim.18), calls=%async_computation.4 | async-start | bytes 7340032 | tf_op jit(solution)/shard_map/all_to_all | solution.py:24
  253.3 41.6 %all-to-all-done.4 = bf16[16,128,896]{2,1,0:T(8,128)(2,1)} async-done(((bf16[16,128,896]{2,1,0:T(8,128)(2,1)}), bf16[16,128,896]{2,1,0:T(8,128)(2,1)}, u32[]{:S(2)}, u32[]{:S(2)}) %all-to-all-start.4) | async-done | bytes 3670048 | tf_op jit(solution)/shard_map/all_to_all | solution.py:24
  294.9 3.2 convolution_convert_fusion.4
  298.4 4.7 %convolution_convert_fusion.3 = bf16[2048,512]{0,1:T(8,128)(2,1)S(1)} fusion(bf16[2048,896]{1,0:T(8,128)(2,1)} %bitcast.13, bf16[896,512]{1,0:T(8,128)(2,1)} %param.17), kind=kOutput, calls=%fused_computation.20 | convolution fusion | flops 1880096768 | bytes 6684672 | tf_op jit(solution)/shard_map/dot_general | solution.py:156
  305.1 4.6 %all-to-all-start.6 = ((bf16[16,128,560]{1,2,0:T(8,128)(2,1)}), bf16[16,128,560]{1,2,0:T(8,128)(2,1)}, u32[]{:S(2)}, u32[]{:S(2)}) async-start(bf16[16,128,560]{1,2,0:T(8,128)(2,1)} %pad_maximum_fusion.3), calls=%async_computation.6 | async-start | bytes 4587520 | tf_op jit(solution)/shard_map/all_to_all | solution.py:15
  310.1 53.0 %all-to-all-done.6 = bf16[16,128,560]{1,2,0:T(8,128)(2,1)} async-done(((bf16[16,128,560]{1,2,0:T(8,128)(2,1)}), bf16[16,128,560]{1,2,0:T(8,128)(2,1)}, u32[]{:S(2)}, u32[]{:S(2)}) %all-to-all-start.6) | async-done | bytes 2293792 | tf_op jit(solution)/shard_map/all_to_all | solution.py:15
  366.9 7.9 %all-to-all-start.7 = ((bf16[16,72,896]{2,1,0:T(8,128)(2,1)}), bf16[16,72,896]{2,1,0:T(8,128)(2,1)}, u32[]{:S(2)}, u32[]{:S(2)}) async-start(bf16[16,72,896]{2,1,0:T(8,128)(2,1)} %broadcast_in_dim.22), calls=%async_computation.7 | async-start | bytes 4128768 | tf_op jit(solution)/shard_map/all_to_all | solution.py:24
  379.1 16.0 %all_gather.11 = bf16[2048,16]{0,1:T(8,128)(2,1)S(1)} all-gather(bf16[128,16]{0,1:T(8,128)(2,1)S(1)} %slice.128), channel_id=1, replica_groups=mesh['dp'=16,'tensor'=16] {'tensor'}, dimensions={0}, use_global_device_ids=true | all-gather | bytes 69632 | tf_op jit(solution)/shard_map/all_gather | solution.py:195
  395.0 2.7 fusion.5
  397.8 6.0 %all-to-all-done.7 = bf16[16,72,896]{2,1,0:T(8,128)(2,1)} async-done(((bf16[16,72,896]{2,1,0:T(8,128)(2,1)}), bf16[16,72,896]{2,1,0:T(8,128)(2,1)}, u32[]{:S(2)}, u32[]{:S(2)}) %all-to-all-start.7) | async-done | bytes 2064416 | tf_op jit(solution)/shard_map/all_to_all | solution.py:24
  411.9 3.5 convolution_bitcast_fusion
  (134 shorter events, 66.6 us)
Async XLA Ops:
  7.2 188.9 %copy-start = (bf16[64,896,16]{1,2,0:T(8,128)(2,1)S(1)}, bf16[64,896,16]{1,2,0:T(8,128)(2,1)}, u32[]{:S(2)}) copy-start(bf16[64,896,16]{1,2,0:T(8,128)(2,1)} %param.23) | copy-start | bytes 5505028
  7.2 45.0 %all-gather.3.cloned.1.call-start = ((), (), s32[]{:S(2)}) async-start(), calls=%async_computation.8 | async-start | bytes 2228224 | tf_op jit(solution)/shard_map/all_gather | solution.py:66
  10.4 44.3 %copy-start.15 = (bf16[512,896]{1,0:T(8,128)(2,1)S(1)}, bf16[512,896]{1,0:T(8,128)(2,1)}, u32[]{:S(2)}) copy-start(bf16[512,896]{1,0:T(8,128)(2,1)} %param.16) | copy-start | bytes 2752516
  58.7 2.5 copy-start.5
  65.0 7.4 %copy-start.3 = (bf16[64,512,16]{1,2,0:T(8,128)(2,1)S(1)}, bf16[64,512,16]{1,2,0:T(8,128)(2,1)}, u32[]{:S(2)}) copy-start(bf16[64,512,16]{1,2,0:T(8,128)(2,1)} %param.18) | copy-start | bytes 3145732
  65.0 31.5 %all-to-all-start.3 = ((bf16[16,128,400]{1,2,0:T(8,128)(2,1)}), bf16[16,128,400]{1,2,0:T(8,128)(2,1)}, u32[]{:S(2)}, u32[]{:S(2)}) async-start(bf16[16,128,400]{1,2,0:T(8,128)(2,1)} %copy.134), calls=%async_computation.3 | async-start | bytes 3276800 | tf_op jit(solution)/shard_map/all_to_all | solution.py:15
  79.7 2.5 copy-start.6
  96.5 26.8 %all-to-all-start.1 = ((bf16[16,128,400]{1,2,0:T(8,128)(2,1)}), bf16[16,128,400]{1,2,0:T(8,128)(2,1)S(1)}, u32[]{:S(2)}, u32[]{:S(2)}) async-start(bf16[16,128,400]{1,2,0:T(8,128)(2,1)} %copy.129), calls=%async_computation.1 | async-start | bytes 3276800 | tf_op jit(solution)/shard_map/all_to_all | solution.py:15
  101.5 62.0 %all-gather.5.cloned.1.call-start = ((), (), s32[]{:S(2)}) async-start(), calls=%async_computation.9 | async-start | bytes 2228224 | tf_op jit(solution)/shard_map/all_gather | solution.py:68
  123.2 31.4 %all-to-all-start.2 = ((bf16[16,128,512]{2,1,0:T(8,128)(2,1)}), bf16[16,128,512]{2,1,0:T(8,128)(2,1)}, u32[]{:S(2)}, u32[]{:S(2)}) async-start(bf16[16,128,512]{2,1,0:T(8,128)(2,1)} %bitcast.158), calls=%async_computation.2 | async-start | bytes 4194304 | tf_op jit(solution)/shard_map/all_to_all | solution.py:15
  154.6 30.2 %all-to-all-start = ((bf16[16,128,512]{2,1,0:T(8,128)(2,1)}), bf16[16,128,512]{2,1,0:T(8,128)(2,1)}, u32[]{:S(2)}, u32[]{:S(2)}) async-start(bf16[16,128,512]{2,1,0:T(8,128)(2,1)} %bitcast.157), calls=%async_computation | async-start | bytes 4194304 | tf_op jit(solution)/shard_map/all_to_all | solution.py:15
  174.5 16.1 %copy-start.14 = (s32[32]{0:T(128)S(1)}, s32[32]{0:T(128)}, u32[]{:S(2)}) copy-start(s32[32]{0:T(128)} %param.24) | copy-start | bytes 388
  184.8 51.1 %all-to-all-start.5 = ((bf16[16,128,912]{1,2,0:T(8,128)(2,1)}), bf16[16,128,912]{1,2,0:T(8,128)(2,1)}, u32[]{:S(2)}, u32[]{:S(2)}) async-start(bf16[16,128,912]{1,2,0:T(8,128)(2,1)} %copy_bitcast_fusion), calls=%async_computation.5 | async-start | bytes 7471104 | tf_op jit(solution)/shard_map/all_to_all | solution.py:15
  203.3 3.2 copy-start.4
  206.5 2.4 copy-start.10
  206.5 2.4 copy-start.9
  206.6 3.4 copy-start.8
  208.9 29.7 %copy-start.7 = (f32[128,912]{1,0:T(8,128)}, f32[128,912]{1,0:T(8,128)S(1)}, u32[]{:S(2)}) copy-start(f32[128,912]{1,0:T(8,128)S(1)} %convert_reduce_fusion.1) | copy-start | bytes 1400836
  208.9 2.0 copy-start.12
  245.8 49.2 %all-to-all-start.4 = ((bf16[16,128,896]{2,1,0:T(8,128)(2,1)}), bf16[16,128,896]{2,1,0:T(8,128)(2,1)}, u32[]{:S(2)}, u32[]{:S(2)}) async-start(bf16[16,128,896]{2,1,0:T(8,128)(2,1)} %broadcast_in_dim.18), calls=%async_computation.4 | async-start | bytes 7340032 | tf_op jit(solution)/shard_map/all_to_all | solution.py:24
  305.1 4.6 %copy-start.11 = (bf16[128,16]{1,0:T(8,128)(2,1)S(1)}, bf16[128,16]{1,0:T(8,128)(2,1)}, u32[]{:S(2)}) copy-start(bf16[128,16]{1,0:T(8,128)(2,1)} %copy-done.10) | copy-start | bytes 12292
  305.1 4.8 %copy-start.13 = (bf16[128,16]{1,0:T(8,128)(2,1)S(1)}, bf16[128,16]{1,0:T(8,128)(2,1)}, u32[]{:S(2)}) copy-start(bf16[128,16]{1,0:T(8,128)(2,1)} %copy-done.12) | copy-start | bytes 12292
  305.1 58.0 %all-to-all-start.6 = ((bf16[16,128,560]{1,2,0:T(8,128)(2,1)}), bf16[16,128,560]{1,2,0:T(8,128)(2,1)}, u32[]{:S(2)}, u32[]{:S(2)}) async-start(bf16[16,128,560]{1,2,0:T(8,128)(2,1)} %pad_maximum_fusion.3), calls=%async_computation.6 | async-start | bytes 4587520 | tf_op jit(solution)/shard_map/all_to_all | solution.py:15
  366.9 9.8 %copy-start.1 = (s32[64]{0:T(128)S(1)}, s32[64]{0:T(128)}, u32[]{:S(2)}) copy-start(s32[64]{0:T(128)} %param.25) | copy-start | bytes 772
  366.9 36.8 %all-to-all-start.7 = ((bf16[16,72,896]{2,1,0:T(8,128)(2,1)}), bf16[16,72,896]{2,1,0:T(8,128)(2,1)}, u32[]{:S(2)}, u32[]{:S(2)}) async-start(bf16[16,72,896]{2,1,0:T(8,128)(2,1)} %broadcast_in_dim.22), calls=%async_computation.7 | async-start | bytes 4128768 | tf_op jit(solution)/shard_map/all_to_all | solution.py:24
  411.9 3.5 copy-start.2
Sparse Core Ops, SparseCore 0:
  9.8 42.3 all-gather.2
  104.1 37.7 all-gather.4
